TPU v7x, 512 devices: a whole 4x4x16 slice. The times are simulated.
512 devices in a mesh: seq: 128 (over x, z, core), grp: 4 (over y).
Axes of the slice: x: 4, y: 4, z: 16, core: 2. Of those that a mesh axis runs over, the one named last changes fastest.
Arguments:
- linear_query: bfloat16 [65536, 256], P(('grp', 'seq')), parts along dimension 0, may hold values from -6 to 6
- linear_key: bfloat16 [65536, 256], P(('grp', 'seq')), parts along dimension 0, may hold values from -16 to 16
- values: bfloat16 [65536, 2048], P(('grp', 'seq')), parts along dimension 0, may hold values from -6 to 6
- window_query: bfloat16 [65536, 2048], P(('grp', 'seq')), parts along dimension 0, may hold values from -5 to 5
- window_key: bfloat16 [65536, 2048], P(('grp', 'seq')), parts along dimension 0, may hold values from -5 to 5
Outputs:
- linear_out: float32 [65536, 2048], P(('grp', 'seq')), parts along dimension 0
- window_out: bfloat16 [65536, 2048], P(('grp', 'seq')), parts along dimension 0
There are 4 independent parts, one for each index of `grp`. A program takes and returns all parts, laid end to end along the dimension named above; each array names one. Nothing has to cross between parts.
All inputs are finite; a program needn't handle non-finite values.
Results may differ from a plain program's by a relative error of at most 0.0085.
Values may be sent and summed in bfloat16 or wider, within the bound.
No kernel may reach another device: no remote copies, remote signals or barrier semaphores. Data moves between devices by JAX's collectives and lax.ppermute only.
A program may use at most 64 MiB of HBM per device.

v0:
```python
import jax
import jax.numpy as jnp
import numpy as np
from jax import lax
from jax.sharding import PartitionSpec as P

FEAT = 16
WINDOW = 256


PRECISE = lax.Precision.HIGHEST
HALF_ROOT = 0.7071067811865476


def passed_along(block, axis, distance):
    devices = range(lax.axis_size(axis))
    route = [(i - distance, i) for i in devices if i - distance in devices]
    return lax.ppermute(block, axis, route)


def pair_features(scaled):
    row_count, head_count, feat_count = scaled.shape
    columns = jnp.transpose(scaled, (1, 2, 0))
    lower_index, upper_index = np.triu_indices(feat_count)
    identity = np.eye(feat_count, dtype=np.float32)
    pick_lower = jnp.asarray(identity[:, lower_index])
    pick_upper = jnp.asarray(identity[:, upper_index])
    pair_weight = jnp.asarray(
        np.where(lower_index == upper_index, HALF_ROOT, 1.0).astype(np.float32)
    )
    left_side = jnp.einsum("hfr,fp->hpr", columns, pick_lower, precision=PRECISE)
    right_side = jnp.einsum("hfr,fp->hpr", columns, pick_upper, precision=PRECISE)
    paired = left_side * right_side * pair_weight[None, :, None]
    return jnp.concatenate(
        [jnp.ones((head_count, 1, row_count), jnp.float32), columns, paired], axis=1
    )


def on_device(linear_query, linear_key, values, window_query, window_key):
    row_count = values.shape[0]
    head_count = linear_query.shape[1] // FEAT
    value_width = values.shape[1] // head_count
    seq_count = lax.axis_size("seq")
    seq_index = lax.axis_index("seq")
    start_pos = seq_index * row_count
    query_scaled = (linear_query.astype(jnp.float32) * FEAT ** (-0.25)).reshape(
        row_count, head_count, FEAT
    )
    key_scaled = (linear_key.astype(jnp.float32) * FEAT ** (-0.25)).reshape(
        row_count, head_count, FEAT
    )
    value_heads = values.astype(jnp.float32).reshape(row_count, head_count, value_width)
    query_feats = pair_features(query_scaled)
    key_feats = pair_features(key_scaled)
    local_state = jnp.einsum("hpr,rhv->hpv", key_feats, value_heads, precision=PRECISE)
    local_norm = jnp.sum(key_feats, axis=2)
    running_state = local_state
    running_norm = local_norm
    distance = 1
    while distance < seq_count:
        arrived = passed_along((running_state, running_norm), "seq", distance)
        running_state = running_state + arrived[0]
        running_norm = running_norm + arrived[1]
        distance = distance * 2
    prior_state = running_state - local_state
    prior_norm = running_norm - local_norm
    causal = jnp.arange(row_count)[:, None] >= jnp.arange(row_count)[None, :]
    inner_prod = jnp.einsum("thf,jhf->htj", query_scaled, key_scaled, precision=PRECISE)
    kernel = jnp.where(causal[None], 1.0 + inner_prod + 0.5 * inner_prod * inner_prod, 0.0)
    numerator = jnp.einsum("htj,jhv->thv", kernel, value_heads, precision=PRECISE) + jnp.einsum(
        "hpt,hpv->thv", query_feats, prior_state, precision=PRECISE
    )
    denominator = jnp.sum(kernel, axis=2).T + jnp.einsum(
        "hpt,hp->th", query_feats, prior_norm, precision=PRECISE
    )
    linear_out = (numerator / denominator[:, :, None]).reshape(row_count, head_count * value_width)
    span_rows = min(row_count, WINDOW)
    reach_count = -(-WINDOW // row_count)
    moved_keys = []
    moved_values = []
    for distance in range(1, reach_count + 1):
        arrived = passed_along((window_key, values), "seq", distance)
        moved_keys.append(arrived[0])
        moved_values.append(arrived[1])
    all_keys = jnp.concatenate(moved_keys[::-1] + [window_key], axis=0)
    all_values = jnp.concatenate(moved_values[::-1] + [values], axis=0)
    key_count = all_keys.shape[0]
    query_pos = start_pos + jnp.arange(row_count, dtype=jnp.int32)
    key_pos = start_pos - reach_count * span_rows + jnp.arange(key_count, dtype=jnp.int32)
    allowed = (
        (key_pos[None, :] <= query_pos[:, None])
        & (key_pos[None, :] > query_pos[:, None] - WINDOW)
        & (key_pos[None, :] >= 0)
    )
    scores = jnp.einsum(
        "thd,jhd->htj",
        window_query.reshape(row_count, head_count, value_width),
        all_keys.reshape(key_count, head_count, value_width),
        preferred_element_type=jnp.float32,
    ) * value_width ** (-0.5)
    masked = jnp.where(allowed[None], scores, -jnp.inf)
    largest = jnp.max(masked, axis=2, keepdims=True)
    exponent = jnp.exp(masked - largest)
    weights = (exponent / jnp.sum(exponent, axis=2, keepdims=True)).astype(jnp.bfloat16)
    mixed = jnp.einsum(
        "htj,jhv->thv",
        weights,
        all_values.reshape(key_count, head_count, value_width),
        preferred_element_type=jnp.float32,
    )
    window_out = mixed.astype(jnp.bfloat16).reshape(row_count, head_count * value_width)
    return (linear_out, window_out)


def solution(mesh):
    return jax.shard_map(
        on_device,
        mesh=mesh,
        in_specs=(
            P(("grp", "seq"), None),
            P(("grp", "seq"), None),
            P(("grp", "seq"), None),
            P(("grp", "seq"), None),
            P(("grp", "seq"), None),
        ),
        out_specs=(P(("grp", "seq"), None), P(("grp", "seq"), None)),
        check_vma=False,
    )
```

profile of v0, /device:TPU:1, one launch (start us, length us, event | category | flops | bytes accessed | tf_op | source)
XLA Modules:
  0.0 477.6 jit_solution(8356810080770783427)
XLA Ops:
  0.6 0.0 copy-start
  0.7 0.9 convert_multiply_fusion
  1.6 0.1 copy.66
  1.7 1.8 fusion.37
  3.5 1.1 fusion.7
  4.6 1.9 fusion.18
  6.5 0.7 copy.71
  7.3 4.9 %collective-permute-start = (f32[16,153,128]{2,0,1:T(8,128)S(1)}, f32[16,153,128]{2,0,1:T(8,128)S(1)}, u32[]{:S(2)}, u32[]{:S(2)}) collective-permute-start(f32[16,153,128]{2,0,1:T(8,128)S(1)} %copy.71), channel_id=1, source_target_pairs={{0,4},{4,8},{8,12},{12,16},{16,20},{20,24},{24,28},{28,32},{32,36}... | collective-permute-start | bytes 3760136 | tf_op jit(solution)/shard_map/ppermute | solution.py:18
  12.2 13.9 %collective-permute-done = f32[16,153,128]{2,0,1:T(8,128)S(1)} collective-permute-done((f32[16,153,128]{2,0,1:T(8,128)S(1)}, f32[16,153,128]{2,0,1:T(8,128)S(1)}, u32[]{:S(2)}, u32[]{:S(2)}) %collective-permute-start) | collective-permute-done | bytes 1253408 | tf_op jit(solution)/shard_map/ppermute | solution.py:18
  26.1 0.8 copy_add_fusion
  26.9 3.6 collective-permute-start.1
  30.5 25.8 %collective-permute-done.1 = f32[16,153,128]{2,0,1:T(8,128)S(1)} collective-permute-done((f32[16,153,128]{2,0,1:T(8,128)S(1)}, f32[16,153,128]{2,0,1:T(8,128)S(1)}, u32[]{:S(2)}, u32[]{:S(2)}) %collective-permute-start.1) | collective-permute-done | bytes 1253408 | tf_op jit(solution)/shard_map/ppermute | solution.py:18
  56.4 0.2 add.97
  56.6 7.4 %collective-permute-start.2 = (f32[16,153,128]{2,0,1:T(8,128)S(1)}, f32[16,153,128]{2,0,1:T(8,128)S(1)}, u32[]{:S(2)}, u32[]{:S(2)}) collective-permute-start(f32[16,153,128]{2,0,1:T(8,128)S(1)} %add.97), channel_id=1, source_target_pairs={{0,16},{4,20},{8,24},{12,28},{16,32},{20,36},{24,40},{28,44},{32,4... | collective-permute-start | bytes 3760136 | tf_op jit(solution)/shard_map/ppermute | solution.py:18
  64.0 41.0 %collective-permute-done.2 = f32[16,153,128]{2,0,1:T(8,128)S(1)} collective-permute-done((f32[16,153,128]{2,0,1:T(8,128)S(1)}, f32[16,153,128]{2,0,1:T(8,128)S(1)}, u32[]{:S(2)}, u32[]{:S(2)}) %collective-permute-start.2) | collective-permute-done | bytes 1253408 | tf_op jit(solution)/shard_map/ppermute | solution.py:18
  104.9 1.3 add.98
  106.2 22.4 %collective-permute-start.3 = (f32[16,153,128]{2,0,1:T(8,128)}, f32[16,153,128]{2,0,1:T(8,128)}, u32[]{:S(2)}, u32[]{:S(2)}) collective-permute-start(f32[16,153,128]{2,0,1:T(8,128)} %add.98), channel_id=1, source_target_pairs={{0,32},{4,36},{8,40},{12,44},{16,48},{20,52},{24,56},{28,60},{32,6... | collective-permute-start | bytes 3760136 | tf_op jit(solution)/shard_map/ppermute | solution.py:18
  128.6 2.0 copy.75
  130.6 4.5 collective-permute-start.16
  135.1 3.7 collective-permute-start.17
  138.9 5.4 %collective-permute-start.14 = (bf16[128,2048]{1,0:T(8,128)(2,1)}, bf16[128,2048]{1,0:T(8,128)(2,1)}, u32[]{:S(2)}, u32[]{:S(2)}) collective-permute-start(bf16[128,2048]{1,0:T(8,128)(2,1)} %param.13), channel_id=1, source_target_pairs={{0,8},{4,12},{8,16},{12,20},{16,24},{20,28},{24,32},{28,36},{32,40... | collective-permute-start | bytes 1572872 | tf_op jit(solution)/shard_map/ppermute | solution.py:18
  144.2 0.8 fusion.17
  145.0 1.9 collective-permute-start.7
  147.0 0.1 copy.65
  147.1 82.1 %collective-permute-done.3 = f32[16,153,128]{2,0,1:T(8,128)} collective-permute-done((f32[16,153,128]{2,0,1:T(8,128)}, f32[16,153,128]{2,0,1:T(8,128)}, u32[]{:S(2)}, u32[]{:S(2)}) %collective-permute-start.3) | collective-permute-done | bytes 1253408 | tf_op jit(solution)/shard_map/ppermute | solution.py:18
  229.3 1.8 add.99
  231.1 2.3 collective-permute-start.4
  233.4 1.8 fusion.35
  235.3 2.8 convolution_bitcast_fusion.1
  238.1 40.3 %collective-permute-done.7 = f32[16,153]{1,0:T(8,128)S(1)} collective-permute-done((f32[16,153]{1,0:T(8,128)S(1)}, f32[16,153]{1,0:T(8,128)S(1)}, u32[]{:S(2)}, u32[]{:S(2)}) %collective-permute-start.7) | collective-permute-done | bytes 9824 | tf_op jit(solution)/shard_map/ppermute | solution.py:18
  278.4 3.1 collective-permute-start.8
  281.5 1.1 fusion.38
  282.6 63.0 %collective-permute-done.8 = f32[16,153]{1,0:T(8,128)S(1)} collective-permute-done((f32[16,153]{1,0:T(8,128)S(1)}, f32[16,153]{1,0:T(8,128)S(1)}, u32[]{:S(2)}, u32[]{:S(2)}) %collective-permute-start.8) | collective-permute-done | bytes 9824 | tf_op jit(solution)/shard_map/ppermute | solution.py:18
  345.6 30.4 %collective-permute-start.9 = (f32[16,153]{1,0:T(8,128)S(1)}, f32[16,153]{1,0:T(8,128)S(1)}, u32[]{:S(2)}, u32[]{:S(2)}) collective-permute-start(f32[16,153]{1,0:T(8,128)S(1)} %add.105), channel_id=1, source_target_pairs={{0,16},{4,20},{8,24},{12,28},{16,32},{20,36},{24,40},{28,44},{32,4... | collective-permute-start | bytes 29384 | tf_op jit(solution)/shard_map/ppermute | solution.py:18
  376.0 2.2 fusion.9
  378.2 8.0 %collective-permute-start.10 = (f32[16,153]{1,0:T(8,128)S(1)}, f32[16,153]{1,0:T(8,128)S(1)}, u32[]{:S(2)}, u32[]{:S(2)}) collective-permute-start(f32[16,153]{1,0:T(8,128)S(1)} %add.106), channel_id=1, source_target_pairs={{0,32},{4,36},{8,40},{12,44},{16,48},{20,52},{24,56},{28,60},{32,6... | collective-permute-start | bytes 29384 | tf_op jit(solution)/shard_map/ppermute | solution.py:18
  386.2 0.8 collective-permute-done.10
  387.1 7.3 %collective-permute-start.11 = (f32[16,153]{1,0:T(8,128)S(1)}, f32[16,153]{1,0:T(8,128)S(1)}, u32[]{:S(2)}, u32[]{:S(2)}) collective-permute-start(f32[16,153]{1,0:T(8,128)S(1)} %add.107), channel_id=1, source_target_pairs={{0,64},{4,68},{8,72},{12,76},{16,80},{20,84},{24,88},{28,92},{32,9... | collective-permute-start | bytes 29384 | tf_op jit(solution)/shard_map/ppermute | solution.py:18
  394.4 0.8 collective-permute-done.11
  395.2 9.6 %collective-permute-start.12 = (f32[16,153]{1,0:T(8,128)S(1)}, f32[16,153]{1,0:T(8,128)S(1)}, u32[]{:S(2)}, u32[]{:S(2)}) collective-permute-start(f32[16,153]{1,0:T(8,128)S(1)} %add.108), channel_id=1, source_target_pairs={{0,128},{4,132},{8,136},{12,140},{16,144},{20,148},{24,152},{28,15... | collective-permute-start | bytes 29384 | tf_op jit(solution)/shard_map/ppermute | solution.py:18
  404.8 0.8 collective-permute-done.12
  405.6 5.5 %collective-permute-start.13 = (f32[16,153]{1,0:T(8,128)S(1)}, f32[16,153]{1,0:T(8,128)S(1)}, u32[]{:S(2)}, u32[]{:S(2)}) collective-permute-start(f32[16,153]{1,0:T(8,128)S(1)} %add.109), channel_id=1, source_target_pairs={{0,256},{4,260},{8,264},{12,268},{16,272},{20,276},{24,280},{28,28... | collective-permute-start | bytes 29384 | tf_op jit(solution)/shard_map/ppermute | solution.py:18
  411.1 2.5 add.100
  413.6 2.4 collective-permute-start.5
  416.0 0.8 and_and_fusion
  416.8 8.3 %collective-permute-start.15 = (bf16[128,2048]{1,0:T(8,128)(2,1)}, bf16[128,2048]{1,0:T(8,128)(2,1)S(1)}, u32[]{:S(2)}, u32[]{:S(2)}) collective-permute-start(bf16[128,2048]{1,0:T(8,128)(2,1)} %param.13), channel_id=1, source_target_pairs={{0,4},{4,8},{8,12},{12,16},{16,20},{20,24},{24,28},{28,32},{32,36}... | collective-permute-start | bytes 1572872 | tf_op jit(solution)/shard_map/ppermute | solution.py:18
  425.1 1.3 fusion.16
  426.4 4.9 %collective-permute-done.15 = bf16[128,2048]{1,0:T(8,128)(2,1)S(1)} collective-permute-done((bf16[128,2048]{1,0:T(8,128)(2,1)}, bf16[128,2048]{1,0:T(8,128)(2,1)S(1)}, u32[]{:S(2)}, u32[]{:S(2)}) %collective-permute-start.15) | collective-permute-done | bytes 524320 | tf_op jit(solution)/shard_map/ppermute | solution.py:18
  431.3 1.3 pad_maximum_fusion
  432.6 1.6 copy.74
  434.2 1.6 pad_maximum_fusion.1
  435.8 7.0 %collective-permute-done.5 = f32[16,153,128]{2,0,1:T(8,128)} collective-permute-done((f32[16,153,128]{2,0,1:T(8,128)}, f32[16,153,128]{2,0,1:T(8,128)}, u32[]{:S(2)}, u32[]{:S(2)}) %collective-permute-start.5) | collective-permute-done | bytes 1253408 | tf_op jit(solution)/shard_map/ppermute | solution.py:18
  442.8 1.8 add.101
  444.6 5.8 %collective-permute-start.6 = (f32[16,153,128]{2,0,1:T(8,128)S(1)}, f32[16,153,128]{2,0,1:T(8,128)}, u32[]{:S(2)}, u32[]{:S(2)}) collective-permute-start(f32[16,153,128]{2,0,1:T(8,128)S(1)} %add.101), channel_id=1, source_target_pairs={{0,256},{4,260},{8,264},{12,268},{16,272},{20,276},{24,280},{28,28... | collective-permute-start | bytes 3760136 | tf_op jit(solution)/shard_map/ppermute | solution.py:18
  450.4 0.6 fusion.22
  451.0 0.2 copy-done.8
  451.2 0.9 fusion.36
  452.1 0.5 copy-done.1
  452.6 1.4 fusion.13
  454.0 2.0 copy.82
  456.0 14.5 %collective-permute-done.6 = f32[16,153,128]{2,0,1:T(8,128)} collective-permute-done((f32[16,153,128]{2,0,1:T(8,128)S(1)}, f32[16,153,128]{2,0,1:T(8,128)}, u32[]{:S(2)}, u32[]{:S(2)}) %collective-permute-start.6) | collective-permute-done | bytes 1253408 | tf_op jit(solution)/shard_map/ppermute | solution.py:18
  470.5 2.1 add_subtract_fusion
  472.6 3.7 fusion.11
  476.3 1.3 copy.81
  (37 shorter events, 0.2 us)
Async XLA Ops:
  0.6 449.7 %copy-start = (bf16[128,2048]{1,0:T(8,128)(2,1)S(1)}, bf16[128,2048]{1,0:T(8,128)(2,1)}, u32[]{:S(2)}) copy-start(bf16[128,2048]{1,0:T(8,128)(2,1)} %param.14) | copy-start | bytes 1572868
  0.6 2.8 copy-start.9
  0.7 2.8 copy-start.5
  7.3 18.8 %collective-permute-start = (f32[16,153,128]{2,0,1:T(8,128)S(1)}, f32[16,153,128]{2,0,1:T(8,128)S(1)}, u32[]{:S(2)}, u32[]{:S(2)}) collective-permute-start(f32[16,153,128]{2,0,1:T(8,128)S(1)} %copy.71), channel_id=1, source_target_pairs={{0,4},{4,8},{8,12},{12,16},{16,20},{20,24},{24,28},{28,32},{32,36}... | collective-permute-start | bytes 3760136 | tf_op jit(solution)/shard_map/ppermute | solution.py:18
  26.9 29.5 %collective-permute-start.1 = (f32[16,153,128]{2,0,1:T(8,128)S(1)}, f32[16,153,128]{2,0,1:T(8,128)S(1)}, u32[]{:S(2)}, u32[]{:S(2)}) collective-permute-start(f32[16,153,128]{2,0,1:T(8,128)S(1)} %copy_add_fusion), channel_id=1, source_target_pairs={{0,8},{4,12},{8,16},{12,20},{16,24},{20,28},{24,32},{28,36},{32,40... | collective-permute-start | bytes 3760136 | tf_op jit(solution)/shard_map/ppermute | solution.py:18
  56.6 48.4 %collective-permute-start.2 = (f32[16,153,128]{2,0,1:T(8,128)S(1)}, f32[16,153,128]{2,0,1:T(8,128)S(1)}, u32[]{:S(2)}, u32[]{:S(2)}) collective-permute-start(f32[16,153,128]{2,0,1:T(8,128)S(1)} %add.97), channel_id=1, source_target_pairs={{0,16},{4,20},{8,24},{12,28},{16,32},{20,36},{24,40},{28,44},{32,4... | collective-permute-start | bytes 3760136 | tf_op jit(solution)/shard_map/ppermute | solution.py:18
  106.2 40.8 %copy-start.7 = (bf16[128,256]{1,0:T(8,128)(2,1)S(1)}, bf16[128,256]{1,0:T(8,128)(2,1)}, u32[]{:S(2)}) copy-start(bf16[128,256]{1,0:T(8,128)(2,1)} %param.11) | copy-start | bytes 196612
  106.2 123.1 %collective-permute-start.3 = (f32[16,153,128]{2,0,1:T(8,128)}, f32[16,153,128]{2,0,1:T(8,128)}, u32[]{:S(2)}, u32[]{:S(2)}) collective-permute-start(f32[16,153,128]{2,0,1:T(8,128)} %add.98), channel_id=1, source_target_pairs={{0,32},{4,36},{8,40},{12,44},{16,48},{20,52},{24,56},{28,60},{32,6... | collective-permute-start | bytes 3760136 | tf_op jit(solution)/shard_map/ppermute | solution.py:18
  130.6 303.6 %collective-permute-start.16 = (bf16[128,2048]{0,1:T(8,128)(2,1)}, bf16[128,2048]{0,1:T(8,128)(2,1)}, u32[]{:S(2)}, u32[]{:S(2)}) collective-permute-start(bf16[128,2048]{0,1:T(8,128)(2,1)} %copy.75), channel_id=1, source_target_pairs={{0,8},{4,12},{8,16},{12,20},{16,24},{20,28},{24,32},{28,36},{32,40... | collective-permute-start | bytes 1572872 | tf_op jit(solution)/shard_map/ppermute | solution.py:18
  135.1 299.1 %collective-permute-start.17 = (bf16[128,2048]{0,1:T(8,128)(2,1)}, bf16[128,2048]{0,1:T(8,128)(2,1)}, u32[]{:S(2)}, u32[]{:S(2)}) collective-permute-start(bf16[128,2048]{0,1:T(8,128)(2,1)} %copy.75), channel_id=1, source_target_pairs={{0,4},{4,8},{8,12},{12,16},{16,20},{20,24},{24,28},{28,32},{32,36}... | collective-permute-start | bytes 1572872 | tf_op jit(solution)/shard_map/ppermute | solution.py:18
  138.9 287.5 %collective-permute-start.14 = (bf16[128,2048]{1,0:T(8,128)(2,1)}, bf16[128,2048]{1,0:T(8,128)(2,1)}, u32[]{:S(2)}, u32[]{:S(2)}) collective-permute-start(bf16[128,2048]{1,0:T(8,128)(2,1)} %param.13), channel_id=1, source_target_pairs={{0,8},{4,12},{8,16},{12,20},{16,24},{20,28},{24,32},{28,36},{32,40... | collective-permute-start | bytes 1572872 | tf_op jit(solution)/shard_map/ppermute | solution.py:18
  145.0 133.4 %collective-permute-start.7 = (f32[16,153]{1,0:T(8,128)S(1)}, f32[16,153]{1,0:T(8,128)S(1)}, u32[]{:S(2)}, u32[]{:S(2)}) collective-permute-start(f32[16,153]{1,0:T(8,128)S(1)} %fusion.17), channel_id=1, source_target_pairs={{0,4},{4,8},{8,12},{12,16},{16,20},{20,24},{24,28},{28,32},{32,36}... | collective-permute-start | bytes 29384 | tf_op jit(solution)/shard_map/ppermute | solution.py:18
  231.1 180.0 %collective-permute-start.4 = (f32[16,153,128]{2,0,1:T(8,128)S(1)}, f32[16,153,128]{2,0,1:T(8,128)}, u32[]{:S(2)}, u32[]{:S(2)}) collective-permute-start(f32[16,153,128]{2,0,1:T(8,128)S(1)} %add.99), channel_id=1, source_target_pairs={{0,64},{4,68},{8,72},{12,76},{16,80},{20,84},{24,88},{28,92},{32,9... | collective-permute-start | bytes 3760136 | tf_op jit(solution)/shard_map/ppermute | solution.py:18
  235.3 46.2 %copy-start.6 = (f32[16,136,1]{1,0,2:T(8,128)S(1)}, f32[16,136,1]{1,0,2:T(8,128)}, u32[]{:S(2)}) copy-start(f32[16,136,1]{1,0,2:T(8,128)} %constant.41) | copy-start | bytes 26116
  278.4 67.2 %collective-permute-start.8 = (f32[16,153]{1,0:T(8,128)S(1)}, f32[16,153]{1,0:T(8,128)S(1)}, u32[]{:S(2)}, u32[]{:S(2)}) collective-permute-start(f32[16,153]{1,0:T(8,128)S(1)} %add.104), channel_id=1, source_target_pairs={{0,8},{4,12},{8,16},{12,20},{16,24},{20,28},{24,32},{28,36},{32,40... | collective-permute-start | bytes 29384 | tf_op jit(solution)/shard_map/ppermute | solution.py:18
  345.6 32.6 %collective-permute-start.9 = (f32[16,153]{1,0:T(8,128)S(1)}, f32[16,153]{1,0:T(8,128)S(1)}, u32[]{:S(2)}, u32[]{:S(2)}) collective-permute-start(f32[16,153]{1,0:T(8,128)S(1)} %add.105), channel_id=1, source_target_pairs={{0,16},{4,20},{8,24},{12,28},{16,32},{20,36},{24,40},{28,44},{32,4... | collective-permute-start | bytes 29384 | tf_op jit(solution)/shard_map/ppermute | solution.py:18
  378.2 8.9 %collective-permute-start.10 = (f32[16,153]{1,0:T(8,128)S(1)}, f32[16,153]{1,0:T(8,128)S(1)}, u32[]{:S(2)}, u32[]{:S(2)}) collective-permute-start(f32[16,153]{1,0:T(8,128)S(1)} %add.106), channel_id=1, source_target_pairs={{0,32},{4,36},{8,40},{12,44},{16,48},{20,52},{24,56},{28,60},{32,6... | collective-permute-start | bytes 29384 | tf_op jit(solution)/shard_map/ppermute | solution.py:18
  387.1 8.1 %collective-permute-start.11 = (f32[16,153]{1,0:T(8,128)S(1)}, f32[16,153]{1,0:T(8,128)S(1)}, u32[]{:S(2)}, u32[]{:S(2)}) collective-permute-start(f32[16,153]{1,0:T(8,128)S(1)} %add.107), channel_id=1, source_target_pairs={{0,64},{4,68},{8,72},{12,76},{16,80},{20,84},{24,88},{28,92},{32,9... | collective-permute-start | bytes 29384 | tf_op jit(solution)/shard_map/ppermute | solution.py:18
  395.2 10.4 %collective-permute-start.12 = (f32[16,153]{1,0:T(8,128)S(1)}, f32[16,153]{1,0:T(8,128)S(1)}, u32[]{:S(2)}, u32[]{:S(2)}) collective-permute-start(f32[16,153]{1,0:T(8,128)S(1)} %add.108), channel_id=1, source_target_pairs={{0,128},{4,132},{8,136},{12,140},{16,144},{20,148},{24,152},{28,15... | collective-permute-start | bytes 29384 | tf_op jit(solution)/shard_map/ppermute | solution.py:18
  405.6 19.5 %copy-start.2 = (f32[16,136,128]{2,1,0:T(8,128)S(1)}, f32[16,136,128]{2,1,0:T(8,128)}, u32[]{:S(2)}) copy-start(f32[16,136,128]{2,1,0:T(8,128)} %fusion.9) | copy-start | bytes 3342340
  405.6 11.1 %collective-permute-start.13 = (f32[16,153]{1,0:T(8,128)S(1)}, f32[16,153]{1,0:T(8,128)S(1)}, u32[]{:S(2)}, u32[]{:S(2)}) collective-permute-start(f32[16,153]{1,0:T(8,128)S(1)} %add.109), channel_id=1, source_target_pairs={{0,256},{4,260},{8,264},{12,268},{16,272},{20,276},{24,280},{28,28... | collective-permute-start | bytes 29384 | tf_op jit(solution)/shard_map/ppermute | solution.py:18
  413.6 29.1 %collective-permute-start.5 = (f32[16,153,128]{2,0,1:T(8,128)}, f32[16,153,128]{2,0,1:T(8,128)}, u32[]{:S(2)}, u32[]{:S(2)}) collective-permute-start(f32[16,153,128]{2,0,1:T(8,128)} %add.100), channel_id=1, source_target_pairs={{0,128},{4,132},{8,136},{12,140},{16,144},{20,148},{24,152},{28,15... | collective-permute-start | bytes 3760136 | tf_op jit(solution)/shard_map/ppermute | solution.py:18
  416.8 14.5 %collective-permute-start.15 = (bf16[128,2048]{1,0:T(8,128)(2,1)}, bf16[128,2048]{1,0:T(8,128)(2,1)S(1)}, u32[]{:S(2)}, u32[]{:S(2)}) collective-permute-start(bf16[128,2048]{1,0:T(8,128)(2,1)} %param.13), channel_id=1, source_target_pairs={{0,4},{4,8},{8,12},{12,16},{16,20},{20,24},{24,28},{28,32},{32,36}... | collective-permute-start | bytes 1572872 | tf_op jit(solution)/shard_map/ppermute | solution.py:18
  444.6 25.9 %collective-permute-start.6 = (f32[16,153,128]{2,0,1:T(8,128)S(1)}, f32[16,153,128]{2,0,1:T(8,128)}, u32[]{:S(2)}, u32[]{:S(2)}) collective-permute-start(f32[16,153,128]{2,0,1:T(8,128)S(1)} %add.101), channel_id=1, source_target_pairs={{0,256},{4,260},{8,264},{12,268},{16,272},{20,276},{24,280},{28,28... | collective-permute-start | bytes 3760136 | tf_op jit(solution)/shard_map/ppermute | solution.py:18
  450.4 0.8 copy-start.8
  451.2 1.4 copy-start.1
  456.0 16.5 %copy-start.3 = (f32[16,136,128]{2,1,0:T(8,128)S(1)}, f32[16,136,128]{2,1,0:T(8,128)}, u32[]{:S(2)}) copy-start(f32[16,136,128]{2,1,0:T(8,128)} %fusion.9) | copy-start | bytes 3342340
  456.0 16.5 %copy-start.4 = (f32[128,16,128]{0,2,1:T(8,128)S(1)}, f32[128,16,128]{0,2,1:T(8,128)}, u32[]{:S(2)}) copy-start(f32[128,16,128]{0,2,1:T(8,128)} %convolution_bitcast_fusion.1) | copy-start | bytes 3145732
where the time goes:
time: 485 us; the launch traced here: 478 us
  waiting for transfers between devices  295 us (61%)
  starting transfers between devices  136 us (28%)
  matrix products  19.6 us (4%)
  other arithmetic  16.8 us (3%)
  local copies, waits for them, and re-layouts  8.56 us (2%)
    ppermute x18, waiting for transfers between devices, passed_along(): return lax.ppermute(block, axis, route)  295 us
    ppermute x18, starting transfers between devices, passed_along(): return lax.ppermute(block, axis, route)  136 us
  transfers between devices with their start and end apart: 18, of which 12 were waited for; matrix products, arithmetic and copies ran while one was open for 6% of the time, Pallas kernels for 0%

commit v1 on v0

--- a/solution.py
+++ b/solution.py
@@ -2,6 +2,7 @@
 import jax.numpy as jnp
 import numpy as np
 from jax import lax
+from jax.sharding import Mesh
 from jax.sharding import PartitionSpec as P
 
 FEAT = 16
@@ -10,12 +11,21 @@
 
 PRECISE = lax.Precision.HIGHEST
 HALF_ROOT = 0.7071067811865476
+ROWS = ("grp", "sx", "sz", "sc")
 
 
 def passed_along(block, axis, distance):
     devices = range(lax.axis_size(axis))
     route = [(i - distance, i) for i in devices if i - distance in devices]
     return lax.ppermute(block, axis, route)
+
+
+def seq_index_of():
+    return (
+        lax.axis_index("sx") * (lax.axis_size("sz") * lax.axis_size("sc"))
+        + lax.axis_index("sz") * lax.axis_size("sc")
+        + lax.axis_index("sc")
+    )
 
 
 def pair_features(scaled):
@@ -36,12 +46,42 @@
     )
 
 
+def prefix_before(local):
+    nz = lax.axis_size("sz")
+    nx = lax.axis_size("sx")
+    core = lax.axis_index("sc")
+    size = local.size
+    unit = 2 * nz * 128
+    padded = -(-size // unit) * unit
+    width = padded // (2 * nz)
+    flat = jnp.pad(local.reshape(-1), (0, padded - size)).reshape(2, nz, width)
+    sent = jnp.where(core == 0, flat[1], flat[0])
+    other = lax.ppermute(sent, "sc", [(0, 1), (1, 0)])
+    mine = jnp.where(core == 0, flat[0], flat[1])
+    chip_half = mine + other
+    gathered = lax.all_to_all(chip_half, "sz", 0, 0, tiled=True)
+    running = jnp.cumsum(gathered, axis=0)
+    line_total = running[nz - 1]
+    before_chip = running - gathered
+    totals = lax.all_gather(line_total, "sx", axis=0, tiled=False)
+    earlier_line = (jnp.arange(nx) < lax.axis_index("sx"))[:, None]
+    line_offset = jnp.sum(jnp.where(earlier_line, totals, 0.0), axis=0)
+    before_chip = before_chip + line_offset[None, :]
+    chip_prefix = lax.all_to_all(before_chip, "sz", 0, 0, tiled=True)
+    first_core = jnp.where(core == 0, flat[0], other)
+    with_first = chip_prefix + first_core
+    keep = jnp.where(core == 0, chip_prefix, with_first)
+    give = jnp.where(core == 0, with_first, chip_prefix)
+    got = lax.ppermute(give, "sc", [(0, 1), (1, 0)])
+    halves = jnp.where(core == 0, jnp.stack([keep, got]), jnp.stack([got, keep]))
+    return halves.reshape(-1)[:size].reshape(local.shape)
+
+
 def on_device(linear_query, linear_key, values, window_query, window_key):
     row_count = values.shape[0]
     head_count = linear_query.shape[1] // FEAT
     value_width = values.shape[1] // head_count
-    seq_count = lax.axis_size("seq")
-    seq_index = lax.axis_index("seq")
+    seq_index = seq_index_of()
     start_pos = seq_index * row_count
     query_scaled = (linear_query.astype(jnp.float32) * FEAT ** (-0.25)).reshape(
         row_count, head_count, FEAT
@@ -54,16 +94,10 @@
     key_feats = pair_features(key_scaled)
     local_state = jnp.einsum("hpr,rhv->hpv", key_feats, value_heads, precision=PRECISE)
     local_norm = jnp.sum(key_feats, axis=2)
-    running_state = local_state
-    running_norm = local_norm
-    distance = 1
-    while distance < seq_count:
-        arrived = passed_along((running_state, running_norm), "seq", distance)
-        running_state = running_state + arrived[0]
-        running_norm = running_norm + arrived[1]
-        distance = distance * 2
-    prior_state = running_state - local_state
-    prior_norm = running_norm - local_norm
+    local = jnp.concatenate([local_state, local_norm[:, :, None]], axis=2)
+    prior = prefix_before(local)
+    prior_state = prior[:, :, :value_width]
+    prior_norm = prior[:, :, value_width]
     causal = jnp.arange(row_count)[:, None] >= jnp.arange(row_count)[None, :]
     inner_prod = jnp.einsum("thf,jhf->htj", query_scaled, key_scaled, precision=PRECISE)
     kernel = jnp.where(causal[None], 1.0 + inner_prod + 0.5 * inner_prod * inner_prod, 0.0)
@@ -74,12 +108,15 @@
         "hpt,hp->th", query_feats, prior_norm, precision=PRECISE
     )
     linear_out = (numerator / denominator[:, :, None]).reshape(row_count, head_count * value_width)
+    seq_count = lax.axis_size("sx") * lax.axis_size("sz") * lax.axis_size("sc")
     span_rows = min(row_count, WINDOW)
     reach_count = -(-WINDOW // row_count)
     moved_keys = []
     moved_values = []
+    flat_axes = ("sx", "sz", "sc")
     for distance in range(1, reach_count + 1):
-        arrived = passed_along((window_key, values), "seq", distance)
+        route = [(i - distance, i) for i in range(seq_count) if i - distance >= 0]
+        arrived = lax.ppermute((window_key, values), flat_axes, route)
         moved_keys.append(arrived[0])
         moved_values.append(arrived[1])
     all_keys = jnp.concatenate(moved_keys[::-1] + [window_key], axis=0)
@@ -112,17 +149,30 @@
     return (linear_out, window_out)
 
 
+def split_seq(mesh):
+    seq_devices = np.moveaxis(mesh.devices, mesh.axis_names.index("seq"), 0)[:, 0]
+    seq_count = len(seq_devices)
+    try:
+        chips = sorted({tuple(d.coords) for d in seq_devices})
+        cores = seq_count // len(chips)
+        xs = sorted({c[0] for c in chips})
+        nx = len(xs)
+    except (AttributeError, TypeError):
+        cores, nx = 2, max(1, seq_count // 32)
+    nz = seq_count // (nx * cores)
+    return nx, nz, cores
+
+
 def solution(mesh):
+    nx, nz, nc = split_seq(mesh)
+    parts = {"seq": ((nx, nz, nc), ("sx", "sz", "sc")), "grp": ((mesh.shape["grp"],), ("grp",))}
+    shape = sum((parts[name][0] for name in mesh.axis_names), ())
+    names = sum((parts[name][1] for name in mesh.axis_names), ())
+    inner = Mesh(mesh.devices.reshape(shape), names)
     return jax.shard_map(
         on_device,
-        mesh=mesh,
-        in_specs=(
-            P(("grp", "seq"), None),
-            P(("grp", "seq"), None),
-            P(("grp", "seq"), None),
-            P(("grp", "seq"), None),
-            P(("grp", "seq"), None),
-        ),
-        out_specs=(P(("grp", "seq"), None), P(("grp", "seq"), None)),
+        mesh=inner,
+        in_specs=(P(ROWS, None),) * 5,
+        out_specs=(P(ROWS, None), P(ROWS, None)),
         check_vma=False,
     )

time: 485 us -> 170 us (0.35); the launches traced: 478 us -> 170 us
  waiting for transfers between devices: 295 us -> 30.3 us
  starting transfers between devices: 136 us -> 45.9 us
  blocking collectives: 0 us -> 38.6 us
  local copies, waits for them, and re-layouts: 8.56 us -> 18.8 us
    ppermute x18 -> x6, waiting for transfers between devices: 295 us -> 1.69 us  [the longest x1 1.68 us: prefix_before(): other = lax.ppermute(sent, 'sc', [(0, 1), (1, 0)])]
    ppermute x18 -> x6, starting transfers between devices: 136 us -> 32.4 us  [the longest x4 13.3 us: on_device(): arrived = lax.ppermute((window_key, values), flat_axes, route)]
    all_gather x0 -> x1, blocking collectives: none -> 38.6 us  [prefix_before(): totals = lax.all_gather(line_total, 'sx', axis=0, tiled=False)]
    all_to_all x0 -> x2, waiting for transfers between devices: none -> 28.6 us  [the longest x1 14.7 us: prefix_before(): chip_prefix = lax.all_to_all(before_chip, 'sz', 0, 0, tiled=True)]
    all_to_all x0 -> x2, starting transfers between devices: none -> 13.5 us  [the longest x1 9.7 us: prefix_before(): gathered = lax.all_to_all(chip_half, 'sz', 0, 0, tiled=True)]
    add x12 -> x2, other arithmetic: 8.43 us -> 0.18 us  [the longest x1 0.09 us: prefix_before(): chip_half = mine + other]
    reshape x0 -> x2, local copies, waits for them, and re-layouts: none -> 5.17 us  [the longest x1 3.08 us: prefix_before(): return halves.reshape(-1)[:size].reshape(local.shape)]
  transfers between devices with their start and end apart: 18 -> 8, of which waited for: 12 -> 3; matrix products, arithmetic and copies ran while one was open for 6% -> 13% of each run, Pallas kernels for 0% -> 0%
where the time goes in v1:
time: 170 us
  starting transfers between devices  45.9 us (27%)
  blocking collectives  38.6 us (23%)
  waiting for transfers between devices  30.3 us (18%)
  matrix products  22.2 us (13%)
  local copies, waits for them, and re-layouts  18.8 us (11%)
  other arithmetic  12.8 us (8%)
    all_gather x1, blocking collectives, prefix_before(): totals = lax.all_gather(line_total, 'sx', axis=0, tiled=False)  38.6 us
    all_to_all x1, waiting for transfers between devices, prefix_before(): chip_prefix = lax.all_to_all(before_chip, 'sz', 0, 0, tiled=True)  14.7 us
    all_to_all x1, waiting for transfers between devices, prefix_before(): gathered = lax.all_to_all(chip_half, 'sz', 0, 0, tiled=True)  13.9 us
    ppermute x4, starting transfers between devices, on_device(): arrived = lax.ppermute((window_key, values), flat_axes, route)  13.3 us
    ppermute x1, starting transfers between devices, prefix_before(): got = lax.ppermute(give, 'sc', [(0, 1), (1, 0)])  10.4 us
    all_to_all x1, starting transfers between devices, prefix_before(): gathered = lax.all_to_all(chip_half, 'sz', 0, 0, tiled=True)  9.7 us
    ppermute x1, starting transfers between devices, prefix_before(): other = lax.ppermute(sent, 'sc', [(0, 1), (1, 0)])  8.75 us
    unnamed x31, local copies, waits for them, and re-layouts  4.06 us
  transfers between devices with their start and end apart: 8, of which 3 were waited for; matrix products, arithmetic and copies ran while one was open for 13% of the time, Pallas kernels for 0%

profile of v1, /device:TPU:1, one launch (start us, length us, event | category | flops | bytes accessed | tf_op | source)
XLA Modules:
  0.0 169.7 jit_solution(11046260437547708853)
XLA Ops:
  0.6 0.0 copy-start
  0.6 0.0 copy-start.10
  0.7 0.0 copy-start.5
  0.7 0.9 convert_multiply_fusion
  1.6 0.1 copy.39
  1.7 1.8 %fusion.40 = f32[16,128,136]{1,2,0:T(8,128)S(1)} fusion(f32[16,16,128]{2,1,0:T(8,128)S(1)} %bitcast.96, f32[16,136,1]{1,0,2:T(8,128)} %constant.62), kind=kOutput, calls=%fused_computation.75 | convolution fusion | flops 53477376 | bytes 1253888 | tf_op jit(solution)/shard_map/hfr,fp->hpr/dot_general | solution.py:41
  3.5 1.1 fusion.7
  4.7 0.8 fusion.17
  5.5 3.0 %fusion.18 = f32[16,153,128]{2,1,0:T(8,128)} fusion(f32[16,136,128]{2,1,0:T(8,128)S(1)} %fusion.7, f32[16,16,128]{2,1,0:T(8,128)S(1)} %bitcast.99, f32[153]{0:T(256)S(1)} %pad.20.clone, bf16[128,2048]{1,0:T(8,128)(2,1)} %param.13), kind=kOutput, calls=%fused_computation.34 | convolution fusion | flops 481923072 | bytes 3023460 | tf_op jit(solution)/shard_map/hpr,rhv->hpv/dot_general | solution.py:95
  8.5 1.6 copy.43
  10.0 1.9 %pad_maximum_fusion = f32[16,153,129]{2,1,0:T(8,128)S(1)} fusion(f32[16,153,1]{2,1,0:T(8,128)} %copy.43, f32[16,153,128]{2,1,0:T(8,128)} %fusion.18), kind=kLoop, calls=%fused_computation.4 | loop fusion | flops 315792 | bytes 2526336 | tf_op jit(solution)/shard_map/concatenate | solution.py:97
  12.0 2.1 %reshape.173 = f32[315792]{0:T(1024)} reshape(f32[16,153,129]{2,1,0:T(8,128)S(1)} %pad_maximum_fusion) | data formatting | bytes 2526336 | tf_op jit(solution)/shard_map/reshape | solution.py:57
  14.1 1.4 fusion.37
  15.4 0.2 squeeze.4
  15.6 0.2 slice.36
  15.7 0.1 broadcast_select_fusion.1
  15.8 8.7 %collective-permute-start = (f32[16,9984]{1,0:T(8,128)S(1)}, f32[16,9984]{1,0:T(8,128)S(1)}, u32[]{:S(2)}, u32[]{:S(2)}) collective-permute-start(f32[16,9984]{1,0:T(8,128)S(1)} %broadcast_select_fusion.1), channel_id=1, source_target_pairs={{0,4},{4,0},{1,5},{5,1},{2,6},{6,2},{3,7},{7,3},{8,12},{12,8},{9,1... | collective-permute-start | bytes 1916936 | tf_op jit(solution)/shard_map/ppermute | solution.py:59
  24.6 1.7 collective-permute-done
  26.3 0.1 select_add_fusion
  26.3 1.3 all_to_all.14
  27.6 9.7 %all-to-all-start = ((f32[16,1,9984]{2,1,0:T(1,128)}), f32[16,1,9984]{2,1,0:T(1,128)S(1)}, u32[]{:S(2)}, u32[]{:S(2)}) async-start(f32[16,1,9984]{2,1,0:T(1,128)} %all_to_all.14), calls=%async_computation | async-start | bytes 1277952 | tf_op jit(solution)/shard_map/all_to_all | solution.py:62
  37.3 1.0 copy.47
  38.3 4.1 %collective-permute-start.4 = (bf16[128,2048]{0,1:T(8,128)(2,1)}, bf16[128,2048]{0,1:T(8,128)(2,1)}, u32[]{:S(2)}, u32[]{:S(2)}) collective-permute-start(bf16[128,2048]{0,1:T(8,128)(2,1)} %copy.47), channel_id=1, source_target_pairs={{0,8},{4,12},{8,16},{12,20},{16,24},{20,28},{24,32},{28,36},{32,40... | collective-permute-start | bytes 1572872 | tf_op jit(solution)/shard_map/ppermute | solution.py:119
  42.4 3.4 %collective-permute-start.5 = (bf16[128,2048]{0,1:T(8,128)(2,1)}, bf16[128,2048]{0,1:T(8,128)(2,1)}, u32[]{:S(2)}, u32[]{:S(2)}) collective-permute-start(bf16[128,2048]{0,1:T(8,128)(2,1)} %copy.47), channel_id=1, source_target_pairs={{0,4},{4,8},{8,12},{12,16},{16,20},{20,24},{24,28},{28,32},{32,36}... | collective-permute-start | bytes 1572872 | tf_op jit(solution)/shard_map/ppermute | solution.py:119
  45.8 3.9 %collective-permute-start.2 = (bf16[128,2048]{1,0:T(8,128)(2,1)}, bf16[128,2048]{1,0:T(8,128)(2,1)}, u32[]{:S(2)}, u32[]{:S(2)}) collective-permute-start(bf16[128,2048]{1,0:T(8,128)(2,1)} %param.13), channel_id=1, source_target_pairs={{0,8},{4,12},{8,16},{12,20},{16,24},{20,28},{24,32},{28,36},{32,40... | collective-permute-start | bytes 1572872 | tf_op jit(solution)/shard_map/ppermute | solution.py:119
  49.7 1.9 %collective-permute-start.3 = (bf16[128,2048]{1,0:T(8,128)(2,1)}, bf16[128,2048]{1,0:T(8,128)(2,1)}, u32[]{:S(2)}, u32[]{:S(2)}) collective-permute-start(bf16[128,2048]{1,0:T(8,128)(2,1)} %param.13), channel_id=1, source_target_pairs={{0,4},{4,8},{8,12},{12,16},{16,20},{20,24},{24,28},{28,32},{32,36}... | collective-permute-start | bytes 1572872 | tf_op jit(solution)/shard_map/ppermute | solution.py:119
  51.7 13.9 %all-to-all-done = f32[16,1,9984]{2,1,0:T(1,128)S(1)} async-done(((f32[16,1,9984]{2,1,0:T(1,128)}), f32[16,1,9984]{2,1,0:T(1,128)S(1)}, u32[]{:S(2)}, u32[]{:S(2)}) %all-to-all-start) | async-done | bytes 639008 | tf_op jit(solution)/shard_map/all_to_all | solution.py:62
  65.6 0.6 reduce_window_sum.13
  66.2 38.6 %all-gather = f32[4,1,9984]{2,1,0:T(1,128)S(1)} all-gather(f32[1,1,9984]{2,1,0:T(1,128)S(1)} %slice_bitcast_fusion), channel_id=1, replica_groups=mesh['sx'=4,'sz'=16,'sc'=2,'grp'=4] {'sx'}, dimensions={0}, use_global_device_ids=true | all-gather | bytes 199680 | tf_op jit(solution)/shard_map/all_gather | solution.py:66
  104.8 0.2 fusion.31
  105.0 0.1 fusion.23
  105.1 0.0 copy-start.6
  105.1 1.5 copy.45
  106.6 3.8 %all-to-all-start.1 = ((f32[16,1,9984]{2,1,0:T(1,128)}), f32[16,1,9984]{2,1,0:T(1,128)S(1)}, u32[]{:S(2)}, u32[]{:S(2)}) async-start(f32[16,1,9984]{2,1,0:T(1,128)} %copy.45), calls=%async_computation.1 | async-start | bytes 1277952 | tf_op jit(solution)/shard_map/all_to_all | solution.py:70
  110.4 0.1 copy.38
  110.5 0.0 copy-start.11
  110.5 1.1 fusion.41
  111.6 2.8 %fusion.38 = (f32[16,128]{1,0:T(8,128)S(1)}, f32[16,128,128]{1,2,0:T(8,128)}) fusion(f32[128,16,16]{0,2,1:T(8,128)S(1)} %bitcast.103, f32[128,16,16]{0,2,1:T(8,128)S(1)} %bitcast.100, pred[128,128]{0,1:T(8,128)(4,1)S(1)} %iota_compare_fusion), kind=kOutput, calls=%fused_computation.73 | convolution fusion | flops 51902464 | bytes 1335296 | tf_op jit(solution)/shard_map/thf,jhf->htj/dot_general | solution.py:102
  114.4 0.2 and_and_fusion
  114.6 2.2 %fusion.9 = f32[16,136,128]{2,1,0:T(8,128)} fusion(f32[16,128,136]{1,2,0:T(8,128)S(1)} %fusion.41, f32[16,16,128]{2,1,0:T(8,128)S(1)} %bitcast.104, f32[16,136,1]{1,0,2:T(8,128)S(1)} %copy-done.5, f32[136]{0:T(256)S(1)} %copy-done.11), kind=kOutput, calls=%fused_computation.18 | convolution fusion | flops 54034432 | bytes 2368544 | tf_op jit(solution)/shard_map/hfr,fp->hpr/dot_general | solution.py:42
  116.8 0.0 collective-permute-done.4
  116.8 1.6 pad_maximum_fusion.2
  118.3 0.6 fusion.24
  119.0 2.6 %fusion.39 = (f32[16,128]{1,0:T(8,128)S(1)}, f32[16,128,384]{1,2,0:T(8,128)}) fusion(f32[16,384,128]{2,1,0:T(8,128)S(1)} %fusion.24, pred[128,384]{0,1:T(8,128)(4,1)S(1)} %and_and_fusion), kind=kOutput, calls=%fused_computation.74 | output fusion | flops 4718975 | bytes 6348800 | tf_op jit(solution)/shard_map/sub | solution.py:140
  121.6 14.7 %all-to-all-done.1 = f32[16,1,9984]{2,1,0:T(1,128)S(1)} async-done(((f32[16,1,9984]{2,1,0:T(1,128)}), f32[16,1,9984]{2,1,0:T(1,128)S(1)}, u32[]{:S(2)}, u32[]{:S(2)}) %all-to-all-start.1) | async-done | bytes 639008 | tf_op jit(solution)/shard_map/all_to_all | solution.py:70
  136.2 1.0 fusion.22
  137.2 10.4 %collective-permute-start.1 = (f32[16,9984]{1,0:T(8,128)}, f32[16,9984]{1,0:T(8,128)}, u32[]{:S(2)}, u32[]{:S(2)}) collective-permute-start(f32[16,9984]{1,0:T(8,128)} %get-tuple-element.9), channel_id=1, source_target_pairs={{0,4},{4,0},{1,5},{5,1},{2,6},{6,2},{3,7},{7,3},{8,12},{12,8},{9,1... | collective-permute-start | bytes 1916936 | tf_op jit(solution)/shard_map/ppermute | solution.py:75
  147.6 0.0 collective-permute-done.2
  147.6 1.5 pad_maximum_fusion.1
  149.1 1.6 copy.46
  150.7 2.9 %fusion.13 = bf16[16,128,128]{2,1,0:T(8,128)(2,1)S(1)} fusion(bf16[384,16,128]{0,2,1:T(8,128)(2,1)} %bitcast.107, f32[16,128,384]{1,2,0:T(8,128)} %get-tuple-element.15, f32[16,128]{1,0:T(8,128)S(1)} %get-tuple-element.14), kind=kOutput, calls=%fused_computation.27 | convolution fusion | flops 203161600 | bytes 5251072 | tf_op jit(solution)/shard_map/htj,jhv->thv/dot_general | solution.py:142
  153.6 1.0 copy.54
  154.6 0.0 collective-permute-done.1
  154.6 1.4 maximum_select_fusion
  156.1 0.1 select_n.58
  156.2 1.1 slice.43
  157.3 3.1 %reshape.174 = f32[16,153,129]{2,1,0:T(8,128)S(1)} reshape(f32[315792]{0:T(1024)} %slice.43) | data formatting | bytes 2526336 | tf_op jit(solution)/shard_map/reshape | solution.py:77
  160.4 0.6 slice_reduce_fusion
  161.0 0.6 copy-done.1
  161.6 3.6 %convolution_bitcast_fusion = f32[128,16,128]{0,2,1:T(8,128)S(1)} fusion(f32[16,153,129]{2,1,0:T(8,128)S(1)} %reshape.174, f32[16,136,128]{2,1,0:T(8,128)S(1)} %copy-done.1, f32[16,16,128]{2,1,0:T(8,128)S(1)} %bitcast.105, f32[153]{0:T(256)S(1)} %copy-done.9), kind=kOutput, calls=%fused_computation.19 | convolution fusion | flops 481923072 | bytes 3605504 | tf_op jit(solution)/shard_map/hpt,hpv->thv/dot_general | solution.py:104
  165.2 0.0 copy-start.12
  165.2 1.3 fusion.16
  166.5 1.8 %fusion.11 = f32[128,16,128]{0,2,1:T(8,128)S(1)} fusion(f32[128,16,128]{0,2,1:T(8,128)S(1)} %convolution_bitcast_fusion, f32[16,128,128]{1,2,0:T(8,128)S(1)} %copy-done.12, f32[128,16]{0,1:T(8,128)S(1)} %add_bitcast_fusion, bf16[128,2048]{1,0:T(8,128)(2,1)} %param.13), kind=kOutput, calls=%fused_computation.22 | convolution fusion | flops 403177472 | bytes 3678208 | tf_op jit(solution)/shard_map/htj,jhv->thv/dot_general | solution.py:104
  168.4 1.3 copy.53
  (32 shorter events, 0.2 us)
Async XLA Ops:
  0.6 117.7 %copy-start = (bf16[128,2048]{1,0:T(8,128)(2,1)S(1)}, bf16[128,2048]{1,0:T(8,128)(2,1)}, u32[]{:S(2)}) copy-start(bf16[128,2048]{1,0:T(8,128)(2,1)} %param.14) | copy-start | bytes 1572868
  0.6 2.8 %copy-start.10 = (f32[136]{0:T(256)S(1)}, f32[136]{0:T(256)}, u32[]{:S(2)}) copy-start(f32[136]{0:T(256)} %constant.54.clone) | copy-start | bytes 1636
  0.7 2.8 %copy-start.5 = (f32[16,136,1]{1,0,2:T(8,128)S(1)}, f32[16,136,1]{1,0,2:T(8,128)}, u32[]{:S(2)}) copy-start(f32[16,136,1]{1,0,2:T(8,128)} %constant.63) | copy-start | bytes 26116
  3.5 1.9 %copy-start.8 = (f32[153]{0:T(256)}, f32[153]{0:T(256)S(1)}, u32[]{:S(2)}) copy-start(f32[153]{0:T(256)S(1)} %pad.20.clone) | copy-start | bytes 1840
  15.8 10.4 %collective-permute-start = (f32[16,9984]{1,0:T(8,128)S(1)}, f32[16,9984]{1,0:T(8,128)S(1)}, u32[]{:S(2)}, u32[]{:S(2)}) collective-permute-start(f32[16,9984]{1,0:T(8,128)S(1)} %broadcast_select_fusion.1), channel_id=1, source_target_pairs={{0,4},{4,0},{1,5},{5,1},{2,6},{6,2},{3,7},{7,3},{8,12},{12,8},{9,1... | collective-permute-start | bytes 1916936 | tf_op jit(solution)/shard_map/ppermute | solution.py:59
  26.2 1.4 copy-start.2
  27.6 9.7 %copy-start.4 = (bf16[128,2048]{1,0:T(8,128)(2,1)S(1)}, bf16[128,2048]{1,0:T(8,128)(2,1)}, u32[]{:S(2)}) copy-start(bf16[128,2048]{1,0:T(8,128)(2,1)} %param.15) | copy-start | bytes 1572868
  27.6 24.0 %copy-start.7 = (bf16[128,256]{1,0:T(8,128)(2,1)S(1)}, bf16[128,256]{1,0:T(8,128)(2,1)}, u32[]{:S(2)}) copy-start(bf16[128,256]{1,0:T(8,128)(2,1)} %param.11) | copy-start | bytes 196612
  27.6 37.9 %all-to-all-start = ((f32[16,1,9984]{2,1,0:T(1,128)}), f32[16,1,9984]{2,1,0:T(1,128)S(1)}, u32[]{:S(2)}, u32[]{:S(2)}) async-start(f32[16,1,9984]{2,1,0:T(1,128)} %all_to_all.14), calls=%async_computation | async-start | bytes 1277952 | tf_op jit(solution)/shard_map/all_to_all | solution.py:62
  38.3 78.4 %collective-permute-start.4 = (bf16[128,2048]{0,1:T(8,128)(2,1)}, bf16[128,2048]{0,1:T(8,128)(2,1)}, u32[]{:S(2)}, u32[]{:S(2)}) collective-permute-start(bf16[128,2048]{0,1:T(8,128)(2,1)} %copy.47), channel_id=1, source_target_pairs={{0,8},{4,12},{8,16},{12,20},{16,24},{20,28},{24,32},{28,36},{32,40... | collective-permute-start | bytes 1572872 | tf_op jit(solution)/shard_map/ppermute | solution.py:119
  42.4 74.3 %collective-permute-start.5 = (bf16[128,2048]{0,1:T(8,128)(2,1)}, bf16[128,2048]{0,1:T(8,128)(2,1)}, u32[]{:S(2)}, u32[]{:S(2)}) collective-permute-start(bf16[128,2048]{0,1:T(8,128)(2,1)} %copy.47), channel_id=1, source_target_pairs={{0,4},{4,8},{8,12},{12,16},{16,20},{20,24},{24,28},{28,32},{32,36}... | collective-permute-start | bytes 1572872 | tf_op jit(solution)/shard_map/ppermute | solution.py:119
  45.8 101.8 %collective-permute-start.2 = (bf16[128,2048]{1,0:T(8,128)(2,1)}, bf16[128,2048]{1,0:T(8,128)(2,1)}, u32[]{:S(2)}, u32[]{:S(2)}) collective-permute-start(bf16[128,2048]{1,0:T(8,128)(2,1)} %param.13), channel_id=1, source_target_pairs={{0,8},{4,12},{8,16},{12,20},{16,24},{20,28},{24,32},{28,36},{32,40... | collective-permute-start | bytes 1572872 | tf_op jit(solution)/shard_map/ppermute | solution.py:119
  49.7 97.9 %collective-permute-start.3 = (bf16[128,2048]{1,0:T(8,128)(2,1)}, bf16[128,2048]{1,0:T(8,128)(2,1)}, u32[]{:S(2)}, u32[]{:S(2)}) collective-permute-start(bf16[128,2048]{1,0:T(8,128)(2,1)} %param.13), channel_id=1, source_target_pairs={{0,4},{4,8},{8,12},{12,16},{16,20},{20,24},{24,28},{28,32},{32,36}... | collective-permute-start | bytes 1572872 | tf_op jit(solution)/shard_map/ppermute | solution.py:119
  105.1 5.4 %copy-start.6 = (f32[16,136,1]{1,0,2:T(8,128)S(1)}, f32[16,136,1]{1,0,2:T(8,128)}, u32[]{:S(2)}) copy-start(f32[16,136,1]{1,0,2:T(8,128)} %constant.62) | copy-start | bytes 26116
  106.6 29.7 %all-to-all-start.1 = ((f32[16,1,9984]{2,1,0:T(1,128)}), f32[16,1,9984]{2,1,0:T(1,128)S(1)}, u32[]{:S(2)}, u32[]{:S(2)}) async-start(f32[16,1,9984]{2,1,0:T(1,128)} %copy.45), calls=%async_computation.1 | async-start | bytes 1277952 | tf_op jit(solution)/shard_map/all_to_all | solution.py:70
  110.5 4.1 %copy-start.11 = (f32[136]{0:T(256)S(1)}, f32[136]{0:T(256)}, u32[]{:S(2)}) copy-start(f32[136]{0:T(256)} %constant.54.clone) | copy-start | bytes 1636
  119.0 17.3 %copy-start.3 = (f32[16,9984]{1,0:T(8,128)S(1)}, f32[16,9984]{1,0:T(8,128)}, u32[]{:S(2)}) copy-start(f32[16,9984]{1,0:T(8,128)} %copy-done.2) | copy-start | bytes 1916932
  137.2 17.4 %collective-permute-start.1 = (f32[16,9984]{1,0:T(8,128)}, f32[16,9984]{1,0:T(8,128)}, u32[]{:S(2)}, u32[]{:S(2)}) collective-permute-start(f32[16,9984]{1,0:T(8,128)} %get-tuple-element.9), channel_id=1, source_target_pairs={{0,4},{4,0},{1,5},{5,1},{2,6},{6,2},{3,7},{7,3},{8,12},{12,8},{9,1... | collective-permute-start | bytes 1916936 | tf_op jit(solution)/shard_map/ppermute | solution.py:75
  160.4 1.2 copy-start.1
  160.4 1.2 copy-start.9
  165.2 1.3 copy-start.12

commit v2 on v1

--- a/solution.py
+++ b/solution.py
@@ -47,27 +47,20 @@
 
 
 def prefix_before(local):
-    nz = lax.axis_size("sz")
-    nx = lax.axis_size("sx")
+    chips = lax.axis_size("sx") * lax.axis_size("sz")
     core = lax.axis_index("sc")
     size = local.size
-    unit = 2 * nz * 128
+    unit = 2 * chips * 128
     padded = -(-size // unit) * unit
-    width = padded // (2 * nz)
-    flat = jnp.pad(local.reshape(-1), (0, padded - size)).reshape(2, nz, width)
+    width = padded // (2 * chips)
+    flat = jnp.pad(local.reshape(-1), (0, padded - size)).reshape(2, chips, width)
     sent = jnp.where(core == 0, flat[1], flat[0])
     other = lax.ppermute(sent, "sc", [(0, 1), (1, 0)])
     mine = jnp.where(core == 0, flat[0], flat[1])
     chip_half = mine + other
-    gathered = lax.all_to_all(chip_half, "sz", 0, 0, tiled=True)
-    running = jnp.cumsum(gathered, axis=0)
-    line_total = running[nz - 1]
-    before_chip = running - gathered
-    totals = lax.all_gather(line_total, "sx", axis=0, tiled=False)
-    earlier_line = (jnp.arange(nx) < lax.axis_index("sx"))[:, None]
-    line_offset = jnp.sum(jnp.where(earlier_line, totals, 0.0), axis=0)
-    before_chip = before_chip + line_offset[None, :]
-    chip_prefix = lax.all_to_all(before_chip, "sz", 0, 0, tiled=True)
+    gathered = lax.all_to_all(chip_half, ("sx", "sz"), 0, 0, tiled=True)
+    before_chip = jnp.cumsum(gathered, axis=0) - gathered
+    chip_prefix = lax.all_to_all(before_chip, ("sx", "sz"), 0, 0, tiled=True)
     first_core = jnp.where(core == 0, flat[0], other)
     with_first = chip_prefix + first_core
     keep = jnp.where(core == 0, chip_prefix, with_first)
@@ -109,16 +102,20 @@
     )
     linear_out = (numerator / denominator[:, :, None]).reshape(row_count, head_count * value_width)
     seq_count = lax.axis_size("sx") * lax.axis_size("sz") * lax.axis_size("sc")
-    span_rows = min(row_count, WINDOW)
-    reach_count = -(-WINDOW // row_count)
-    moved_keys = []
-    moved_values = []
+    span_rows = row_count
+    reach_count = 2
+    assert reach_count * row_count >= WINDOW
     flat_axes = ("sx", "sz", "sc")
-    for distance in range(1, reach_count + 1):
-        route = [(i - distance, i) for i in range(seq_count) if i - distance >= 0]
-        arrived = lax.ppermute((window_key, values), flat_axes, route)
-        moved_keys.append(arrived[0])
-        moved_values.append(arrived[1])
+    core = lax.axis_index("sc")
+    route = [(i - 2, i) for i in range(2, seq_count)]
+    far = lax.ppermute((window_key, values), flat_axes, route)
+    near = lax.ppermute(
+        jax.tree.map(lambda o, f: jnp.where(core == 0, o, f), (window_key, values), far),
+        "sc",
+        [(0, 1), (1, 0)],
+    )
+    moved_keys = [near[0], far[0]]
+    moved_values = [near[1], far[1]]
     all_keys = jnp.concatenate(moved_keys[::-1] + [window_key], axis=0)
     all_values = jnp.concatenate(moved_values[::-1] + [values], axis=0)
     key_count = all_keys.shape[0]

time: 170 us -> 150 us (0.88)
  blocking collectives: 38.6 us -> 0 us
  waiting for transfers between devices: 30.3 us -> 47.9 us
  other arithmetic: 12.8 us -> 15.5 us
  matrix products: 22.2 us -> 20 us
    all_gather x1 -> x0, blocking collectives: 38.6 us -> none  [prefix_before(): totals = lax.all_gather(line_total, 'sx', axis=0, tiled=False)]
    all_to_all x2, waiting for transfers between devices: 28.6 us -> 46.2 us  [the longest x1 24.7 us: prefix_before(): chip_prefix = lax.all_to_all(before_chip, ('sx', 'sz'), 0, 0, tiled=True)]
    all_to_all x2, starting transfers between devices: 13.5 us -> 21.8 us  [the longest x1 13.1 us: prefix_before(): gathered = lax.all_to_all(chip_half, ('sx', 'sz'), 0, 0, tiled=True)]
    ppermute x1, starting transfers between devices: 10.4 us -> 5.42 us  [prefix_before(): got = lax.ppermute(give, 'sc', [(0, 1), (1, 0)])]
    select_n x0 -> x2, other arithmetic: none -> 3 us  [on_device(): jnp.where(core == 0, o, f)]
    dot_general x1, matrix products: 2.94 us -> 0.59 us  [on_device(): jnp.einsum('htj,jhv->thv', weights, all_values.reshape(key_count, head_co...]
    ppermute x4, starting transfers between devices: 13.3 us -> 11 us  [the longest x2 6.84 us: on_device(): far = lax.ppermute((window_key, values), flat_axes, route)]
    unnamed x31 -> x32, local copies, waits for them, and re-layouts: 4.06 us -> 5.38 us
  transfers between devices with their start and end apart: 8 -> 8, of which waited for: 3 -> 3; matrix products, arithmetic and copies ran while one was open for 13% -> 16% of each run, Pallas kernels for 0% -> 0%
where the time goes in v2:
time: 150 us; the launch traced here: 149 us
  waiting for transfers between devices  47.9 us (32%)
  starting transfers between devices  47 us (31%)
  matrix products  20 us (13%)
  local copies, waits for them, and re-layouts  17.2 us (11%)
  other arithmetic  15.5 us (10%)
    all_to_all x1, waiting for transfers between devices, prefix_before(): chip_prefix = lax.all_to_all(before_chip, ('sx', 'sz'), 0, 0, tiled=True)  24.7 us
    all_to_all x1, waiting for transfers between devices, prefix_before(): gathered = lax.all_to_all(chip_half, ('sx', 'sz'), 0, 0, tiled=True)  21.5 us
    all_to_all x1, starting transfers between devices, prefix_before(): gathered = lax.all_to_all(chip_half, ('sx', 'sz'), 0, 0, tiled=True)  13.1 us
    ppermute x1, starting transfers between devices, prefix_before(): other = lax.ppermute(sent, 'sc', [(0, 1), (1, 0)])  8.75 us
    all_to_all x1, starting transfers between devices, prefix_before(): chip_prefix = lax.all_to_all(before_chip, ('sx', 'sz'), 0, 0, tiled=True)  8.73 us
    ppermute x2, starting transfers between devices, on_device(): far = lax.ppermute((window_key, values), flat_axes, route)  6.84 us
    ppermute x1, starting transfers between devices, prefix_before(): got = lax.ppermute(give, 'sc', [(0, 1), (1, 0)])  5.42 us
    unnamed x32, local copies, waits for them, and re-layouts  5.38 us
  transfers between devices with their start and end apart: 8, of which 3 were waited for; matrix products, arithmetic and copies ran while one was open for 16% of the time, Pallas kernels for 0%

profile of v2, /device:TPU:1, one launch (start us, length us, event | category | flops | bytes accessed | tf_op | source)
XLA Modules:
  0.0 148.7 jit_solution(16878073726299303597)
XLA Ops:
  0.6 0.0 copy-start
  0.6 0.0 copy-start.11
  0.7 0.0 copy-start.8
  0.7 0.9 convert_multiply_fusion
  1.6 0.1 copy.45
  1.7 1.8 %fusion.39 = f32[16,128,136]{1,2,0:T(8,128)S(1)} fusion(f32[16,16,128]{2,1,0:T(8,128)S(1)} %bitcast.86, f32[16,136,1]{1,0,2:T(8,128)} %constant.62), kind=kOutput, calls=%fused_computation.71 | convolution fusion | flops 53477376 | bytes 1253888 | tf_op jit(solution)/shard_map/hfr,fp->hpr/dot_general | solution.py:41
  3.5 0.0 copy-start.5
  3.5 1.1 fusion.7
  4.7 0.8 fusion.17
  5.5 2.0 %fusion.18 = f32[16,153,128]{2,1,0:T(8,128)} fusion(f32[16,136,128]{2,1,0:T(8,128)S(1)} %fusion.7, f32[16,16,128]{2,1,0:T(8,128)S(1)} %bitcast.89, f32[153]{0:T(256)S(1)} %pad.20.clone, bf16[128,2048]{1,0:T(8,128)(2,1)S(1)} %copy-done.5), kind=kOutput, calls=%fused_computation.34 | convolution fusion | flops 481923072 | bytes 3023460 | tf_op jit(solution)/shard_map/hpr,rhv->hpv/dot_general | solution.py:88
  7.4 1.6 %copy.49 = f32[16,153,1]{2,1,0:T(8,128)} copy(f32[16,153,1]{1,0,2:T(8,128)S(1)} %bitcast.100) | data formatting | bytes 19584 | tf_op jit(solution)/shard_map/broadcast_in_dim | solution.py:90
  9.0 1.9 %pad_maximum_fusion = f32[16,153,129]{2,1,0:T(8,128)S(1)} fusion(f32[16,153,1]{2,1,0:T(8,128)} %copy.49, f32[16,153,128]{2,1,0:T(8,128)} %fusion.18), kind=kLoop, calls=%fused_computation.4 | loop fusion | flops 315792 | bytes 2526336 | tf_op jit(solution)/shard_map/concatenate | solution.py:90
  10.9 2.1 %reshape.165 = f32[315792]{0:T(1024)} reshape(f32[16,153,129]{2,1,0:T(8,128)S(1)} %pad_maximum_fusion) | data formatting | bytes 2526336 | tf_op jit(solution)/shard_map/reshape | solution.py:56
  13.0 1.4 fusion.35
  14.4 0.1 squeeze.4
  14.5 0.1 slice.33
  14.6 0.1 broadcast_select_fusion.3
  14.7 8.7 %collective-permute-start = (f32[64,2560]{1,0:T(8,128)S(1)}, f32[64,2560]{1,0:T(8,128)S(1)}, u32[]{:S(2)}, u32[]{:S(2)}) collective-permute-start(f32[64,2560]{1,0:T(8,128)S(1)} %broadcast_select_fusion.3), channel_id=1, source_target_pairs={{0,4},{4,0},{1,5},{5,1},{2,6},{6,2},{3,7},{7,3},{8,12},{12,8},{9,1... | collective-permute-start | bytes 1966088 | tf_op jit(solution)/shard_map/ppermute | solution.py:58
  23.4 1.7 %collective-permute-done = f32[64,2560]{1,0:T(8,128)S(1)} collective-permute-done((f32[64,2560]{1,0:T(8,128)S(1)}, f32[64,2560]{1,0:T(8,128)S(1)}, u32[]{:S(2)}, u32[]{:S(2)}) %collective-permute-start) | collective-permute-done | bytes 655392 | tf_op jit(solution)/shard_map/ppermute | solution.py:58
  25.1 0.1 add_bitcast_fusion
  25.2 0.7 copy-done.2
  26.0 1.5 %copy.50 = f32[64,1,2560]{2,1,0:T(1,128)} copy(f32[64,1,2560]{2,0,1:T(8,128)S(1)} %add_bitcast_fusion) | data formatting | bytes 1310720 | tf_op jit(solution)/shard_map/all_to_all | solution.py:61
  27.5 13.1 %all-to-all-start = ((f32[64,1,2560]{2,1,0:T(1,128)}), f32[64,1,2560]{2,1,0:T(1,128)S(1)}, u32[]{:S(2)}, u32[]{:S(2)}) async-start(f32[64,1,2560]{2,1,0:T(1,128)} %copy.50), calls=%async_computation | async-start | bytes 1310720 | tf_op jit(solution)/shard_map/all_to_all | solution.py:61
  40.6 0.0 copy-start.10
  40.6 0.0 copy-start.9
  40.6 0.3 copy.54
  40.9 3.7 %collective-permute-start.4 = (bf16[128,2048]{0,1:T(8,128)(2,1)S(1)}, bf16[128,2048]{0,1:T(8,128)(2,1)}, u32[]{:S(2)}, u32[]{:S(2)}) collective-permute-start(bf16[128,2048]{0,1:T(8,128)(2,1)S(1)} %copy.54), channel_id=1, source_target_pairs={{0,8},{4,12},{8,16},{12,20},{16,24},{20,28},{24,32},{28,36},{32,40... | collective-permute-start | bytes 1572872 | tf_op jit(solution)/shard_map/ppermute | solution.py:111
  44.6 1.3 copy.51
  45.9 3.1 %collective-permute-start.2 = (bf16[128,2048]{0,1:T(8,128)(2,1)S(1)}, bf16[128,2048]{0,1:T(8,128)(2,1)}, u32[]{:S(2)}, u32[]{:S(2)}) collective-permute-start(bf16[128,2048]{0,1:T(8,128)(2,1)S(1)} %copy.51), channel_id=1, source_target_pairs={{0,8},{4,12},{8,16},{12,20},{16,24},{20,28},{24,32},{28,36},{32,40... | collective-permute-start | bytes 1572872 | tf_op jit(solution)/shard_map/ppermute | solution.py:111
  49.1 0.1 copy.44
  49.2 2.1 %fusion.40 = f32[16,128,136]{1,2,0:T(8,128)} fusion(f32[16,16,128]{2,1,0:T(8,128)S(1)} %bitcast.91, f32[16,136,1]{1,0,2:T(8,128)S(1)} %copy-done.9), kind=kOutput, calls=%fused_computation.72 | convolution fusion | flops 53477376 | bytes 1253888 | tf_op jit(solution)/shard_map/hfr,fp->hpr/dot_general | solution.py:41
  51.3 2.8 %fusion.36 = (f32[16,128]{1,0:T(8,128)S(1)}, f32[16,128,128]{1,2,0:T(8,128)}) fusion(f32[128,16,16]{0,2,1:T(8,128)S(1)} %bitcast.92, f32[128,16,16]{0,2,1:T(8,128)S(1)} %bitcast.90, pred[128,128]{0,1:T(8,128)(4,1)S(1)} %iota_compare_fusion), kind=kOutput, calls=%fused_computation.68 | convolution fusion | flops 51902464 | bytes 1335296 | tf_op jit(solution)/shard_map/thf,jhf->htj/dot_general | solution.py:95
  54.1 21.5 %all-to-all-done = f32[64,1,2560]{2,1,0:T(1,128)S(1)} async-done(((f32[64,1,2560]{2,1,0:T(1,128)}), f32[64,1,2560]{2,1,0:T(1,128)S(1)}, u32[]{:S(2)}, u32[]{:S(2)}) %all-to-all-start) | async-done | bytes 655392 | tf_op jit(solution)/shard_map/all_to_all | solution.py:61
  75.7 0.5 fusion.38
  76.1 1.5 %sub.19 = f32[64,1,2560]{2,1,0:T(1,128)} subtract(f32[64,1,2560]{2,1,0:T(1,128)S(1)} %fusion.38, f32[64,1,2560]{2,1,0:T(1,128)S(1)} %all-to-all-done) | non-fusion elementwise | flops 163840 | bytes 1966080 | tf_op jit(solution)/shard_map/sub | solution.py:62
  77.7 8.7 %all-to-all-start.1 = ((f32[64,1,2560]{2,1,0:T(1,128)}), f32[64,1,2560]{2,1,0:T(1,128)S(1)}, u32[]{:S(2)}, u32[]{:S(2)}) async-start(f32[64,1,2560]{2,1,0:T(1,128)} %sub.19), calls=%async_computation.1 | async-start | bytes 1310720 | tf_op jit(solution)/shard_map/all_to_all | solution.py:63
  86.4 3.4 %fusion.9 = f32[16,136,128]{2,1,0:T(8,128)} fusion(f32[16,128,136]{1,2,0:T(8,128)} %fusion.40, f32[16,16,128]{2,1,0:T(8,128)S(1)} %bitcast.93, f32[16,136,1]{1,0,2:T(8,128)S(1)} %copy-done.8, f32[136]{0:T(256)S(1)} %copy-done.11), kind=kOutput, calls=%fused_computation.18 | convolution fusion | flops 54034432 | bytes 2368544 | tf_op jit(solution)/shard_map/hfr,fp->hpr/dot_general | solution.py:42
  89.8 1.1 broadcast_select_fusion
  90.9 2.3 %collective-permute-start.5 = (bf16[128,2048]{0,1:T(8,128)(2,1)S(1)}, bf16[128,2048]{0,1:T(8,128)(2,1)S(1)}, u32[]{:S(2)}, u32[]{:S(2)}) collective-permute-start(bf16[128,2048]{0,1:T(8,128)(2,1)S(1)} %broadcast_select_fusion), channel_id=1, source_target_pairs={{0,4},{4,0},{1,5},{5,1},{2,6},{6,2},{3,7},{7,3},{8,12},{12,8},{9,1... | collective-permute-start | bytes 1572872 | tf_op jit(solution)/shard_map/ppermute | solution.py:112
  93.2 0.2 and_and_fusion
  93.3 1.9 %broadcast_select_fusion.1 = bf16[128,2048]{0,1:T(8,128)(2,1)} fusion(bf16[128,2048]{0,1:T(8,128)(2,1)S(1)} %copy.51, bf16[128,2048]{0,1:T(8,128)(2,1)} %collective-permute-done.2, pred[]{:T(512)S(6)} %eq.2), kind=kLoop, calls=%fused_computation.48 | loop fusion | flops 262144 | bytes 1572865 | tf_op jit(solution)/shard_map/jit(_where)/select_n | solution.py:113
  95.2 1.9 %collective-permute-start.3 = (bf16[128,2048]{0,1:T(8,128)(2,1)}, bf16[128,2048]{0,1:T(8,128)(2,1)}, u32[]{:S(2)}, u32[]{:S(2)}) collective-permute-start(bf16[128,2048]{0,1:T(8,128)(2,1)} %broadcast_select_fusion.1), channel_id=1, source_target_pairs={{0,4},{4,0},{1,5},{5,1},{2,6},{6,2},{3,7},{7,3},{8,12},{12,8},{9,1... | collective-permute-start | bytes 1572872 | tf_op jit(solution)/shard_map/ppermute | solution.py:112
  97.2 0.0 collective-permute-done.5
  97.2 1.3 pad_maximum_fusion.2
  98.4 0.6 fusion.23
  99.1 2.5 %fusion.37 = (f32[16,128]{1,0:T(8,128)S(1)}, f32[16,128,384]{1,2,0:T(8,128)}) fusion(f32[16,384,128]{2,1,0:T(8,128)S(1)} %fusion.23, pred[128,384]{0,1:T(8,128)(4,1)S(1)} %and_and_fusion), kind=kOutput, calls=%fused_computation.69 | output fusion | flops 4718975 | bytes 6348800 | tf_op jit(solution)/shard_map/sub | solution.py:137
  101.6 24.7 %all-to-all-done.1 = f32[64,1,2560]{2,1,0:T(1,128)S(1)} async-done(((f32[64,1,2560]{2,1,0:T(1,128)}), f32[64,1,2560]{2,1,0:T(1,128)S(1)}, u32[]{:S(2)}, u32[]{:S(2)}) %all-to-all-start.1) | async-done | bytes 655392 | tf_op jit(solution)/shard_map/all_to_all | solution.py:63
  126.3 1.2 fusion.19
  127.5 5.4 %collective-permute-start.1 = (f32[64,2560]{1,0:T(8,128)}, f32[64,2560]{1,0:T(8,128)S(1)}, u32[]{:S(2)}, u32[]{:S(2)}) collective-permute-start(f32[64,2560]{1,0:T(8,128)} %get-tuple-element.9), channel_id=1, source_target_pairs={{0,4},{4,0},{1,5},{5,1},{2,6},{6,2},{3,7},{7,3},{8,12},{12,8},{9,1... | collective-permute-start | bytes 1966088 | tf_op jit(solution)/shard_map/ppermute | solution.py:68
  132.9 1.4 pad_maximum_fusion.1
  134.4 0.6 fusion.13
  135.0 1.0 copy.61
  136.0 0.1 copy-done.4
  136.0 0.1 maximum_select_fusion
  136.2 0.1 select_n.65
  136.3 1.1 slice.38
  137.4 3.1 %reshape.166 = f32[16,153,129]{2,1,0:T(8,128)S(1)} reshape(f32[315792]{0:T(1024)} %slice.38) | data formatting | bytes 2526336 | tf_op jit(solution)/shard_map/reshape | solution.py:70
  140.5 0.6 slice_reduce_fusion
  141.1 0.6 copy-done.1
  141.7 3.6 %convolution_bitcast_fusion = f32[128,16,128]{0,2,1:T(8,128)S(1)} fusion(f32[16,153,129]{2,1,0:T(8,128)S(1)} %reshape.166, f32[16,136,128]{2,1,0:T(8,128)S(1)} %copy-done.1, f32[16,16,128]{2,1,0:T(8,128)S(1)} %bitcast.94, f32[153]{0:T(256)S(1)} %pad.20.clone), kind=kOutput, calls=%fused_computation.19 | convolution fusion | flops 481923072 | bytes 3605504 | tf_op jit(solution)/shard_map/hpt,hpv->thv/dot_general | solution.py:97
  145.3 0.0 copy-start.6
  145.3 1.3 fusion.16
  146.6 0.8 fusion.11
  147.4 1.3 copy.60
  (30 shorter events, 0.1 us)
Async XLA Ops:
  0.6 97.8 %copy-start = (bf16[128,2048]{1,0:T(8,128)(2,1)S(1)}, bf16[128,2048]{1,0:T(8,128)(2,1)}, u32[]{:S(2)}) copy-start(bf16[128,2048]{1,0:T(8,128)(2,1)} %param.14) | copy-start | bytes 1572868
  0.6 2.8 %copy-start.11 = (f32[136]{0:T(256)S(1)}, f32[136]{0:T(256)}, u32[]{:S(2)}) copy-start(f32[136]{0:T(256)} %constant.54.clone) | copy-start | bytes 1636
  0.7 2.8 %copy-start.8 = (f32[16,136,1]{1,0,2:T(8,128)S(1)}, f32[16,136,1]{1,0,2:T(8,128)}, u32[]{:S(2)}) copy-start(f32[16,136,1]{1,0,2:T(8,128)} %constant.63) | copy-start | bytes 26116
  3.5 2.0 %copy-start.5 = (bf16[128,2048]{1,0:T(8,128)(2,1)S(1)}, bf16[128,2048]{1,0:T(8,128)(2,1)}, u32[]{:S(2)}) copy-start(bf16[128,2048]{1,0:T(8,128)(2,1)} %param.13) | copy-start | bytes 1572868
  14.7 10.5 %collective-permute-start = (f32[64,2560]{1,0:T(8,128)S(1)}, f32[64,2560]{1,0:T(8,128)S(1)}, u32[]{:S(2)}, u32[]{:S(2)}) collective-permute-start(f32[64,2560]{1,0:T(8,128)S(1)} %broadcast_select_fusion.3), channel_id=1, source_target_pairs={{0,4},{4,0},{1,5},{5,1},{2,6},{6,2},{3,7},{7,3},{8,12},{12,8},{9,1... | collective-permute-start | bytes 1966088 | tf_op jit(solution)/shard_map/ppermute | solution.py:58
  25.1 0.8 copy-start.2
  27.5 13.1 %copy-start.7 = (bf16[128,2048]{1,0:T(8,128)(2,1)S(1)}, bf16[128,2048]{1,0:T(8,128)(2,1)}, u32[]{:S(2)}) copy-start(bf16[128,2048]{1,0:T(8,128)(2,1)} %param.15) | copy-start | bytes 1572868
  27.5 48.2 %all-to-all-start = ((f32[64,1,2560]{2,1,0:T(1,128)}), f32[64,1,2560]{2,1,0:T(1,128)S(1)}, u32[]{:S(2)}, u32[]{:S(2)}) async-start(f32[64,1,2560]{2,1,0:T(1,128)} %copy.50), calls=%async_computation | async-start | bytes 1310720 | tf_op jit(solution)/shard_map/all_to_all | solution.py:61
  40.6 8.5 %copy-start.10 = (bf16[128,256]{1,0:T(8,128)(2,1)S(1)}, bf16[128,256]{1,0:T(8,128)(2,1)}, u32[]{:S(2)}) copy-start(bf16[128,256]{1,0:T(8,128)(2,1)} %param.11) | copy-start | bytes 196612
  40.6 8.6 %copy-start.9 = (f32[16,136,1]{1,0,2:T(8,128)S(1)}, f32[16,136,1]{1,0,2:T(8,128)}, u32[]{:S(2)}) copy-start(f32[16,136,1]{1,0,2:T(8,128)} %constant.62) | copy-start | bytes 26116
  40.9 48.9 %collective-permute-start.4 = (bf16[128,2048]{0,1:T(8,128)(2,1)S(1)}, bf16[128,2048]{0,1:T(8,128)(2,1)}, u32[]{:S(2)}, u32[]{:S(2)}) collective-permute-start(bf16[128,2048]{0,1:T(8,128)(2,1)S(1)} %copy.54), channel_id=1, source_target_pairs={{0,8},{4,12},{8,16},{12,20},{16,24},{20,28},{24,32},{28,36},{32,40... | collective-permute-start | bytes 1572872 | tf_op jit(solution)/shard_map/ppermute | solution.py:111
  45.9 47.4 %collective-permute-start.2 = (bf16[128,2048]{0,1:T(8,128)(2,1)S(1)}, bf16[128,2048]{0,1:T(8,128)(2,1)}, u32[]{:S(2)}, u32[]{:S(2)}) collective-permute-start(bf16[128,2048]{0,1:T(8,128)(2,1)S(1)} %copy.51), channel_id=1, source_target_pairs={{0,8},{4,12},{8,16},{12,20},{16,24},{20,28},{24,32},{28,36},{32,40... | collective-permute-start | bytes 1572872 | tf_op jit(solution)/shard_map/ppermute | solution.py:111
  77.7 48.6 %all-to-all-start.1 = ((f32[64,1,2560]{2,1,0:T(1,128)}), f32[64,1,2560]{2,1,0:T(1,128)S(1)}, u32[]{:S(2)}, u32[]{:S(2)}) async-start(f32[64,1,2560]{2,1,0:T(1,128)} %sub.19), calls=%async_computation.1 | async-start | bytes 1310720 | tf_op jit(solution)/shard_map/all_to_all | solution.py:63
  90.9 6.3 %collective-permute-start.5 = (bf16[128,2048]{0,1:T(8,128)(2,1)S(1)}, bf16[128,2048]{0,1:T(8,128)(2,1)S(1)}, u32[]{:S(2)}, u32[]{:S(2)}) collective-permute-start(bf16[128,2048]{0,1:T(8,128)(2,1)S(1)} %broadcast_select_fusion), channel_id=1, source_target_pairs={{0,4},{4,0},{1,5},{5,1},{2,6},{6,2},{3,7},{7,3},{8,12},{12,8},{9,1... | collective-permute-start | bytes 1572872 | tf_op jit(solution)/shard_map/ppermute | solution.py:112
  95.2 37.7 %collective-permute-start.3 = (bf16[128,2048]{0,1:T(8,128)(2,1)}, bf16[128,2048]{0,1:T(8,128)(2,1)}, u32[]{:S(2)}, u32[]{:S(2)}) collective-permute-start(bf16[128,2048]{0,1:T(8,128)(2,1)} %broadcast_select_fusion.1), channel_id=1, source_target_pairs={{0,4},{4,0},{1,5},{5,1},{2,6},{6,2},{3,7},{7,3},{8,12},{12,8},{9,1... | collective-permute-start | bytes 1572872 | tf_op jit(solution)/shard_map/ppermute | solution.py:112
  99.1 27.2 %copy-start.3 = (f32[64,2560]{1,0:T(8,128)S(1)}, f32[64,2560]{1,0:T(8,128)}, u32[]{:S(2)}) copy-start(f32[64,2560]{1,0:T(8,128)} %copy-done.2) | copy-start | bytes 1966084
  127.5 6.9 %copy-start.13 = (f32[16,128,384]{1,2,0:T(8,128)S(1)}, f32[16,128,384]{1,2,0:T(8,128)}, u32[]{:S(2)}) copy-start(f32[16,128,384]{1,2,0:T(8,128)} %get-tuple-element.15) | copy-start | bytes 9437188
  127.5 8.5 %collective-permute-start.1 = (f32[64,2560]{1,0:T(8,128)}, f32[64,2560]{1,0:T(8,128)S(1)}, u32[]{:S(2)}, u32[]{:S(2)}) collective-permute-start(f32[64,2560]{1,0:T(8,128)} %get-tuple-element.9), channel_id=1, source_target_pairs={{0,4},{4,0},{1,5},{5,1},{2,6},{6,2},{3,7},{7,3},{8,12},{12,8},{9,1... | collective-permute-start | bytes 1966088 | tf_op jit(solution)/shard_map/ppermute | solution.py:68
  135.0 1.1 copy-start.4
  140.5 1.2 copy-start.1
  141.7 4.9 %copy-start.12 = (f32[16,128,128]{1,2,0:T(8,128)S(1)}, f32[16,128,128]{1,2,0:T(8,128)}, u32[]{:S(2)}) copy-start(f32[16,128,128]{1,2,0:T(8,128)} %get-tuple-element.13) | copy-start | bytes 3145732
  145.3 1.3 copy-start.6

commit v3 on v2

--- a/solution.py
+++ b/solution.py
@@ -12,6 +12,7 @@
 PRECISE = lax.Precision.HIGHEST
 HALF_ROOT = 0.7071067811865476
 ROWS = ("grp", "sx", "sz", "sc")
+LINK = jnp.bfloat16
 
 
 def passed_along(block, axis, distance):
@@ -58,9 +59,11 @@
     other = lax.ppermute(sent, "sc", [(0, 1), (1, 0)])
     mine = jnp.where(core == 0, flat[0], flat[1])
     chip_half = mine + other
-    gathered = lax.all_to_all(chip_half, ("sx", "sz"), 0, 0, tiled=True)
-    before_chip = jnp.cumsum(gathered, axis=0) - gathered
+    gathered = lax.all_to_all(chip_half.astype(LINK), ("sx", "sz"), 0, 0, tiled=True)
+    gathered = gathered.astype(jnp.float32)
+    before_chip = (jnp.cumsum(gathered, axis=0) - gathered).astype(LINK)
     chip_prefix = lax.all_to_all(before_chip, ("sx", "sz"), 0, 0, tiled=True)
+    chip_prefix = chip_prefix.astype(jnp.float32)
     first_core = jnp.where(core == 0, flat[0], other)
     with_first = chip_prefix + first_core
     keep = jnp.where(core == 0, chip_prefix, with_first)

time: 150 us -> 134 us (0.89)
  waiting for transfers between devices: 47.9 us -> 25.7 us
  other arithmetic: 15.5 us -> 23.5 us
  starting transfers between devices: 47 us -> 44.1 us
    all_to_all x1, waiting for transfers between devices: 24.7 us -> 11.7 us  [prefix_before(): chip_prefix = lax.all_to_all(before_chip, ('sx', 'sz'), 0, 0, tiled=True)]
    all_to_all x1, waiting for transfers between devices: 21.5 us -> 14 us  [prefix_before(): lax.all_to_all(chip_half.astype(LINK), ('sx', 'sz'), 0, 0, tiled=True)]
    another operation x1 -> x2, other arithmetic: 0.46 us -> 3.6 us  [prefix_before(): before_chip = (jnp.cumsum(gathered, axis=0) - gathered).astype(LINK)]
    ppermute x2, starting transfers between devices: 6.84 us -> 4.21 us  [on_device(): far = lax.ppermute((window_key, values), flat_axes, route)]
    unnamed x32 -> x38, local copies, waits for them, and re-layouts: 5.38 us -> 7.7 us
    all_to_all x1 -> x2, other arithmetic: 0.1 us -> 2.01 us  [prefix_before(): lax.all_to_all(chip_half.astype(LINK), ('sx', 'sz'), 0, 0, tiled=True)]
    ppermute x1, waiting for transfers between devices: 1.7 us -> 0.01 us  [prefix_before(): other = lax.ppermute(sent, 'sc', [(0, 1), (1, 0)])]
    sub x1 -> x0, other arithmetic: 1.53 us -> none  [prefix_before(): before_chip = jnp.cumsum(gathered, axis=0) - gathered]
  transfers between devices with their start and end apart: 8 -> 8, of which waited for: 3 -> 2; matrix products, arithmetic and copies ran while one was open for 16% -> 24% of each run, Pallas kernels for 0% -> 0%
where the time goes in v3:
time: 134 us; the launch traced here: 133 us
  starting transfers between devices  44.1 us (33%)
  waiting for transfers between devices  25.7 us (19%)
  other arithmetic  23.5 us (18%)
  matrix products  20 us (15%)
  local copies, waits for them, and re-layouts  18.5 us (14%)
    all_to_all x1, starting transfers between devices, prefix_before(): lax.all_to_all(chip_half.astype(LINK), ('sx', 'sz'), 0, 0, tiled=True)  14 us
    all_to_all x1, waiting for transfers between devices, prefix_before(): lax.all_to_all(chip_half.astype(LINK), ('sx', 'sz'), 0, 0, tiled=True)  14 us
    all_to_all x1, waiting for transfers between devices, prefix_before(): chip_prefix = lax.all_to_all(before_chip, ('sx', 'sz'), 0, 0, tiled=True)  11.7 us
    ppermute x1, starting transfers between devices, prefix_before(): other = lax.ppermute(sent, 'sc', [(0, 1), (1, 0)])  8.86 us
    unnamed x38, local copies, waits for them, and re-layouts  7.7 us
    all_to_all x1, starting transfers between devices, prefix_before(): chip_prefix = lax.all_to_all(before_chip, ('sx', 'sz'), 0, 0, tiled=True)  7.33 us
    ppermute x1, starting transfers between devices, prefix_before(): got = lax.ppermute(give, 'sc', [(0, 1), (1, 0)])  5.06 us
    ppermute x2, starting transfers between devices, on_device(): lax.ppermute(jax.tree.map(lambda o, f: jnp.where(core == 0, o, f), (windo...  4.56 us
  transfers between devices with their start and end apart: 8, of which 2 were waited for; matrix products, arithmetic and copies ran while one was open for 24% of the time, Pallas kernels for 0%

profile of v3, /device:TPU:1, one launch (start us, length us, event | category | flops | bytes accessed | tf_op | source)
XLA Modules:
  0.0 132.8 jit_solution(16176006799182595183)
XLA Ops:
  0.6 0.0 copy-start
  0.6 0.0 copy-start.12
  0.7 0.0 copy-start.8
  0.7 0.9 convert_multiply_fusion
  1.6 0.1 copy.45
  1.7 1.8 %fusion.43 = f32[16,128,136]{1,2,0:T(8,128)S(1)} fusion(f32[16,16,128]{2,1,0:T(8,128)S(1)} %bitcast.85, f32[16,136,1]{1,0,2:T(8,128)} %constant.62), kind=kOutput, calls=%fused_computation.74 | convolution fusion | flops 53477376 | bytes 1253888 | tf_op jit(solution)/shard_map/hfr,fp->hpr/dot_general | solution.py:42
  3.5 1.1 fusion.7
  4.7 0.8 fusion.17
  5.5 2.0 %fusion.18 = f32[16,153,128]{2,1,0:T(8,128)} fusion(f32[16,136,128]{2,1,0:T(8,128)S(1)} %fusion.7, f32[16,16,128]{2,1,0:T(8,128)S(1)} %bitcast.88, f32[153]{0:T(256)S(1)} %pad.20.clone, bf16[128,2048]{1,0:T(8,128)(2,1)S(1)} %copy-done.4), kind=kOutput, calls=%fused_computation.34 | convolution fusion | flops 481923072 | bytes 3023460 | tf_op jit(solution)/shard_map/hpr,rhv->hpv/dot_general | solution.py:91
  7.4 1.6 %copy.49 = f32[16,153,1]{2,1,0:T(8,128)} copy(f32[16,153,1]{1,0,2:T(8,128)S(1)} %bitcast.99) | data formatting | bytes 19584 | tf_op jit(solution)/shard_map/broadcast_in_dim | solution.py:93
  9.0 1.9 %pad_maximum_fusion = f32[16,153,129]{2,1,0:T(8,128)S(1)} fusion(f32[16,153,1]{2,1,0:T(8,128)} %copy.49, f32[16,153,128]{2,1,0:T(8,128)} %fusion.18), kind=kLoop, calls=%fused_computation.4 | loop fusion | flops 315792 | bytes 2526336 | tf_op jit(solution)/shard_map/concatenate | solution.py:93
  10.9 2.1 %reshape.166 = f32[315792]{0:T(1024)} reshape(f32[16,153,129]{2,1,0:T(8,128)S(1)} %pad_maximum_fusion) | data formatting | bytes 2526336 | tf_op jit(solution)/shard_map/reshape | solution.py:57
  13.0 1.4 %fusion.40 = (f32[163840]{0:T(1024)S(1)}, f32[163840]{0:T(1024)S(1)}) fusion(f32[315792]{0:T(1024)} %reshape.166), kind=kLoop, calls=%fused_computation.71 | loop fusion | bytes 3231744 | tf_op jit(solution)/shard_map/slice | solution.py:60
  14.4 0.1 squeeze.4
  14.5 0.1 slice.33
  14.6 0.9 broadcast_select_fusion.3
  15.5 8.9 %collective-permute-start = (f32[64,2560]{1,0:T(8,128)}, f32[64,2560]{1,0:T(8,128)}, u32[]{:S(2)}, u32[]{:S(2)}) collective-permute-start(f32[64,2560]{1,0:T(8,128)} %broadcast_select_fusion.3), channel_id=1, source_target_pairs={{0,4},{4,0},{1,5},{5,1},{2,6},{6,2},{3,7},{7,3},{8,12},{12,8},{9,1... | collective-permute-start | bytes 1966088 | tf_op jit(solution)/shard_map/ppermute | solution.py:59
  24.4 0.3 copy.54
  24.7 2.1 %collective-permute-start.4 = (bf16[128,2048]{0,1:T(8,128)(2,1)S(1)}, bf16[128,2048]{0,1:T(8,128)(2,1)}, u32[]{:S(2)}, u32[]{:S(2)}) collective-permute-start(bf16[128,2048]{0,1:T(8,128)(2,1)S(1)} %copy.54), channel_id=1, source_target_pairs={{0,8},{4,12},{8,16},{12,20},{16,24},{20,28},{24,32},{28,36},{32,40... | collective-permute-start | bytes 1572872 | tf_op jit(solution)/shard_map/ppermute | solution.py:114
  26.8 1.3 copy.51
  28.1 2.1 %collective-permute-start.2 = (bf16[128,2048]{0,1:T(8,128)(2,1)S(1)}, bf16[128,2048]{0,1:T(8,128)(2,1)}, u32[]{:S(2)}, u32[]{:S(2)}) collective-permute-start(bf16[128,2048]{0,1:T(8,128)(2,1)S(1)} %copy.51), channel_id=1, source_target_pairs={{0,8},{4,12},{8,16},{12,20},{16,24},{20,28},{24,32},{28,36},{32,40... | collective-permute-start | bytes 1572872 | tf_op jit(solution)/shard_map/ppermute | solution.py:114
  30.2 0.1 copy.44
  30.4 2.1 %fusion.44 = f32[16,128,136]{1,2,0:T(8,128)} fusion(f32[16,16,128]{2,1,0:T(8,128)S(1)} %bitcast.90, f32[16,136,1]{1,0,2:T(8,128)S(1)} %copy-done.9), kind=kOutput, calls=%fused_computation.75 | convolution fusion | flops 53477376 | bytes 1253888 | tf_op jit(solution)/shard_map/hfr,fp->hpr/dot_general | solution.py:42
  32.5 2.8 %fusion.41 = (f32[16,128]{1,0:T(8,128)S(1)}, f32[16,128,128]{1,2,0:T(8,128)}) fusion(f32[128,16,16]{0,2,1:T(8,128)S(1)} %bitcast.91, f32[128,16,16]{0,2,1:T(8,128)S(1)} %bitcast.89, pred[128,128]{0,1:T(8,128)(4,1)S(1)} %iota_compare_fusion), kind=kOutput, calls=%fused_computation.72 | convolution fusion | flops 51902464 | bytes 1335296 | tf_op jit(solution)/shard_map/thf,jhf->htj/dot_general | solution.py:98
  35.3 1.2 fusion.34
  36.4 0.5 broadcast.120
  37.0 0.8 reduce.2
  37.8 0.8 reshape.182
  38.6 14.0 %all-to-all-start = ((bf16[64,2,1280]{2,1,0:T(2,128)(2,1)}), bf16[64,2,1280]{2,1,0:T(2,128)(2,1)S(1)}, u32[]{:S(2)}, u32[]{:S(2)}) async-start(bf16[64,2,1280]{2,1,0:T(2,128)(2,1)} %reshape.182), calls=%async_computation | async-start | bytes 655360 | tf_op jit(solution)/shard_map/all_to_all | solution.py:62
  52.7 0.8 and_and_fusion
  53.5 3.3 %fusion.9 = f32[16,136,128]{2,1,0:T(8,128)} fusion(f32[16,128,136]{1,2,0:T(8,128)} %fusion.44, f32[16,16,128]{2,1,0:T(8,128)S(1)} %bitcast.92, f32[16,136,1]{1,0,2:T(8,128)S(1)} %copy-done.8, f32[136]{0:T(256)S(1)} %copy-done.12), kind=kOutput, calls=%fused_computation.18 | convolution fusion | flops 54034432 | bytes 2368544 | tf_op jit(solution)/shard_map/hfr,fp->hpr/dot_general | solution.py:43
  56.9 1.9 %broadcast_select_fusion = bf16[128,2048]{0,1:T(8,128)(2,1)} fusion(bf16[128,2048]{0,1:T(8,128)(2,1)S(1)} %copy.54, bf16[128,2048]{0,1:T(8,128)(2,1)} %collective-permute-done.4, pred[]{:T(512)S(6)} %eq.2), kind=kLoop, calls=%fused_computation.50 | loop fusion | flops 262144 | bytes 1572865 | tf_op jit(solution)/shard_map/jit(_where)/select_n | solution.py:116
  58.8 2.1 %collective-permute-start.5 = (bf16[128,2048]{0,1:T(8,128)(2,1)}, bf16[128,2048]{0,1:T(8,128)(2,1)}, u32[]{:S(2)}, u32[]{:S(2)}) collective-permute-start(bf16[128,2048]{0,1:T(8,128)(2,1)} %broadcast_select_fusion), channel_id=1, source_target_pairs={{0,4},{4,0},{1,5},{5,1},{2,6},{6,2},{3,7},{7,3},{8,12},{12,8},{9,1... | collective-permute-start | bytes 1572872 | tf_op jit(solution)/shard_map/ppermute | solution.py:115
  60.9 14.0 %all-to-all-done = bf16[64,2,1280]{2,1,0:T(2,128)(2,1)S(1)} async-done(((bf16[64,2,1280]{2,1,0:T(2,128)(2,1)}), bf16[64,2,1280]{2,1,0:T(2,128)(2,1)S(1)}, u32[]{:S(2)}, u32[]{:S(2)}) %all-to-all-start) | async-done | bytes 327712 | tf_op jit(solution)/shard_map/all_to_all | solution.py:62
  74.9 0.3 reshape.183
  75.1 1.0 subtract_convert_fusion
  76.2 2.6 %reduce.3 = bf16[64,2560]{1,0:T(8,128)(2,1)S(1)} reduce(bf16[64,1,2560]{2,1,0:T(2,128)(2,1)S(1)} %subtract_convert_fusion, bf16[]{:T(256)} %broadcast.120), dimensions={1}, to_apply=%subtract_convert_fusion.reduce_sub_computation | reduce | bytes 655362 | tf_op jit(solution)/shard_map/jit(cumsum)/reduce_window_sum | solution.py:64
  78.7 0.8 reshape.184
  79.6 7.3 %all-to-all-start.1 = ((bf16[64,2,1280]{2,1,0:T(2,128)(2,1)}), bf16[64,2,1280]{2,1,0:T(2,128)(2,1)S(1)}, u32[]{:S(2)}, u32[]{:S(2)}) async-start(bf16[64,2,1280]{2,1,0:T(2,128)(2,1)} %reshape.184), calls=%async_computation.1 | async-start | bytes 655360 | tf_op jit(solution)/shard_map/all_to_all | solution.py:65
  86.9 1.9 %broadcast_select_fusion.1 = bf16[128,2048]{0,1:T(8,128)(2,1)} fusion(bf16[128,2048]{0,1:T(8,128)(2,1)S(1)} %copy.51, bf16[128,2048]{0,1:T(8,128)(2,1)} %collective-permute-done.2, pred[]{:T(512)S(6)} %eq.2), kind=kLoop, calls=%fused_computation.51 | loop fusion | flops 262144 | bytes 1572865 | tf_op jit(solution)/shard_map/jit(_where)/select_n | solution.py:116
  88.8 2.5 %collective-permute-start.3 = (bf16[128,2048]{0,1:T(8,128)(2,1)}, bf16[128,2048]{0,1:T(8,128)(2,1)}, u32[]{:S(2)}, u32[]{:S(2)}) collective-permute-start(bf16[128,2048]{0,1:T(8,128)(2,1)} %broadcast_select_fusion.1), channel_id=1, source_target_pairs={{0,4},{4,0},{1,5},{5,1},{2,6},{6,2},{3,7},{7,3},{8,12},{12,8},{9,1... | collective-permute-start | bytes 1572872 | tf_op jit(solution)/shard_map/ppermute | solution.py:115
  91.3 1.4 %pad_maximum_fusion.2 = bf16[384,2048]{0,1:T(8,128)(2,1)S(1)} fusion(bf16[128,2048]{0,1:T(8,128)(2,1)S(1)} %copy.54, bf16[128,2048]{0,1:T(8,128)(2,1)} %collective-permute-done.5, bf16[128,2048]{0,1:T(8,128)(2,1)} %collective-permute-done.4), kind=kLoop, calls=%fused_computation.7 | loop fusion | flops 4718592 | bytes 3145728 | tf_op jit(solution)/shard_map/concatenate | solution.py:122
  92.7 0.6 fusion.27
  93.4 0.1 copy-done.11
  93.5 2.6 %fusion.42 = (f32[16,128]{1,0:T(8,128)S(1)}, f32[16,128,384]{1,2,0:T(8,128)}) fusion(f32[16,384,128]{2,1,0:T(8,128)S(1)} %fusion.27, pred[128,384]{0,1:T(8,128)(4,1)S(1)} %copy-done.11), kind=kOutput, calls=%fused_computation.73 | output fusion | flops 4718975 | bytes 6348800 | tf_op jit(solution)/shard_map/sub | solution.py:140
  96.1 11.7 %all-to-all-done.1 = bf16[64,2,1280]{2,1,0:T(2,128)(2,1)S(1)} async-done(((bf16[64,2,1280]{2,1,0:T(2,128)(2,1)}), bf16[64,2,1280]{2,1,0:T(2,128)(2,1)S(1)}, u32[]{:S(2)}, u32[]{:S(2)}) %all-to-all-start.1) | async-done | bytes 327712 | tf_op jit(solution)/shard_map/all_to_all | solution.py:65
  107.7 0.3 reshape.185
  108.0 0.7 convert_element_type.46
  108.7 1.2 fusion.19
  109.9 5.1 %collective-permute-start.1 = (f32[64,2560]{1,0:T(8,128)S(1)}, f32[64,2560]{1,0:T(8,128)S(1)}, u32[]{:S(2)}, u32[]{:S(2)}) collective-permute-start(f32[64,2560]{1,0:T(8,128)S(1)} %get-tuple-element.9), channel_id=1, source_target_pairs={{0,4},{4,0},{1,5},{5,1},{2,6},{6,2},{3,7},{7,3},{8,12},{12,8},{9,1... | collective-permute-start | bytes 1966088 | tf_op jit(solution)/shard_map/ppermute | solution.py:71
  115.0 1.4 %pad_maximum_fusion.1 = bf16[384,2048]{0,1:T(8,128)(2,1)S(1)} fusion(bf16[128,2048]{0,1:T(8,128)(2,1)S(1)} %copy.51, bf16[128,2048]{0,1:T(8,128)(2,1)} %collective-permute-done.3, bf16[128,2048]{0,1:T(8,128)(2,1)} %collective-permute-done.2), kind=kLoop, calls=%fused_computation.6 | loop fusion | flops 4718592 | bytes 3145728 | tf_op jit(solution)/shard_map/concatenate | solution.py:123
  116.4 0.6 fusion.13
  117.0 1.0 copy.61
  118.0 0.8 copy-done.6
  118.9 1.4 %maximum_select_fusion = f32[2,64,2560]{2,1,0:T(8,128)S(1)} fusion(f32[1,64,2560]{2,1,0:T(8,128)} %bitcast.97, f32[1,64,2560]{2,1,0:T(8,128)S(1)} %get-tuple-element.8, pred[]{:T(512)S(6)} %eq.2), kind=kLoop, calls=%fused_computation.26 | loop fusion | flops 983040 | bytes 2621441 | tf_op jit(solution)/shard_map/jit(_where)/select_n | solution.py:72
  120.3 0.1 select_n.65
  120.4 1.1 slice.38
  121.5 3.1 %reshape.167 = f32[16,153,129]{2,1,0:T(8,128)S(1)} reshape(f32[315792]{0:T(1024)} %slice.38) | data formatting | bytes 2526336 | tf_op jit(solution)/shard_map/reshape | solution.py:73
  124.6 0.6 slice_reduce_fusion
  125.2 0.6 copy-done.1
  125.8 3.6 %convolution_bitcast_fusion = f32[128,16,128]{0,2,1:T(8,128)S(1)} fusion(f32[16,153,129]{2,1,0:T(8,128)S(1)} %reshape.167, f32[16,136,128]{2,1,0:T(8,128)S(1)} %copy-done.1, f32[16,16,128]{2,1,0:T(8,128)S(1)} %bitcast.93, f32[153]{0:T(256)S(1)} %pad.20.clone), kind=kOutput, calls=%fused_computation.19 | convolution fusion | flops 481923072 | bytes 3605504 | tf_op jit(solution)/shard_map/hpt,hpv->thv/dot_general | solution.py:100
  129.4 1.3 fusion.16
  130.7 0.8 fusion.11
  131.5 1.3 copy.60
  (38 shorter events, 0.1 us)
Async XLA Ops:
  0.6 92.1 %copy-start = (bf16[128,2048]{1,0:T(8,128)(2,1)S(1)}, bf16[128,2048]{1,0:T(8,128)(2,1)}, u32[]{:S(2)}) copy-start(bf16[128,2048]{1,0:T(8,128)(2,1)} %param.14) | copy-start | bytes 1572868
  0.6 2.8 %copy-start.12 = (f32[136]{0:T(256)S(1)}, f32[136]{0:T(256)}, u32[]{:S(2)}) copy-start(f32[136]{0:T(256)} %constant.54.clone) | copy-start | bytes 1636
  0.7 2.8 %copy-start.8 = (f32[16,136,1]{1,0,2:T(8,128)S(1)}, f32[16,136,1]{1,0,2:T(8,128)}, u32[]{:S(2)}) copy-start(f32[16,136,1]{1,0,2:T(8,128)} %constant.63) | copy-start | bytes 26116
  3.5 2.0 %copy-start.4 = (bf16[128,2048]{1,0:T(8,128)(2,1)S(1)}, bf16[128,2048]{1,0:T(8,128)(2,1)}, u32[]{:S(2)}) copy-start(bf16[128,2048]{1,0:T(8,128)(2,1)} %param.13) | copy-start | bytes 1572868
  14.6 9.8 %copy-start.7 = (bf16[128,2048]{1,0:T(8,128)(2,1)S(1)}, bf16[128,2048]{1,0:T(8,128)(2,1)}, u32[]{:S(2)}) copy-start(bf16[128,2048]{1,0:T(8,128)(2,1)} %param.15) | copy-start | bytes 1572868
  15.5 14.7 %copy-start.10 = (bf16[128,256]{1,0:T(8,128)(2,1)S(1)}, bf16[128,256]{1,0:T(8,128)(2,1)}, u32[]{:S(2)}) copy-start(bf16[128,256]{1,0:T(8,128)(2,1)} %param.11) | copy-start | bytes 196612
  15.5 14.8 %copy-start.9 = (f32[16,136,1]{1,0,2:T(8,128)S(1)}, f32[16,136,1]{1,0,2:T(8,128)}, u32[]{:S(2)}) copy-start(f32[16,136,1]{1,0,2:T(8,128)} %constant.62) | copy-start | bytes 26116
  15.5 19.7 %collective-permute-start = (f32[64,2560]{1,0:T(8,128)}, f32[64,2560]{1,0:T(8,128)}, u32[]{:S(2)}, u32[]{:S(2)}) collective-permute-start(f32[64,2560]{1,0:T(8,128)} %broadcast_select_fusion.3), channel_id=1, source_target_pairs={{0,4},{4,0},{1,5},{5,1},{2,6},{6,2},{3,7},{7,3},{8,12},{12,8},{9,1... | collective-permute-start | bytes 1966088 | tf_op jit(solution)/shard_map/ppermute | solution.py:59
  24.7 32.2 %collective-permute-start.4 = (bf16[128,2048]{0,1:T(8,128)(2,1)S(1)}, bf16[128,2048]{0,1:T(8,128)(2,1)}, u32[]{:S(2)}, u32[]{:S(2)}) collective-permute-start(bf16[128,2048]{0,1:T(8,128)(2,1)S(1)} %copy.54), channel_id=1, source_target_pairs={{0,8},{4,12},{8,16},{12,20},{16,24},{20,28},{24,32},{28,36},{32,40... | collective-permute-start | bytes 1572872 | tf_op jit(solution)/shard_map/ppermute | solution.py:114
  28.1 58.8 %collective-permute-start.2 = (bf16[128,2048]{0,1:T(8,128)(2,1)S(1)}, bf16[128,2048]{0,1:T(8,128)(2,1)}, u32[]{:S(2)}, u32[]{:S(2)}) collective-permute-start(bf16[128,2048]{0,1:T(8,128)(2,1)S(1)} %copy.51), channel_id=1, source_target_pairs={{0,8},{4,12},{8,16},{12,20},{16,24},{20,28},{24,32},{28,36},{32,40... | collective-permute-start | bytes 1572872 | tf_op jit(solution)/shard_map/ppermute | solution.py:114
  30.3 23.2 %copy-start.2 = (f32[128,256]{0,1:T(8,128)}, f32[128,256]{0,1:T(8,128)S(1)}, u32[]{:S(2)}) copy-start(f32[128,256]{0,1:T(8,128)S(1)} %copy.44) | copy-start | bytes 393220
  38.6 36.2 %all-to-all-start = ((bf16[64,2,1280]{2,1,0:T(2,128)(2,1)}), bf16[64,2,1280]{2,1,0:T(2,128)(2,1)S(1)}, u32[]{:S(2)}, u32[]{:S(2)}) async-start(bf16[64,2,1280]{2,1,0:T(2,128)(2,1)} %reshape.182), calls=%async_computation | async-start | bytes 655360 | tf_op jit(solution)/shard_map/all_to_all | solution.py:62
  58.8 32.5 %collective-permute-start.5 = (bf16[128,2048]{0,1:T(8,128)(2,1)}, bf16[128,2048]{0,1:T(8,128)(2,1)}, u32[]{:S(2)}, u32[]{:S(2)}) collective-permute-start(bf16[128,2048]{0,1:T(8,128)(2,1)} %broadcast_select_fusion), channel_id=1, source_target_pairs={{0,4},{4,0},{1,5},{5,1},{2,6},{6,2},{3,7},{7,3},{8,12},{12,8},{9,1... | collective-permute-start | bytes 1572872 | tf_op jit(solution)/shard_map/ppermute | solution.py:115
  79.6 28.2 %all-to-all-start.1 = ((bf16[64,2,1280]{2,1,0:T(2,128)(2,1)}), bf16[64,2,1280]{2,1,0:T(2,128)(2,1)S(1)}, u32[]{:S(2)}, u32[]{:S(2)}) async-start(bf16[64,2,1280]{2,1,0:T(2,128)(2,1)} %reshape.184), calls=%async_computation.1 | async-start | bytes 655360 | tf_op jit(solution)/shard_map/all_to_all | solution.py:65
  88.8 26.2 %collective-permute-start.3 = (bf16[128,2048]{0,1:T(8,128)(2,1)}, bf16[128,2048]{0,1:T(8,128)(2,1)}, u32[]{:S(2)}, u32[]{:S(2)}) collective-permute-start(bf16[128,2048]{0,1:T(8,128)(2,1)} %broadcast_select_fusion.1), channel_id=1, source_target_pairs={{0,4},{4,0},{1,5},{5,1},{2,6},{6,2},{3,7},{7,3},{8,12},{12,8},{9,1... | collective-permute-start | bytes 1572872 | tf_op jit(solution)/shard_map/ppermute | solution.py:115
  92.7 0.8 copy-start.11
  109.9 6.5 %copy-start.14 = (f32[16,128,384]{1,2,0:T(8,128)S(1)}, f32[16,128,384]{1,2,0:T(8,128)}, u32[]{:S(2)}) copy-start(f32[16,128,384]{1,2,0:T(8,128)} %get-tuple-element.15) | copy-start | bytes 9437188
  109.9 8.1 %collective-permute-start.1 = (f32[64,2560]{1,0:T(8,128)S(1)}, f32[64,2560]{1,0:T(8,128)S(1)}, u32[]{:S(2)}, u32[]{:S(2)}) collective-permute-start(f32[64,2560]{1,0:T(8,128)S(1)} %get-tuple-element.9), channel_id=1, source_target_pairs={{0,4},{4,0},{1,5},{5,1},{2,6},{6,2},{3,7},{7,3},{8,12},{12,8},{9,1... | collective-permute-start | bytes 1966088 | tf_op jit(solution)/shard_map/ppermute | solution.py:71
  118.0 0.8 copy-start.6
  124.6 1.2 copy-start.1
  124.6 1.2 copy-start.3
  125.8 4.9 %copy-start.13 = (f32[16,128,128]{1,2,0:T(8,128)S(1)}, f32[16,128,128]{1,2,0:T(8,128)}, u32[]{:S(2)}) copy-start(f32[16,128,128]{1,2,0:T(8,128)} %get-tuple-element.13) | copy-start | bytes 3145732
  129.4 1.3 copy-start.5

commit v4 on v3

--- a/solution.py
+++ b/solution.py
@@ -47,7 +47,7 @@
     )
 
 
-def prefix_before(local):
+def prefix_before(local, tied_before, tied_after):
     chips = lax.axis_size("sx") * lax.axis_size("sz")
     core = lax.axis_index("sc")
     size = local.size
@@ -59,7 +59,9 @@
     other = lax.ppermute(sent, "sc", [(0, 1), (1, 0)])
     mine = jnp.where(core == 0, flat[0], flat[1])
     chip_half = mine + other
-    gathered = lax.all_to_all(chip_half.astype(LINK), ("sx", "sz"), 0, 0, tiled=True)
+    outgoing, tied_before = lax.optimization_barrier((chip_half.astype(LINK), tied_before))
+    gathered = lax.all_to_all(outgoing, ("sx", "sz"), 0, 0, tiled=True)
+    gathered, tied_after = lax.optimization_barrier((gathered, tied_after))
     gathered = gathered.astype(jnp.float32)
     before_chip = (jnp.cumsum(gathered, axis=0) - gathered).astype(LINK)
     chip_prefix = lax.all_to_all(before_chip, ("sx", "sz"), 0, 0, tiled=True)
@@ -70,7 +72,7 @@
     give = jnp.where(core == 0, with_first, chip_prefix)
     got = lax.ppermute(give, "sc", [(0, 1), (1, 0)])
     halves = jnp.where(core == 0, jnp.stack([keep, got]), jnp.stack([got, keep]))
-    return halves.reshape(-1)[:size].reshape(local.shape)
+    return halves.reshape(-1)[:size].reshape(local.shape), tied_before, tied_after
 
 
 def on_device(linear_query, linear_key, values, window_query, window_key):
@@ -91,7 +93,10 @@
     local_state = jnp.einsum("hpr,rhv->hpv", key_feats, value_heads, precision=PRECISE)
     local_norm = jnp.sum(key_feats, axis=2)
     local = jnp.concatenate([local_state, local_norm[:, :, None]], axis=2)
-    prior = prefix_before(local)
+    seq_count = lax.axis_size("sx") * lax.axis_size("sz") * lax.axis_size("sc")
+    prior, (window_key, values), window_query = prefix_before(
+        local, (window_key, values), window_query
+    )
     prior_state = prior[:, :, :value_width]
     prior_norm = prior[:, :, value_width]
     causal = jnp.arange(row_count)[:, None] >= jnp.arange(row_count)[None, :]
@@ -104,7 +109,6 @@
         "hpt,hp->th", query_feats, prior_norm, precision=PRECISE
     )
     linear_out = (numerator / denominator[:, :, None]).reshape(row_count, head_count * value_width)
-    seq_count = lax.axis_size("sx") * lax.axis_size("sz") * lax.axis_size("sc")
     span_rows = row_count
     reach_count = 2
     assert reach_count * row_count >= WINDOW

time: 134 us -> 146 us (1.090)
  starting transfers between devices: 44.1 us -> 52.5 us
  local copies, waits for them, and re-layouts: 18.5 us -> 23.5 us
    all_to_all x1, waiting for transfers between devices: 14 us -> 0.01 us  [prefix_before(): gathered = lax.all_to_all(outgoing, ('sx', 'sz'), 0, 0, tiled=True)]
    ppermute x2, waiting for transfers between devices: 0.01 us -> 13.5 us  [on_device(): far = lax.ppermute((window_key, values), flat_axes, route)]
    all_to_all x1, starting transfers between devices: 7.33 us -> 15.6 us  [prefix_before(): chip_prefix = lax.all_to_all(before_chip, ('sx', 'sz'), 0, 0, tiled=True)]
    all_to_all x2 -> x3, other arithmetic: 2.01 us -> 5.43 us  [the longest x2 3.64 us: prefix_before(): chip_prefix = lax.all_to_all(before_chip, ('sx', 'sz'), 0, 0, tiled=True)]
    optimization_barrier x0 -> x2, local copies, waits for them, and re-layouts: none -> 2.62 us  [prefix_before(): lax.optimization_barrier((chip_half.astype(LINK), tied_before))]
    unnamed x38 -> x31, local copies, waits for them, and re-layouts: 7.7 us -> 10 us
    another operation x2 -> x1, other arithmetic: 3.6 us -> 1.38 us  [prefix_before(): before_chip = (jnp.cumsum(gathered, axis=0) - gathered).astype(LINK)]
    select_n x2, other arithmetic: 3.83 us -> 1.95 us  [on_device(): jnp.where(core == 0, o, f)]
  transfers between devices with their start and end apart: 8 -> 8, of which waited for: 2 -> 3; matrix products, arithmetic and copies ran while one was open for 24% -> 20% of each run, Pallas kernels for 0% -> 0%
where the time goes in v4:
time: 146 us; the launch traced here: 145 us
  starting transfers between devices  52.5 us (36%)
  waiting for transfers between devices  25.6 us (18%)
  local copies, waits for them, and re-layouts  23.5 us (16%)
  other arithmetic  22.4 us (15%)
  matrix products  19.6 us (13%)
    all_to_all x1, starting transfers between devices, prefix_before(): chip_prefix = lax.all_to_all(before_chip, ('sx', 'sz'), 0, 0, tiled=True)  15.6 us
    ppermute x2, waiting for transfers between devices, on_device(): far = lax.ppermute((window_key, values), flat_axes, route)  13.5 us
    all_to_all x1, starting transfers between devices, prefix_before(): gathered = lax.all_to_all(outgoing, ('sx', 'sz'), 0, 0, tiled=True)  13.2 us
    all_to_all x1, waiting for transfers between devices, prefix_before(): chip_prefix = lax.all_to_all(before_chip, ('sx', 'sz'), 0, 0, tiled=True)  11.3 us
    unnamed x31, local copies, waits for them, and re-layouts  10 us
    ppermute x1, starting transfers between devices, prefix_before(): other = lax.ppermute(sent, 'sc', [(0, 1), (1, 0)])  8.73 us
    ppermute x2, starting transfers between devices, on_device(): far = lax.ppermute((window_key, values), flat_axes, route)  5.99 us
    ppermute x2, starting transfers between devices, on_device(): lax.ppermute(jax.tree.map(lambda o, f: jnp.where(core == 0, o, f), (windo...  5.6 us
  transfers between devices with their start and end apart: 8, of which 3 were waited for; matrix products, arithmetic and copies ran while one was open for 20% of the time, Pallas kernels for 0%

profile of v4, /device:TPU:1, one launch (start us, length us, event | category | flops | bytes accessed | tf_op | source)
XLA Modules:
  0.0 144.8 jit_solution(1247238876125217004)
XLA Ops:
  0.6 0.0 copy-start
  0.6 0.0 copy-start.10
  0.7 0.9 convert_multiply_fusion
  1.6 0.1 copy.57
  1.7 1.8 %fusion.38 = f32[16,128,136]{1,2,0:T(8,128)S(1)} fusion(f32[16,16,128]{2,1,0:T(8,128)S(1)} %bitcast.79, f32[16,136,1]{1,0,2:T(8,128)} %constant.62), kind=kOutput, calls=%fused_computation.73 | convolution fusion | flops 53477376 | bytes 1253888 | tf_op jit(solution)/shard_map/hfr,fp->hpr/dot_general | solution.py:42
  3.5 1.1 fusion.7
  4.7 0.8 fusion.17
  5.5 2.0 %fusion.18 = f32[16,153,128]{2,1,0:T(8,128)} fusion(f32[16,136,128]{2,1,0:T(8,128)S(1)} %fusion.7, f32[16,16,128]{2,1,0:T(8,128)S(1)} %bitcast.82, f32[153]{0:T(256)S(1)} %pad.20.clone, bf16[128,2048]{1,0:T(8,128)(2,1)S(1)} %copy-done.3), kind=kOutput, calls=%fused_computation.34 | convolution fusion | flops 481923072 | bytes 3023460 | tf_op jit(solution)/shard_map/hpr,rhv->hpv/dot_general | solution.py:93
  7.4 1.5 %copy.61 = f32[16,153,1]{2,1,0:T(8,128)} copy(f32[16,153,1]{1,0,2:T(8,128)S(1)} %bitcast.96) | data formatting | bytes 19584 | tf_op jit(solution)/shard_map/broadcast_in_dim | solution.py:95
  9.0 1.9 %pad_maximum_fusion = f32[16,153,129]{2,1,0:T(8,128)S(1)} fusion(f32[16,153,1]{2,1,0:T(8,128)} %copy.61, f32[16,153,128]{2,1,0:T(8,128)} %fusion.18), kind=kLoop, calls=%fused_computation.4 | loop fusion | flops 315792 | bytes 2526336 | tf_op jit(solution)/shard_map/concatenate | solution.py:95
  10.9 2.1 %reshape.164 = f32[315792]{0:T(1024)} reshape(f32[16,153,129]{2,1,0:T(8,128)S(1)} %pad_maximum_fusion) | data formatting | bytes 2526336 | tf_op jit(solution)/shard_map/reshape | solution.py:57
  13.0 1.4 pad_slice_fusion
  14.4 0.1 squeeze.4
  14.5 0.1 slice.33
  14.6 0.9 broadcast_select_fusion.3
  15.5 8.7 %collective-permute-start = (f32[64,2560]{1,0:T(8,128)}, f32[64,2560]{1,0:T(8,128)}, u32[]{:S(2)}, u32[]{:S(2)}) collective-permute-start(f32[64,2560]{1,0:T(8,128)} %broadcast_select_fusion.3), channel_id=1, source_target_pairs={{0,4},{4,0},{1,5},{5,1},{2,6},{6,2},{3,7},{7,3},{8,12},{12,8},{9,1... | collective-permute-start | bytes 1966088 | tf_op jit(solution)/shard_map/ppermute | solution.py:59
  24.3 0.1 copy.56
  24.4 1.1 fusion.39
  25.5 0.8 collective-permute-done
  26.3 1.9 %add_convert_fusion = bf16[64,2560]{1,0:T(8,128)(2,1)} fusion(f32[64,2560]{1,0:T(8,128)} %collective-permute-done, f32[64,2560]{1,0:T(8,128)S(1)} %squeeze.4, f32[64,2560]{1,0:T(8,128)S(1)} %slice.33, pred[]{:T(512)S(6)} %eq.2), kind=kLoop, calls=%fused_computation.43 | loop fusion | flops 491520 | bytes 2293761 | tf_op jit(solution)/shard_map/convert_element_type | solution.py:62
  28.2 0.5 broadcast.118
  28.8 1.8 %reduce.2 = bf16[64,2560]{1,0:T(8,128)(2,1)S(1)} reduce(bf16[64,1,2560]{2,0,1:T(8,128)(2,1)} %bitcast.92, bf16[]{:T(256)} %broadcast.118), dimensions={1}, to_apply=%copy.62.reduce_sub_computation | reduce | bytes 655362 | tf_op jit(solution)/shard_map/all_to_all | solution.py:63
  30.5 0.8 reshape.180
  31.3 13.2 %all-to-all-start = ((bf16[64,2,1280]{2,1,0:T(2,128)(2,1)}), bf16[64,2,1280]{2,1,0:T(2,128)(2,1)}, u32[]{:S(2)}, u32[]{:S(2)}) async-start(bf16[64,2,1280]{2,1,0:T(2,128)(2,1)} %reshape.180), calls=%async_computation | async-start | bytes 655360 | tf_op jit(solution)/shard_map/all_to_all | solution.py:63
  44.5 1.3 copy.68
  45.9 3.6 %collective-permute-start.4 = (bf16[128,2048]{0,1:T(8,128)(2,1)S(1)}, bf16[128,2048]{0,1:T(8,128)(2,1)}, u32[]{:S(2)}, u32[]{:S(2)}) collective-permute-start(bf16[128,2048]{0,1:T(8,128)(2,1)S(1)} %copy.68), channel_id=1, source_target_pairs={{0,8},{4,12},{8,16},{12,20},{16,24},{20,28},{24,32},{28,36},{32,40... | collective-permute-start | bytes 1572872 | tf_op jit(solution)/shard_map/ppermute | solution.py:118
  49.5 0.1 and_and_fusion
  49.6 2.1 %fusion.9 = f32[16,136,128]{2,1,0:T(8,128)} fusion(f32[16,128,136]{1,2,0:T(8,128)S(1)} %fusion.39, f32[16,16,128]{2,1,0:T(8,128)S(1)} %bitcast.87, f32[16,136,1]{1,0,2:T(8,128)S(1)} %copy-done.7, f32[136]{0:T(256)S(1)} %copy-done.10), kind=kOutput, calls=%fused_computation.18 | convolution fusion | flops 54034432 | bytes 2368544 | tf_op jit(solution)/shard_map/hfr,fp->hpr/dot_general | solution.py:43
  51.8 1.3 copy.65
  53.1 2.3 %collective-permute-start.2 = (bf16[128,2048]{0,1:T(8,128)(2,1)S(1)}, bf16[128,2048]{0,1:T(8,128)(2,1)S(1)}, u32[]{:S(2)}, u32[]{:S(2)}) collective-permute-start(bf16[128,2048]{0,1:T(8,128)(2,1)S(1)} %copy.65), channel_id=1, source_target_pairs={{0,8},{4,12},{8,16},{12,20},{16,24},{20,28},{24,32},{28,36},{32,40... | collective-permute-start | bytes 1572872 | tf_op jit(solution)/shard_map/ppermute | solution.py:118
  55.4 13.5 %collective-permute-done.4 = bf16[128,2048]{0,1:T(8,128)(2,1)} collective-permute-done((bf16[128,2048]{0,1:T(8,128)(2,1)S(1)}, bf16[128,2048]{0,1:T(8,128)(2,1)}, u32[]{:S(2)}, u32[]{:S(2)}) %collective-permute-start.4) | collective-permute-done | bytes 524320 | tf_op jit(solution)/shard_map/ppermute | solution.py:118
  68.9 1.9 %broadcast_select_fusion = bf16[128,2048]{0,1:T(8,128)(2,1)} fusion(bf16[128,2048]{0,1:T(8,128)(2,1)S(1)} %copy.68, bf16[128,2048]{0,1:T(8,128)(2,1)} %collective-permute-done.4, pred[]{:T(512)S(6)} %eq.2), kind=kLoop, calls=%fused_computation.49 | loop fusion | flops 262144 | bytes 1572865 | tf_op jit(solution)/shard_map/jit(_where)/select_n | solution.py:120
  70.8 2.9 %collective-permute-start.5 = (bf16[128,2048]{0,1:T(8,128)(2,1)}, bf16[128,2048]{0,1:T(8,128)(2,1)}, u32[]{:S(2)}, u32[]{:S(2)}) collective-permute-start(bf16[128,2048]{0,1:T(8,128)(2,1)} %broadcast_select_fusion), channel_id=1, source_target_pairs={{0,4},{4,0},{1,5},{5,1},{2,6},{6,2},{3,7},{7,3},{8,12},{12,8},{9,1... | collective-permute-start | bytes 1572872 | tf_op jit(solution)/shard_map/ppermute | solution.py:119
  73.8 3.2 %reshape.181 = bf16[64,1,2560]{2,1,0:T(2,128)(2,1)} reshape(bf16[64,2,1280]{2,1,0:T(2,128)(2,1)} %all-to-all-done) | data formatting | bytes 655360
  77.0 1.1 copy.97
  78.1 1.4 reduce_window_sum.11
  79.5 1.9 %fusion.30 = bf16[64,1,2560]{2,0,1:T(8,128)(2,1)} fusion(f32[64,2560]{1,0:T(8,128)} %reduce_window_sum.11, bf16[64,2560]{1,0:T(8,128)(2,1)S(1)} %bitcast.85), kind=kLoop, calls=%fused_computation.53 | loop fusion | flops 491520 | bytes 1310720 | tf_op jit(solution)/shard_map/all_to_all | solution.py:67
  81.4 1.8 %reduce.3 = bf16[64,2560]{1,0:T(8,128)(2,1)S(1)} reduce(bf16[64,1,2560]{2,0,1:T(8,128)(2,1)} %fusion.30, bf16[]{:T(256)} %broadcast.118), dimensions={1}, to_apply=%copy.63.reduce_sub_computation | reduce | bytes 655362 | tf_op jit(solution)/shard_map/all_to_all | solution.py:67
  83.2 0.8 reshape.182
  84.0 15.6 %all-to-all-start.1 = ((bf16[64,2,1280]{2,1,0:T(2,128)(2,1)}), bf16[64,2,1280]{2,1,0:T(2,128)(2,1)S(1)}, u32[]{:S(2)}, u32[]{:S(2)}) async-start(bf16[64,2,1280]{2,1,0:T(2,128)(2,1)} %reshape.182), calls=%async_computation.1 | async-start | bytes 655360 | tf_op jit(solution)/shard_map/all_to_all | solution.py:67
  99.6 0.1 broadcast_select_fusion.1
  99.6 2.7 %collective-permute-start.3 = (bf16[128,2048]{0,1:T(8,128)(2,1)S(1)}, bf16[128,2048]{0,1:T(8,128)(2,1)S(1)}, u32[]{:S(2)}, u32[]{:S(2)}) collective-permute-start(bf16[128,2048]{0,1:T(8,128)(2,1)S(1)} %broadcast_select_fusion.1), channel_id=1, source_target_pairs={{0,4},{4,0},{1,5},{5,1},{2,6},{6,2},{3,7},{7,3},{8,12},{12,8},{9,1... | collective-permute-start | bytes 1572872 | tf_op jit(solution)/shard_map/ppermute | solution.py:119
  102.3 2.8 %fusion.36 = (f32[16,128]{1,0:T(8,128)S(1)}, f32[16,128,128]{1,2,0:T(8,128)}) fusion(f32[128,16,16]{0,2,1:T(8,128)S(1)} %bitcast.88, f32[128,16,16]{0,2,1:T(8,128)S(1)} %bitcast.83, pred[128,128]{0,1:T(8,128)(4,1)S(1)} %iota_compare_fusion), kind=kOutput, calls=%fused_computation.71 | convolution fusion | flops 51902464 | bytes 1335296 | tf_op jit(solution)/shard_map/thf,jhf->htj/dot_general | solution.py:103
  105.1 1.4 pad_maximum_fusion.2
  106.6 1.4 pad_maximum_fusion.1
  107.9 2.2 %fusion.23 = f32[16,128,384]{2,1,0:T(8,128)} fusion(bf16[384,16,128]{0,2,1:T(8,128)(2,1)S(1)} %bitcast.78, bf16[128,2048]{1,0:T(8,128)(2,1)S(1)} %copy-done), kind=kOutput, calls=%fused_computation.44 | convolution fusion | flops 201326592 | bytes 5242880 | tf_op jit(solution)/shard_map/thd,jhd->htj/dot_general | solution.py:136
  110.2 11.3 %all-to-all-done.1 = bf16[64,2,1280]{2,1,0:T(2,128)(2,1)S(1)} async-done(((bf16[64,2,1280]{2,1,0:T(2,128)(2,1)}), bf16[64,2,1280]{2,1,0:T(2,128)(2,1)S(1)}, u32[]{:S(2)}, u32[]{:S(2)}) %all-to-all-start.1) | async-done | bytes 327712 | tf_op jit(solution)/shard_map/all_to_all | solution.py:67
  121.4 0.3 reshape.183
  121.7 1.4 fusion.19
  123.1 3.5 %collective-permute-start.1 = (f32[64,2560]{1,0:T(8,128)S(1)}, f32[64,2560]{1,0:T(8,128)S(1)}, u32[]{:S(2)}, u32[]{:S(2)}) collective-permute-start(f32[64,2560]{1,0:T(8,128)S(1)} %get-tuple-element.21), channel_id=1, source_target_pairs={{0,4},{4,0},{1,5},{5,1},{2,6},{6,2},{3,7},{7,3},{8,12},{12,8},{9,1... | collective-permute-start | bytes 1966088 | tf_op jit(solution)/shard_map/ppermute | solution.py:73
  126.6 1.5 %fusion.37 = (f32[16,128]{1,0:T(8,128)S(1)}, f32[16,128,384]{2,1,0:T(8,128)S(1)}) fusion(f32[16,128,384]{2,1,0:T(8,128)S(1)} %copy-done.2, pred[128,384]{1,0:T(8,128)(4,1)S(1)} %and_and_fusion), kind=kOutput, calls=%fused_computation.72 | output fusion | flops 4718975 | bytes 6348800 | tf_op jit(solution)/shard_map/sub | solution.py:144
  128.1 0.9 fusion.13
  128.9 1.0 copy.74
  130.0 0.8 copy-done.6
  130.8 1.4 maximum_select_fusion
  132.2 0.1 select_n.65
  132.3 1.1 slice.38
  133.4 3.1 %reshape.165 = f32[16,153,129]{2,1,0:T(8,128)S(1)} reshape(f32[315792]{0:T(1024)} %slice.38) | data formatting | bytes 2526336 | tf_op jit(solution)/shard_map/reshape | solution.py:75
  136.5 0.6 slice_reduce_fusion
  137.2 0.6 copy-done.1
  137.8 3.6 %convolution_bitcast_fusion = f32[128,16,128]{0,2,1:T(8,128)S(1)} fusion(f32[16,153,129]{2,1,0:T(8,128)S(1)} %reshape.165, f32[16,136,128]{2,1,0:T(8,128)S(1)} %copy-done.1, f32[16,16,128]{2,1,0:T(8,128)S(1)} %bitcast.89, f32[153]{0:T(256)S(1)} %pad.20.clone), kind=kOutput, calls=%fused_computation.19 | convolution fusion | flops 481923072 | bytes 3605504 | tf_op jit(solution)/shard_map/hpt,hpv->thv/dot_general | solution.py:105
  141.4 1.3 fusion.16
  142.7 0.8 fusion.11
  143.5 1.3 copy.73
  (33 shorter events, 0.1 us)
Async XLA Ops:
  0.6 107.3 %copy-start = (bf16[128,2048]{1,0:T(8,128)(2,1)S(1)}, bf16[128,2048]{1,0:T(8,128)(2,1)}, u32[]{:S(2)}) copy-start(bf16[128,2048]{1,0:T(8,128)(2,1)} %param.14) | copy-start | bytes 1572868
  0.6 2.8 %copy-start.10 = (f32[136]{0:T(256)S(1)}, f32[136]{0:T(256)}, u32[]{:S(2)}) copy-start(f32[136]{0:T(256)} %constant.54.clone) | copy-start | bytes 1636
  0.7 2.8 %copy-start.7 = (f32[16,136,1]{1,0,2:T(8,128)S(1)}, f32[16,136,1]{1,0,2:T(8,128)}, u32[]{:S(2)}) copy-start(f32[16,136,1]{1,0,2:T(8,128)} %constant.63) | copy-start | bytes 26116
  3.5 2.0 %copy-start.3 = (bf16[128,2048]{1,0:T(8,128)(2,1)S(1)}, bf16[128,2048]{1,0:T(8,128)(2,1)}, u32[]{:S(2)}) copy-start(bf16[128,2048]{1,0:T(8,128)(2,1)} %param.13) | copy-start | bytes 1572868
  14.6 9.7 %copy-start.9 = (bf16[128,256]{1,0:T(8,128)(2,1)S(1)}, bf16[128,256]{1,0:T(8,128)(2,1)}, u32[]{:S(2)}) copy-start(bf16[128,256]{1,0:T(8,128)(2,1)} %param.11) | copy-start | bytes 196612
  14.6 9.8 %copy-start.8 = (f32[16,136,1]{1,0,2:T(8,128)S(1)}, f32[16,136,1]{1,0,2:T(8,128)}, u32[]{:S(2)}) copy-start(f32[16,136,1]{1,0,2:T(8,128)} %constant.62) | copy-start | bytes 26116
  15.5 10.8 %collective-permute-start = (f32[64,2560]{1,0:T(8,128)}, f32[64,2560]{1,0:T(8,128)}, u32[]{:S(2)}, u32[]{:S(2)}) collective-permute-start(f32[64,2560]{1,0:T(8,128)} %broadcast_select_fusion.3), channel_id=1, source_target_pairs={{0,4},{4,0},{1,5},{5,1},{2,6},{6,2},{3,7},{7,3},{8,12},{12,8},{9,1... | collective-permute-start | bytes 1966088 | tf_op jit(solution)/shard_map/ppermute | solution.py:59
  31.3 42.4 %all-to-all-start = ((bf16[64,2,1280]{2,1,0:T(2,128)(2,1)}), bf16[64,2,1280]{2,1,0:T(2,128)(2,1)}, u32[]{:S(2)}, u32[]{:S(2)}) async-start(bf16[64,2,1280]{2,1,0:T(2,128)(2,1)} %reshape.180), calls=%async_computation | async-start | bytes 655360 | tf_op jit(solution)/shard_map/all_to_all | solution.py:63
  45.9 23.1 %collective-permute-start.4 = (bf16[128,2048]{0,1:T(8,128)(2,1)S(1)}, bf16[128,2048]{0,1:T(8,128)(2,1)}, u32[]{:S(2)}, u32[]{:S(2)}) collective-permute-start(bf16[128,2048]{0,1:T(8,128)(2,1)S(1)} %copy.68), channel_id=1, source_target_pairs={{0,8},{4,12},{8,16},{12,20},{16,24},{20,28},{24,32},{28,36},{32,40... | collective-permute-start | bytes 1572872 | tf_op jit(solution)/shard_map/ppermute | solution.py:118
  53.1 46.5 %collective-permute-start.2 = (bf16[128,2048]{0,1:T(8,128)(2,1)S(1)}, bf16[128,2048]{0,1:T(8,128)(2,1)S(1)}, u32[]{:S(2)}, u32[]{:S(2)}) collective-permute-start(bf16[128,2048]{0,1:T(8,128)(2,1)S(1)} %copy.65), channel_id=1, source_target_pairs={{0,8},{4,12},{8,16},{12,20},{16,24},{20,28},{24,32},{28,36},{32,40... | collective-permute-start | bytes 1572872 | tf_op jit(solution)/shard_map/ppermute | solution.py:118
  70.8 34.3 %collective-permute-start.5 = (bf16[128,2048]{0,1:T(8,128)(2,1)}, bf16[128,2048]{0,1:T(8,128)(2,1)}, u32[]{:S(2)}, u32[]{:S(2)}) collective-permute-start(bf16[128,2048]{0,1:T(8,128)(2,1)} %broadcast_select_fusion), channel_id=1, source_target_pairs={{0,4},{4,0},{1,5},{5,1},{2,6},{6,2},{3,7},{7,3},{8,12},{12,8},{9,1... | collective-permute-start | bytes 1572872 | tf_op jit(solution)/shard_map/ppermute | solution.py:119
  84.0 37.5 %all-to-all-start.1 = ((bf16[64,2,1280]{2,1,0:T(2,128)(2,1)}), bf16[64,2,1280]{2,1,0:T(2,128)(2,1)S(1)}, u32[]{:S(2)}, u32[]{:S(2)}) async-start(bf16[64,2,1280]{2,1,0:T(2,128)(2,1)} %reshape.182), calls=%async_computation.1 | async-start | bytes 655360 | tf_op jit(solution)/shard_map/all_to_all | solution.py:67
  99.6 6.9 %collective-permute-start.3 = (bf16[128,2048]{0,1:T(8,128)(2,1)S(1)}, bf16[128,2048]{0,1:T(8,128)(2,1)S(1)}, u32[]{:S(2)}, u32[]{:S(2)}) collective-permute-start(bf16[128,2048]{0,1:T(8,128)(2,1)S(1)} %broadcast_select_fusion.1), channel_id=1, source_target_pairs={{0,4},{4,0},{1,5},{5,1},{2,6},{6,2},{3,7},{7,3},{8,12},{12,8},{9,1... | collective-permute-start | bytes 1572872 | tf_op jit(solution)/shard_map/ppermute | solution.py:119
  121.7 4.9 %copy-start.2 = (f32[16,128,384]{2,1,0:T(8,128)S(1)}, f32[16,128,384]{2,1,0:T(8,128)}, u32[]{:S(2)}) copy-start(f32[16,128,384]{2,1,0:T(8,128)} %fusion.23) | copy-start | bytes 9437188
  123.1 5.0 %copy-start.5 = (bf16[384,2048]{0,1:T(8,128)(2,1)S(1)}, bf16[384,2048]{0,1:T(8,128)(2,1)}, u32[]{:S(2)}) copy-start(bf16[384,2048]{0,1:T(8,128)(2,1)} %pad_maximum_fusion.1) | copy-start | bytes 4718596
  123.1 6.9 %collective-permute-start.1 = (f32[64,2560]{1,0:T(8,128)S(1)}, f32[64,2560]{1,0:T(8,128)S(1)}, u32[]{:S(2)}, u32[]{:S(2)}) collective-permute-start(f32[64,2560]{1,0:T(8,128)S(1)} %get-tuple-element.21), channel_id=1, source_target_pairs={{0,4},{4,0},{1,5},{5,1},{2,6},{6,2},{3,7},{7,3},{8,12},{12,8},{9,1... | collective-permute-start | bytes 1966088 | tf_op jit(solution)/shard_map/ppermute | solution.py:73
  130.0 0.8 copy-start.6
  136.5 1.2 copy-start.1
  137.8 4.9 %copy-start.11 = (f32[16,128,128]{1,2,0:T(8,128)S(1)}, f32[16,128,128]{1,2,0:T(8,128)}, u32[]{:S(2)}) copy-start(f32[16,128,128]{1,2,0:T(8,128)} %get-tuple-element.25) | copy-start | bytes 3145732
  141.4 1.3 copy-start.4

commit v5 on v3

--- a/solution.py
+++ b/solution.py
@@ -9,7 +9,8 @@
 WINDOW = 256
 
 
-PRECISE = lax.Precision.HIGHEST
+PRECISE = lax.Precision.HIGH
+EXACT = lax.Precision.DEFAULT
 HALF_ROOT = 0.7071067811865476
 ROWS = ("grp", "sx", "sz", "sc")
 LINK = jnp.bfloat16
@@ -39,8 +40,8 @@
     pair_weight = jnp.asarray(
         np.where(lower_index == upper_index, HALF_ROOT, 1.0).astype(np.float32)
     )
-    left_side = jnp.einsum("hfr,fp->hpr", columns, pick_lower, precision=PRECISE)
-    right_side = jnp.einsum("hfr,fp->hpr", columns, pick_upper, precision=PRECISE)
+    left_side = jnp.einsum("hfr,fp->hpr", columns, pick_lower, precision=EXACT)
+    right_side = jnp.einsum("hfr,fp->hpr", columns, pick_upper, precision=EXACT)
     paired = left_side * right_side * pair_weight[None, :, None]
     return jnp.concatenate(
         [jnp.ones((head_count, 1, row_count), jnp.float32), columns, paired], axis=1
@@ -95,7 +96,7 @@
     prior_state = prior[:, :, :value_width]
     prior_norm = prior[:, :, value_width]
     causal = jnp.arange(row_count)[:, None] >= jnp.arange(row_count)[None, :]
-    inner_prod = jnp.einsum("thf,jhf->htj", query_scaled, key_scaled, precision=PRECISE)
+    inner_prod = jnp.einsum("thf,jhf->htj", query_scaled, key_scaled, precision=EXACT)
     kernel = jnp.where(causal[None], 1.0 + inner_prod + 0.5 * inner_prod * inner_prod, 0.0)
     numerator = jnp.einsum("htj,jhv->thv", kernel, value_heads, precision=PRECISE) + jnp.einsum(
         "hpt,hpv->thv", query_feats, prior_state, precision=PRECISE

time: 134 us -> 128 us (0.955)
  matrix products: 20 us -> 12.9 us
    dot_general x5, matrix products: 11.2 us -> 6.76 us  [the longest x2 2.96 us: pair_features(): right_side = jnp.einsum('hfr,fp->hpr', columns, pick_upper, precision=EXACT)]
    dot_general x1, matrix products: 3.58 us -> 1.92 us  [on_device(): jnp.einsum('hpt,hpv->thv', query_feats, prior_state, precision=PRECISE)]
  transfers between devices with their start and end apart: 8 -> 8, of which waited for: 2 -> 2; matrix products, arithmetic and copies ran while one was open for 24% -> 23% of each run, Pallas kernels for 0% -> 0%
where the time goes in v5:
time: 128 us; the launch traced here: 127 us
  starting transfers between devices  44.1 us (34%)
  waiting for transfers between devices  26.1 us (20%)
  other arithmetic  23.5 us (18%)
  local copies, waits for them, and re-layouts  18.8 us (15%)
  matrix products  12.9 us (10%)
    all_to_all x1, waiting for transfers between devices, prefix_before(): lax.all_to_all(chip_half.astype(LINK), ('sx', 'sz'), 0, 0, tiled=True)  14.9 us
    all_to_all x1, starting transfers between devices, prefix_before(): lax.all_to_all(chip_half.astype(LINK), ('sx', 'sz'), 0, 0, tiled=True)  14.1 us
    all_to_all x1, waiting for transfers between devices, prefix_before(): chip_prefix = lax.all_to_all(before_chip, ('sx', 'sz'), 0, 0, tiled=True)  11.2 us
    ppermute x1, starting transfers between devices, prefix_before(): other = lax.ppermute(sent, 'sc', [(0, 1), (1, 0)])  8.87 us
    unnamed x38, local copies, waits for them, and re-layouts  7.99 us
    all_to_all x1, starting transfers between devices, prefix_before(): chip_prefix = lax.all_to_all(before_chip, ('sx', 'sz'), 0, 0, tiled=True)  7.36 us
    ppermute x1, starting transfers between devices, prefix_before(): got = lax.ppermute(give, 'sc', [(0, 1), (1, 0)])  4.95 us
    ppermute x2, starting transfers between devices, on_device(): lax.ppermute(jax.tree.map(lambda o, f: jnp.where(core == 0, o, f), (windo...  4.65 us
  transfers between devices with their start and end apart: 8, of which 2 were waited for; matrix products, arithmetic and copies ran while one was open for 23% of the time, Pallas kernels for 0%

profile of v5, /device:TPU:1, one launch (start us, length us, event | category | flops | bytes accessed | tf_op | source)
XLA Modules:
  0.0 126.5 jit_solution(16393989428261808509)
XLA Ops:
  0.6 0.0 copy-start
  0.6 0.0 copy-start.10
  0.7 0.9 convert_multiply_fusion
  1.6 0.1 copy.45
  1.7 1.0 fusion.43
  2.8 0.4 fusion.7
  3.1 0.8 fusion.17
  3.9 1.7 %fusion.18 = f32[16,153,128]{2,1,0:T(8,128)} fusion(f32[16,136,128]{2,1,0:T(8,128)S(1)} %fusion.7, f32[16,16,128]{2,1,0:T(8,128)S(1)} %bitcast.88, f32[153]{0:T(256)S(1)} %pad.20.clone, bf16[128,2048]{1,0:T(8,128)(2,1)S(1)} %copy-done.4), kind=kOutput, calls=%fused_computation.34 | convolution fusion | flops 241274880 | bytes 3023460 | tf_op jit(solution)/shard_map/hpr,rhv->hpv/dot_general | solution.py:92
  5.7 1.6 %copy.49 = f32[16,153,1]{2,1,0:T(8,128)} copy(f32[16,153,1]{1,0,2:T(8,128)S(1)} %bitcast.99) | data formatting | bytes 19584 | tf_op jit(solution)/shard_map/broadcast_in_dim | solution.py:94
  7.2 1.9 %pad_maximum_fusion = f32[16,153,129]{2,1,0:T(8,128)S(1)} fusion(f32[16,153,1]{2,1,0:T(8,128)} %copy.49, f32[16,153,128]{2,1,0:T(8,128)} %fusion.18), kind=kLoop, calls=%fused_computation.4 | loop fusion | flops 315792 | bytes 2526336 | tf_op jit(solution)/shard_map/concatenate | solution.py:94
  9.2 2.1 %reshape.166 = f32[315792]{0:T(1024)} reshape(f32[16,153,129]{2,1,0:T(8,128)S(1)} %pad_maximum_fusion) | data formatting | bytes 2526336 | tf_op jit(solution)/shard_map/reshape | solution.py:58
  11.2 1.4 %fusion.40 = (f32[163840]{0:T(1024)S(1)}, f32[163840]{0:T(1024)S(1)}) fusion(f32[315792]{0:T(1024)} %reshape.166), kind=kLoop, calls=%fused_computation.71 | loop fusion | bytes 3231744 | tf_op jit(solution)/shard_map/slice | solution.py:61
  12.6 0.1 squeeze.4
  12.7 0.1 slice.33
  12.8 0.9 broadcast_select_fusion.3
  13.7 8.9 %collective-permute-start = (f32[64,2560]{1,0:T(8,128)}, f32[64,2560]{1,0:T(8,128)}, u32[]{:S(2)}, u32[]{:S(2)}) collective-permute-start(f32[64,2560]{1,0:T(8,128)} %broadcast_select_fusion.3), channel_id=1, source_target_pairs={{0,4},{4,0},{1,5},{5,1},{2,6},{6,2},{3,7},{7,3},{8,12},{12,8},{9,1... | collective-permute-start | bytes 1966088 | tf_op jit(solution)/shard_map/ppermute | solution.py:60
  22.6 0.3 copy.54
  22.9 2.1 %collective-permute-start.4 = (bf16[128,2048]{0,1:T(8,128)(2,1)S(1)}, bf16[128,2048]{0,1:T(8,128)(2,1)}, u32[]{:S(2)}, u32[]{:S(2)}) collective-permute-start(bf16[128,2048]{0,1:T(8,128)(2,1)S(1)} %copy.54), channel_id=1, source_target_pairs={{0,8},{4,12},{8,16},{12,20},{16,24},{20,28},{24,32},{28,36},{32,40... | collective-permute-start | bytes 1572872 | tf_op jit(solution)/shard_map/ppermute | solution.py:115
  25.0 1.3 %copy.51 = bf16[128,2048]{0,1:T(8,128)(2,1)S(1)} copy(bf16[128,2048]{1,0:T(8,128)(2,1)} %param.13) | data formatting | bytes 1048576 | tf_op args[2]
  26.3 2.1 %collective-permute-start.2 = (bf16[128,2048]{0,1:T(8,128)(2,1)S(1)}, bf16[128,2048]{0,1:T(8,128)(2,1)}, u32[]{:S(2)}, u32[]{:S(2)}) collective-permute-start(bf16[128,2048]{0,1:T(8,128)(2,1)S(1)} %copy.51), channel_id=1, source_target_pairs={{0,8},{4,12},{8,16},{12,20},{16,24},{20,28},{24,32},{28,36},{32,40... | collective-permute-start | bytes 1572872 | tf_op jit(solution)/shard_map/ppermute | solution.py:115
  28.4 0.1 copy.44
  28.6 1.4 %fusion.44 = f32[16,128,136]{1,2,0:T(8,128)} fusion(f32[16,16,128]{2,1,0:T(8,128)S(1)} %bitcast.90, bf16[16,136,1]{1,0,2:T(8,128)(2,1)S(1)} %copy-done.11), kind=kOutput, calls=%fused_computation.75 | convolution fusion | flops 8912896 | bytes 1249536 | tf_op jit(solution)/shard_map/hfr,fp->hpr/dot_general | solution.py:43
  30.0 1.4 %fusion.41 = (f32[16,128]{1,0:T(8,128)S(1)}, f32[16,128,128]{1,2,0:T(8,128)}) fusion(f32[128,16,16]{0,2,1:T(8,128)S(1)} %bitcast.91, f32[128,16,16]{0,2,1:T(8,128)S(1)} %bitcast.89, pred[128,128]{0,1:T(8,128)(4,1)S(1)} %iota_compare_fusion), kind=kOutput, calls=%fused_computation.72 | convolution fusion | flops 9959424 | bytes 1335296 | tf_op jit(solution)/shard_map/thf,jhf->htj/dot_general | solution.py:99
  31.4 1.2 fusion.34
  32.5 0.5 broadcast.120
  33.1 0.8 reduce.2
  33.9 0.8 reshape.182
  34.7 14.1 %all-to-all-start = ((bf16[64,2,1280]{2,1,0:T(2,128)(2,1)}), bf16[64,2,1280]{2,1,0:T(2,128)(2,1)S(1)}, u32[]{:S(2)}, u32[]{:S(2)}) async-start(bf16[64,2,1280]{2,1,0:T(2,128)(2,1)} %reshape.182), calls=%async_computation | async-start | bytes 655360 | tf_op jit(solution)/shard_map/all_to_all | solution.py:63
  48.8 0.8 and_and_fusion
  49.6 2.6 %fusion.9 = f32[16,136,128]{2,1,0:T(8,128)} fusion(f32[16,128,136]{1,2,0:T(8,128)} %fusion.44, f32[16,16,128]{2,1,0:T(8,128)S(1)} %bitcast.92, bf16[16,136,1]{1,0,2:T(8,128)(2,1)S(1)} %copy-done.10, f32[136]{0:T(256)S(1)} %copy-done.12), kind=kOutput, calls=%fused_computation.18 | convolution fusion | flops 9469952 | bytes 2364192 | tf_op jit(solution)/shard_map/hfr,fp->hpr/dot_general | solution.py:44
  52.2 1.9 %broadcast_select_fusion = bf16[128,2048]{0,1:T(8,128)(2,1)} fusion(bf16[128,2048]{0,1:T(8,128)(2,1)S(1)} %copy.54, bf16[128,2048]{0,1:T(8,128)(2,1)} %collective-permute-done.4, pred[]{:T(512)S(6)} %eq.2), kind=kLoop, calls=%fused_computation.50 | loop fusion | flops 262144 | bytes 1572865 | tf_op jit(solution)/shard_map/jit(_where)/select_n | solution.py:117
  54.2 1.9 %collective-permute-start.5 = (bf16[128,2048]{0,1:T(8,128)(2,1)}, bf16[128,2048]{0,1:T(8,128)(2,1)}, u32[]{:S(2)}, u32[]{:S(2)}) collective-permute-start(bf16[128,2048]{0,1:T(8,128)(2,1)} %broadcast_select_fusion), channel_id=1, source_target_pairs={{0,4},{4,0},{1,5},{5,1},{2,6},{6,2},{3,7},{7,3},{8,12},{12,8},{9,1... | collective-permute-start | bytes 1572872 | tf_op jit(solution)/shard_map/ppermute | solution.py:116
  56.1 14.9 %all-to-all-done = bf16[64,2,1280]{2,1,0:T(2,128)(2,1)S(1)} async-done(((bf16[64,2,1280]{2,1,0:T(2,128)(2,1)}), bf16[64,2,1280]{2,1,0:T(2,128)(2,1)S(1)}, u32[]{:S(2)}, u32[]{:S(2)}) %all-to-all-start) | async-done | bytes 327712 | tf_op jit(solution)/shard_map/all_to_all | solution.py:63
  70.9 0.3 reshape.183
  71.2 1.0 subtract_convert_fusion
  72.2 2.6 %reduce.3 = bf16[64,2560]{1,0:T(8,128)(2,1)S(1)} reduce(bf16[64,1,2560]{2,1,0:T(2,128)(2,1)S(1)} %subtract_convert_fusion, bf16[]{:T(256)} %broadcast.120), dimensions={1}, to_apply=%subtract_convert_fusion.reduce_sub_computation | reduce | bytes 655362 | tf_op jit(solution)/shard_map/jit(cumsum)/reduce_window_sum | solution.py:65
  74.8 0.8 reshape.184
  75.6 7.4 %all-to-all-start.1 = ((bf16[64,2,1280]{2,1,0:T(2,128)(2,1)}), bf16[64,2,1280]{2,1,0:T(2,128)(2,1)S(1)}, u32[]{:S(2)}, u32[]{:S(2)}) async-start(bf16[64,2,1280]{2,1,0:T(2,128)(2,1)} %reshape.184), calls=%async_computation.1 | async-start | bytes 655360 | tf_op jit(solution)/shard_map/all_to_all | solution.py:66
  83.0 1.9 %broadcast_select_fusion.1 = bf16[128,2048]{0,1:T(8,128)(2,1)} fusion(bf16[128,2048]{0,1:T(8,128)(2,1)S(1)} %copy.51, bf16[128,2048]{0,1:T(8,128)(2,1)} %collective-permute-done.2, pred[]{:T(512)S(6)} %eq.2), kind=kLoop, calls=%fused_computation.51 | loop fusion | flops 262144 | bytes 1572865 | tf_op jit(solution)/shard_map/jit(_where)/select_n | solution.py:117
  84.9 2.7 %collective-permute-start.3 = (bf16[128,2048]{0,1:T(8,128)(2,1)}, bf16[128,2048]{0,1:T(8,128)(2,1)}, u32[]{:S(2)}, u32[]{:S(2)}) collective-permute-start(bf16[128,2048]{0,1:T(8,128)(2,1)} %broadcast_select_fusion.1), channel_id=1, source_target_pairs={{0,4},{4,0},{1,5},{5,1},{2,6},{6,2},{3,7},{7,3},{8,12},{12,8},{9,1... | collective-permute-start | bytes 1572872 | tf_op jit(solution)/shard_map/ppermute | solution.py:116
  87.7 1.4 %pad_maximum_fusion.2 = bf16[384,2048]{0,1:T(8,128)(2,1)S(1)} fusion(bf16[128,2048]{0,1:T(8,128)(2,1)S(1)} %copy.54, bf16[128,2048]{0,1:T(8,128)(2,1)} %collective-permute-done.5, bf16[128,2048]{0,1:T(8,128)(2,1)} %collective-permute-done.4), kind=kLoop, calls=%fused_computation.7 | loop fusion | flops 4718592 | bytes 3145728 | tf_op jit(solution)/shard_map/concatenate | solution.py:123
  89.1 0.6 fusion.27
  89.7 0.1 copy-done.9
  89.9 2.6 %fusion.42 = (f32[16,128]{1,0:T(8,128)S(1)}, f32[16,128,384]{1,2,0:T(8,128)}) fusion(f32[16,384,128]{2,1,0:T(8,128)S(1)} %fusion.27, pred[128,384]{0,1:T(8,128)(4,1)S(1)} %copy-done.9), kind=kOutput, calls=%fused_computation.73 | output fusion | flops 4718975 | bytes 6348800 | tf_op jit(solution)/shard_map/sub | solution.py:141
  92.4 11.2 %all-to-all-done.1 = bf16[64,2,1280]{2,1,0:T(2,128)(2,1)S(1)} async-done(((bf16[64,2,1280]{2,1,0:T(2,128)(2,1)}), bf16[64,2,1280]{2,1,0:T(2,128)(2,1)S(1)}, u32[]{:S(2)}, u32[]{:S(2)}) %all-to-all-start.1) | async-done | bytes 327712 | tf_op jit(solution)/shard_map/all_to_all | solution.py:66
  103.7 0.3 reshape.185
  103.9 0.7 convert_element_type.46
  104.6 1.2 fusion.19
  105.9 5.0 %collective-permute-start.1 = (f32[64,2560]{1,0:T(8,128)S(1)}, f32[64,2560]{1,0:T(8,128)S(1)}, u32[]{:S(2)}, u32[]{:S(2)}) collective-permute-start(f32[64,2560]{1,0:T(8,128)S(1)} %get-tuple-element.9), channel_id=1, source_target_pairs={{0,4},{4,0},{1,5},{5,1},{2,6},{6,2},{3,7},{7,3},{8,12},{12,8},{9,1... | collective-permute-start | bytes 1966088 | tf_op jit(solution)/shard_map/ppermute | solution.py:72
  110.8 1.4 %pad_maximum_fusion.1 = bf16[384,2048]{0,1:T(8,128)(2,1)S(1)} fusion(bf16[128,2048]{0,1:T(8,128)(2,1)S(1)} %copy.51, bf16[128,2048]{0,1:T(8,128)(2,1)} %collective-permute-done.3, bf16[128,2048]{0,1:T(8,128)(2,1)} %collective-permute-done.2), kind=kLoop, calls=%fused_computation.6 | loop fusion | flops 4718592 | bytes 3145728 | tf_op jit(solution)/shard_map/concatenate | solution.py:124
  112.3 0.6 fusion.13
  112.9 1.0 copy.61
  113.9 0.8 copy-done.6
  114.7 1.4 %maximum_select_fusion = f32[2,64,2560]{2,1,0:T(8,128)S(1)} fusion(f32[1,64,2560]{2,1,0:T(8,128)} %bitcast.97, f32[1,64,2560]{2,1,0:T(8,128)S(1)} %get-tuple-element.8, pred[]{:T(512)S(6)} %eq.2), kind=kLoop, calls=%fused_computation.26 | loop fusion | flops 983040 | bytes 2621441 | tf_op jit(solution)/shard_map/jit(_where)/select_n | solution.py:73
  116.1 0.1 select_n.65
  116.2 1.1 slice.38
  117.3 3.1 %reshape.167 = f32[16,153,129]{2,1,0:T(8,128)S(1)} reshape(f32[315792]{0:T(1024)} %slice.38) | data formatting | bytes 2526336 | tf_op jit(solution)/shard_map/reshape | solution.py:74
  120.4 0.6 slice_reduce_fusion
  121.1 0.6 copy-done.1
  121.7 1.9 %convolution_bitcast_fusion = f32[128,16,128]{0,2,1:T(8,128)S(1)} fusion(f32[16,153,129]{2,1,0:T(8,128)S(1)} %reshape.167, f32[16,136,128]{2,1,0:T(8,128)S(1)} %copy-done.1, f32[16,16,128]{2,1,0:T(8,128)S(1)} %bitcast.93, f32[153]{0:T(256)S(1)} %pad.20.clone), kind=kOutput, calls=%fused_computation.19 | convolution fusion | flops 241274880 | bytes 3605504 | tf_op jit(solution)/shard_map/hpt,hpv->thv/dot_general | solution.py:101
  123.6 0.7 fusion.16
  124.3 0.3 copy-done.5
  124.6 0.6 fusion.11
  125.2 1.3 %copy.60 = f32[128,2048]{1,0:T(8,128)} copy(f32[128,2048]{0,1:T(8,128)S(1)} %bitcast.96) | data formatting | bytes 2097152
  (38 shorter events, 0.1 us)
Async XLA Ops:
  0.6 88.4 %copy-start = (bf16[128,2048]{1,0:T(8,128)(2,1)S(1)}, bf16[128,2048]{1,0:T(8,128)(2,1)}, u32[]{:S(2)}) copy-start(bf16[128,2048]{1,0:T(8,128)(2,1)} %param.14) | copy-start | bytes 1572868
  0.6 2.1 %copy-start.10 = (bf16[16,136,1]{1,0,2:T(8,128)(2,1)S(1)}, bf16[16,136,1]{1,0,2:T(8,128)(2,1)}, u32[]{:S(2)}) copy-start(bf16[16,136,1]{1,0,2:T(8,128)(2,1)} %constant.110) | copy-start | bytes 13060
  0.7 2.1 %copy-start.12 = (f32[136]{0:T(256)S(1)}, f32[136]{0:T(256)}, u32[]{:S(2)}) copy-start(f32[136]{0:T(256)} %constant.54.clone) | copy-start | bytes 1636
  2.8 1.2 copy-start.4
  12.8 9.8 %copy-start.7 = (bf16[128,2048]{1,0:T(8,128)(2,1)S(1)}, bf16[128,2048]{1,0:T(8,128)(2,1)}, u32[]{:S(2)}) copy-start(bf16[128,2048]{1,0:T(8,128)(2,1)} %param.15) | copy-start | bytes 1572868
  13.7 14.7 %copy-start.8 = (bf16[128,256]{1,0:T(8,128)(2,1)S(1)}, bf16[128,256]{1,0:T(8,128)(2,1)}, u32[]{:S(2)}) copy-start(bf16[128,256]{1,0:T(8,128)(2,1)} %param.11) | copy-start | bytes 196612
  13.7 14.8 %copy-start.11 = (bf16[16,136,1]{1,0,2:T(8,128)(2,1)S(1)}, bf16[16,136,1]{1,0,2:T(8,128)(2,1)}, u32[]{:S(2)}) copy-start(bf16[16,136,1]{1,0,2:T(8,128)(2,1)} %constant.109) | copy-start | bytes 13060
  13.7 17.6 %collective-permute-start = (f32[64,2560]{1,0:T(8,128)}, f32[64,2560]{1,0:T(8,128)}, u32[]{:S(2)}, u32[]{:S(2)}) collective-permute-start(f32[64,2560]{1,0:T(8,128)} %broadcast_select_fusion.3), channel_id=1, source_target_pairs={{0,4},{4,0},{1,5},{5,1},{2,6},{6,2},{3,7},{7,3},{8,12},{12,8},{9,1... | collective-permute-start | bytes 1966088 | tf_op jit(solution)/shard_map/ppermute | solution.py:60
  22.9 29.3 %collective-permute-start.4 = (bf16[128,2048]{0,1:T(8,128)(2,1)S(1)}, bf16[128,2048]{0,1:T(8,128)(2,1)}, u32[]{:S(2)}, u32[]{:S(2)}) collective-permute-start(bf16[128,2048]{0,1:T(8,128)(2,1)S(1)} %copy.54), channel_id=1, source_target_pairs={{0,8},{4,12},{8,16},{12,20},{16,24},{20,28},{24,32},{28,36},{32,40... | collective-permute-start | bytes 1572872 | tf_op jit(solution)/shard_map/ppermute | solution.py:115
  26.3 56.7 %collective-permute-start.2 = (bf16[128,2048]{0,1:T(8,128)(2,1)S(1)}, bf16[128,2048]{0,1:T(8,128)(2,1)}, u32[]{:S(2)}, u32[]{:S(2)}) collective-permute-start(bf16[128,2048]{0,1:T(8,128)(2,1)S(1)} %copy.51), channel_id=1, source_target_pairs={{0,8},{4,12},{8,16},{12,20},{16,24},{20,28},{24,32},{28,36},{32,40... | collective-permute-start | bytes 1572872 | tf_op jit(solution)/shard_map/ppermute | solution.py:115
  28.5 21.1 %copy-start.2 = (f32[128,256]{0,1:T(8,128)}, f32[128,256]{0,1:T(8,128)S(1)}, u32[]{:S(2)}) copy-start(f32[128,256]{0,1:T(8,128)S(1)} %copy.44) | copy-start | bytes 393220
  34.7 36.2 %all-to-all-start = ((bf16[64,2,1280]{2,1,0:T(2,128)(2,1)}), bf16[64,2,1280]{2,1,0:T(2,128)(2,1)S(1)}, u32[]{:S(2)}, u32[]{:S(2)}) async-start(bf16[64,2,1280]{2,1,0:T(2,128)(2,1)} %reshape.182), calls=%async_computation | async-start | bytes 655360 | tf_op jit(solution)/shard_map/all_to_all | solution.py:63
  54.2 33.5 %collective-permute-start.5 = (bf16[128,2048]{0,1:T(8,128)(2,1)}, bf16[128,2048]{0,1:T(8,128)(2,1)}, u32[]{:S(2)}, u32[]{:S(2)}) collective-permute-start(bf16[128,2048]{0,1:T(8,128)(2,1)} %broadcast_select_fusion), channel_id=1, source_target_pairs={{0,4},{4,0},{1,5},{5,1},{2,6},{6,2},{3,7},{7,3},{8,12},{12,8},{9,1... | collective-permute-start | bytes 1572872 | tf_op jit(solution)/shard_map/ppermute | solution.py:116
  75.6 28.1 %all-to-all-start.1 = ((bf16[64,2,1280]{2,1,0:T(2,128)(2,1)}), bf16[64,2,1280]{2,1,0:T(2,128)(2,1)S(1)}, u32[]{:S(2)}, u32[]{:S(2)}) async-start(bf16[64,2,1280]{2,1,0:T(2,128)(2,1)} %reshape.184), calls=%async_computation.1 | async-start | bytes 655360 | tf_op jit(solution)/shard_map/all_to_all | solution.py:66
  84.9 25.9 %collective-permute-start.3 = (bf16[128,2048]{0,1:T(8,128)(2,1)}, bf16[128,2048]{0,1:T(8,128)(2,1)}, u32[]{:S(2)}, u32[]{:S(2)}) collective-permute-start(bf16[128,2048]{0,1:T(8,128)(2,1)} %broadcast_select_fusion.1), channel_id=1, source_target_pairs={{0,4},{4,0},{1,5},{5,1},{2,6},{6,2},{3,7},{7,3},{8,12},{12,8},{9,1... | collective-permute-start | bytes 1572872 | tf_op jit(solution)/shard_map/ppermute | solution.py:116
  89.1 0.8 copy-start.9
  105.9 6.4 %copy-start.14 = (f32[16,128,384]{1,2,0:T(8,128)S(1)}, f32[16,128,384]{1,2,0:T(8,128)}, u32[]{:S(2)}) copy-start(f32[16,128,384]{1,2,0:T(8,128)} %get-tuple-element.15) | copy-start | bytes 9437188
  105.9 8.0 %collective-permute-start.1 = (f32[64,2560]{1,0:T(8,128)S(1)}, f32[64,2560]{1,0:T(8,128)S(1)}, u32[]{:S(2)}, u32[]{:S(2)}) collective-permute-start(f32[64,2560]{1,0:T(8,128)S(1)} %get-tuple-element.9), channel_id=1, source_target_pairs={{0,4},{4,0},{1,5},{5,1},{2,6},{6,2},{3,7},{7,3},{8,12},{12,8},{9,1... | collective-permute-start | bytes 1966088 | tf_op jit(solution)/shard_map/ppermute | solution.py:72
  113.9 0.8 copy-start.6
  120.4 1.2 copy-start.1
  120.4 1.2 copy-start.3
  121.7 2.7 %copy-start.13 = (f32[16,128,128]{1,2,0:T(8,128)S(1)}, f32[16,128,128]{1,2,0:T(8,128)}, u32[]{:S(2)}) copy-start(f32[16,128,128]{1,2,0:T(8,128)} %get-tuple-element.13) | copy-start | bytes 3145732
  123.6 1.0 copy-start.5

commit v6 on v5

--- a/solution.py
+++ b/solution.py
@@ -30,7 +30,7 @@
     )
 
 
-def pair_features(scaled):
+def pair_features(scaled, rows):
     row_count, head_count, feat_count = scaled.shape
     columns = jnp.transpose(scaled, (1, 2, 0))
     lower_index, upper_index = np.triu_indices(feat_count)
@@ -43,8 +43,15 @@
     left_side = jnp.einsum("hfr,fp->hpr", columns, pick_lower, precision=EXACT)
     right_side = jnp.einsum("hfr,fp->hpr", columns, pick_upper, precision=EXACT)
     paired = left_side * right_side * pair_weight[None, :, None]
+    filler = rows - 1 - feat_count - paired.shape[1]
     return jnp.concatenate(
-        [jnp.ones((head_count, 1, row_count), jnp.float32), columns, paired], axis=1
+        [
+            jnp.ones((head_count, 1, row_count), jnp.float32),
+            columns,
+            paired,
+            jnp.zeros((head_count, filler, row_count), jnp.float32),
+        ],
+        axis=1,
     )
 
 
@@ -87,14 +94,20 @@
         row_count, head_count, FEAT
     )
     value_heads = values.astype(jnp.float32).reshape(row_count, head_count, value_width)
-    query_feats = pair_features(query_scaled)
-    key_feats = pair_features(key_scaled)
+    feat_total = 1 + FEAT + FEAT * (FEAT + 1) // 2
+    norm_rows = -(-feat_total // value_width)
+    feat_rows = -(-(feat_total + norm_rows) // 8) * 8
+    query_feats = pair_features(query_scaled, feat_rows)
+    key_feats = pair_features(key_scaled, feat_rows)
     local_state = jnp.einsum("hpr,rhv->hpv", key_feats, value_heads, precision=PRECISE)
-    local_norm = jnp.sum(key_feats, axis=2)
-    local = jnp.concatenate([local_state, local_norm[:, :, None]], axis=2)
+    local_norm = jnp.sum(key_feats[:, :feat_total], axis=2)
+    norm_block = jnp.pad(local_norm, ((0, 0), (0, norm_rows * value_width - feat_total)))
+    norm_block = norm_block.reshape(head_count, norm_rows, value_width)
+    local = lax.dynamic_update_slice(local_state, norm_block, (0, feat_total, 0))
     prior = prefix_before(local)
-    prior_state = prior[:, :, :value_width]
-    prior_norm = prior[:, :, value_width]
+    prior_state = prior
+    prior_norm = prior[:, feat_total : feat_total + norm_rows].reshape(head_count, -1)[:, :feat_total]
+    query_feats_only = query_feats[:, :feat_total]
     causal = jnp.arange(row_count)[:, None] >= jnp.arange(row_count)[None, :]
     inner_prod = jnp.einsum("thf,jhf->htj", query_scaled, key_scaled, precision=EXACT)
     kernel = jnp.where(causal[None], 1.0 + inner_prod + 0.5 * inner_prod * inner_prod, 0.0)
@@ -102,7 +115,7 @@
         "hpt,hpv->thv", query_feats, prior_state, precision=PRECISE
     )
     denominator = jnp.sum(kernel, axis=2).T + jnp.einsum(
-        "hpt,hp->th", query_feats, prior_norm, precision=PRECISE
+        "hpt,hp->th", query_feats_only, prior_norm, precision=PRECISE
     )
     linear_out = (numerator / denominator[:, :, None]).reshape(row_count, head_count * value_width)
     seq_count = lax.axis_size("sx") * lax.axis_size("sz") * lax.axis_size("sc")

time: 128 us -> 127 us (level)
  local copies, waits for them, and re-layouts: 18.8 us -> 15.4 us
  waiting for transfers between devices: 26.1 us -> 27.7 us
    reshape x2 -> x1, local copies, waits for them, and re-layouts: 5.16 us -> 0.01 us  [on_device(): norm_block = norm_block.reshape(head_count, norm_rows, value_width)]
    unnamed x38 -> x47, local copies, waits for them, and re-layouts: 7.99 us -> 11.8 us
    all_to_all x2, other arithmetic: 2.01 us -> 4.41 us  [prefix_before(): lax.all_to_all(chip_half.astype(LINK), ('sx', 'sz'), 0, 0, tiled=True)]
    concatenate x1 -> x0, other arithmetic: 1.92 us -> none  [on_device(): local = jnp.concatenate([local_state, local_norm[:, :, None]], axis=2)]
    slice x2, local copies, waits for them, and re-layouts: 1.73 us -> 0.02 us  [on_device(): prior[:, feat_total:feat_total + norm_rows].reshape(head_count, -1)]
    broadcast_in_dim x1 -> x0, local copies, waits for them, and re-layouts: 1.57 us -> none  [on_device(): local = jnp.concatenate([local_state, local_norm[:, :, None]], axis=2)]
    dot_general x1, matrix products: 1.92 us -> 3.27 us  [on_device(): jnp.einsum('hpt,hpv->thv', query_feats, prior_state, precision=PRECISE)]
  transfers between devices with their start and end apart: 8 -> 8, of which waited for: 2 -> 2; matrix products, arithmetic and copies ran while one was open for 23% -> 28% of each run, Pallas kernels for 0% -> 0%
where the time goes in v6:
time: 127 us; the launch traced here: 126 us
  starting transfers between devices  44.1 us (35%)
  waiting for transfers between devices  27.7 us (22%)
  other arithmetic  24.5 us (19%)
  local copies, waits for them, and re-layouts  15.4 us (12%)
  matrix products  13.5 us (11%)
    all_to_all x1, waiting for transfers between devices, prefix_before(): lax.all_to_all(chip_half.astype(LINK), ('sx', 'sz'), 0, 0, tiled=True)  16 us
    all_to_all x1, starting transfers between devices, prefix_before(): lax.all_to_all(chip_half.astype(LINK), ('sx', 'sz'), 0, 0, tiled=True)  14.3 us
    unnamed x47, local copies, waits for them, and re-layouts  11.8 us
    all_to_all x1, waiting for transfers between devices, prefix_before(): chip_prefix = lax.all_to_all(before_chip, ('sx', 'sz'), 0, 0, tiled=True)  11.7 us
    ppermute x1, starting transfers between devices, prefix_before(): other = lax.ppermute(sent, 'sc', [(0, 1), (1, 0)])  8.87 us
    all_to_all x1, starting transfers between devices, prefix_before(): chip_prefix = lax.all_to_all(before_chip, ('sx', 'sz'), 0, 0, tiled=True)  7.33 us
    ppermute x1, starting transfers between devices, prefix_before(): got = lax.ppermute(give, 'sc', [(0, 1), (1, 0)])  4.82 us
    ppermute x2, starting transfers between devices, on_device(): lax.ppermute(jax.tree.map(lambda o, f: jnp.where(core == 0, o, f), (windo...  4.58 us
  transfers between devices with their start and end apart: 8, of which 2 were waited for; matrix products, arithmetic and copies ran while one was open for 28% of the time, Pallas kernels for 0%

profile of v6, /device:TPU:1, one launch (start us, length us, event | category | flops | bytes accessed | tf_op | source)
XLA Modules:
  0.0 126.3 jit_solution(9242762566537516051)
XLA Ops:
  0.6 0.0 copy-start
  0.6 0.0 copy-start.12
  0.7 0.0 copy-start.15
  0.7 0.9 convert_multiply_fusion
  1.6 0.1 copy.44
  1.7 1.0 fusion.57
  2.7 0.4 fusion.7
  3.1 0.6 fusion.13
  3.8 0.1 pad.28.clone
  3.9 1.7 %fusion.19 = f32[16,160,128]{2,1,0:T(8,128)S(1)} fusion(f32[16,1,128]{2,1,0:T(1,128)S(1)} %broadcast.103, f32[16,136,128]{2,1,0:T(8,128)S(1)} %fusion.7, f32[16,16,128]{2,1,0:T(8,128)S(1)} %bitcast.92, f32[160]{0:T(256)S(1)} %pad.28.clone, bf16[128,2048]{1,0:T(8,128)(2,1)} %param.13), kind=kOutput, calls=%fused_computation.32 | convolution fusion | flops 252641280 | bytes 3089024 | tf_op jit(solution)/shard_map/hpr,rhv->hpv/dot_general | solution.py:102
  5.5 0.2 dynamic_update_slice.3
  5.7 1.2 fusion.54
  6.9 1.3 squeeze.4
  8.1 0.0 copy-done.3
  8.2 0.1 squeeze.10
  8.3 0.0 copy-start.9
  8.3 0.9 broadcast_select_fusion.3
  9.2 8.9 %collective-permute-start = (f32[64,2560]{1,0:T(8,128)}, f32[64,2560]{1,0:T(8,128)}, u32[]{:S(2)}, u32[]{:S(2)}) collective-permute-start(f32[64,2560]{1,0:T(8,128)} %broadcast_select_fusion.3), channel_id=1, source_target_pairs={{0,4},{4,0},{1,5},{5,1},{2,6},{6,2},{3,7},{7,3},{8,12},{12,8},{9,1... | collective-permute-start | bytes 1966088 | tf_op jit(solution)/shard_map/ppermute | solution.py:67
  18.1 0.3 copy.52
  18.4 2.1 %collective-permute-start.4 = (bf16[128,2048]{0,1:T(8,128)(2,1)S(1)}, bf16[128,2048]{0,1:T(8,128)(2,1)}, u32[]{:S(2)}, u32[]{:S(2)}) collective-permute-start(bf16[128,2048]{0,1:T(8,128)(2,1)S(1)} %copy.52), channel_id=1, source_target_pairs={{0,8},{4,12},{8,16},{12,20},{16,24},{20,28},{24,32},{28,36},{32,40... | collective-permute-start | bytes 1572872 | tf_op jit(solution)/shard_map/ppermute | solution.py:128
  20.5 1.3 %copy.49 = bf16[128,2048]{0,1:T(8,128)(2,1)S(1)} copy(bf16[128,2048]{1,0:T(8,128)(2,1)} %param.13) | data formatting | bytes 1048576 | tf_op args[2]
  21.8 2.1 %collective-permute-start.2 = (bf16[128,2048]{0,1:T(8,128)(2,1)S(1)}, bf16[128,2048]{0,1:T(8,128)(2,1)}, u32[]{:S(2)}, u32[]{:S(2)}) collective-permute-start(bf16[128,2048]{0,1:T(8,128)(2,1)S(1)} %copy.49), channel_id=1, source_target_pairs={{0,8},{4,12},{8,16},{12,20},{16,24},{20,28},{24,32},{28,36},{32,40... | collective-permute-start | bytes 1572872 | tf_op jit(solution)/shard_map/ppermute | solution.py:128
  23.9 0.1 copy.43
  24.1 1.4 %fusion.58 = f32[16,128,136]{1,2,0:T(8,128)} fusion(f32[16,16,128]{2,1,0:T(8,128)S(1)} %bitcast.94, bf16[16,136,1]{1,0,2:T(8,128)(2,1)S(1)} %copy-done.13), kind=kOutput, calls=%fused_computation.87 | convolution fusion | flops 8912896 | bytes 1249536 | tf_op jit(solution)/shard_map/hfr,fp->hpr/dot_general | solution.py:43
  25.4 2.0 %fusion.55 = (f32[16,128]{1,0:T(8,128)}, f32[16,128,128]{1,2,0:T(8,128)}) fusion(f32[128,16,16]{0,2,1:T(8,128)S(1)} %bitcast.95, f32[128,16,16]{0,2,1:T(8,128)S(1)} %bitcast.93, pred[128,128]{0,1:T(8,128)(4,1)S(1)} %iota_compare_fusion), kind=kOutput, calls=%fused_computation.84 | convolution fusion | flops 9959424 | bytes 1335296 | tf_op jit(solution)/shard_map/thf,jhf->htj/dot_general | solution.py:112
  27.4 1.9 %fusion.47 = bf16[64,1,2560]{2,0,1:T(8,128)(2,1)} fusion(f32[64,2560]{1,0:T(8,128)} %collective-permute-done, f32[64,2560]{1,0:T(8,128)S(1)} %squeeze.4, f32[64,2560]{1,0:T(8,128)S(1)} %squeeze.10, pred[]{:T(512)S(6)} %eq.2), kind=kLoop, calls=%fused_computation.63 | loop fusion | flops 491520 | bytes 2293761 | tf_op jit(solution)/shard_map/all_to_all | solution.py:70
  29.3 0.6 broadcast.118
  29.9 2.5 %reduce = bf16[64,2560]{1,0:T(8,128)(2,1)} reduce(bf16[64,1,2560]{2,0,1:T(8,128)(2,1)} %fusion.47, bf16[]{:T(256)} %broadcast.118), dimensions={1}, to_apply=%copy.48.reduce_sub_computation | reduce | bytes 655362 | tf_op jit(solution)/shard_map/all_to_all | solution.py:70
  32.4 1.8 %reshape.171 = bf16[64,2,1280]{2,1,0:T(2,128)(2,1)} reshape(bf16[64,2560]{1,0:T(8,128)(2,1)} %reduce) | data formatting | bytes 655360
  34.2 14.3 %all-to-all-start = ((bf16[64,2,1280]{2,1,0:T(2,128)(2,1)}), bf16[64,2,1280]{2,1,0:T(2,128)(2,1)}, u32[]{:S(2)}, u32[]{:S(2)}) async-start(bf16[64,2,1280]{2,1,0:T(2,128)(2,1)} %reshape.171), calls=%async_computation | async-start | bytes 655360 | tf_op jit(solution)/shard_map/all_to_all | solution.py:70
  48.6 0.8 and_and_fusion
  49.4 1.4 %fusion.9 = f32[16,136,128]{2,1,0:T(8,128)} fusion(f32[16,128,136]{1,2,0:T(8,128)S(1)} %copy-done.2, f32[16,16,128]{2,1,0:T(8,128)S(1)} %bitcast.96, bf16[16,136,1]{1,0,2:T(8,128)(2,1)S(1)} %copy-done.12, f32[136]{0:T(256)S(1)} %copy-done.15), kind=kOutput, calls=%fused_computation.21 | convolution fusion | flops 9469952 | bytes 2364192 | tf_op jit(solution)/shard_map/hfr,fp->hpr/dot_general | solution.py:44
  50.7 1.9 %broadcast_select_fusion = bf16[128,2048]{0,1:T(8,128)(2,1)} fusion(bf16[128,2048]{0,1:T(8,128)(2,1)S(1)} %copy.52, bf16[128,2048]{0,1:T(8,128)(2,1)} %collective-permute-done.4, pred[]{:T(512)S(6)} %eq.2), kind=kLoop, calls=%fused_computation.59 | loop fusion | flops 262144 | bytes 1572865 | tf_op jit(solution)/shard_map/jit(_where)/select_n | solution.py:130
  52.6 1.9 %collective-permute-start.5 = (bf16[128,2048]{0,1:T(8,128)(2,1)}, bf16[128,2048]{0,1:T(8,128)(2,1)}, u32[]{:S(2)}, u32[]{:S(2)}) collective-permute-start(bf16[128,2048]{0,1:T(8,128)(2,1)} %broadcast_select_fusion), channel_id=1, source_target_pairs={{0,4},{4,0},{1,5},{5,1},{2,6},{6,2},{3,7},{7,3},{8,12},{12,8},{9,1... | collective-permute-start | bytes 1572872 | tf_op jit(solution)/shard_map/ppermute | solution.py:129
  54.6 16.0 %all-to-all-done = bf16[64,2,1280]{2,1,0:T(2,128)(2,1)} async-done(((bf16[64,2,1280]{2,1,0:T(2,128)(2,1)}), bf16[64,2,1280]{2,1,0:T(2,128)(2,1)}, u32[]{:S(2)}, u32[]{:S(2)}) %all-to-all-start) | async-done | bytes 327712 | tf_op jit(solution)/shard_map/all_to_all | solution.py:70
  70.6 2.5 %reshape.172 = bf16[64,1,2560]{2,1,0:T(2,128)(2,1)S(1)} reshape(bf16[64,2,1280]{2,1,0:T(2,128)(2,1)} %all-to-all-done) | data formatting | bytes 655360
  73.0 1.0 subtract_convert_fusion
  74.1 2.6 %reduce.1 = bf16[64,2560]{1,0:T(8,128)(2,1)S(1)} reduce(bf16[64,1,2560]{2,1,0:T(2,128)(2,1)S(1)} %subtract_convert_fusion, bf16[]{:T(256)} %broadcast.118), dimensions={1}, to_apply=%subtract_convert_fusion.reduce_sub_computation | reduce | bytes 655362 | tf_op jit(solution)/shard_map/jit(cumsum)/reduce_window_sum | solution.py:72
  76.7 0.8 reshape.173
  77.5 7.3 %all-to-all-start.1 = ((bf16[64,2,1280]{2,1,0:T(2,128)(2,1)}), bf16[64,2,1280]{2,1,0:T(2,128)(2,1)S(1)}, u32[]{:S(2)}, u32[]{:S(2)}) async-start(bf16[64,2,1280]{2,1,0:T(2,128)(2,1)} %reshape.173), calls=%async_computation.1 | async-start | bytes 655360 | tf_op jit(solution)/shard_map/all_to_all | solution.py:73
  84.8 1.1 broadcast_select_fusion.1
  85.9 2.7 %collective-permute-start.3 = (bf16[128,2048]{0,1:T(8,128)(2,1)S(1)}, bf16[128,2048]{0,1:T(8,128)(2,1)}, u32[]{:S(2)}, u32[]{:S(2)}) collective-permute-start(bf16[128,2048]{0,1:T(8,128)(2,1)S(1)} %broadcast_select_fusion.1), channel_id=1, source_target_pairs={{0,4},{4,0},{1,5},{5,1},{2,6},{6,2},{3,7},{7,3},{8,12},{12,8},{9,1... | collective-permute-start | bytes 1572872 | tf_op jit(solution)/shard_map/ppermute | solution.py:129
  88.6 1.4 %pad_maximum_fusion.5 = bf16[384,2048]{0,1:T(8,128)(2,1)S(1)} fusion(bf16[128,2048]{0,1:T(8,128)(2,1)S(1)} %copy.52, bf16[128,2048]{0,1:T(8,128)(2,1)} %collective-permute-done.5, bf16[128,2048]{0,1:T(8,128)(2,1)} %collective-permute-done.4), kind=kLoop, calls=%fused_computation.10 | loop fusion | flops 4718592 | bytes 3145728 | tf_op jit(solution)/shard_map/concatenate | solution.py:136
  90.1 0.6 fusion.40
  90.7 0.1 copy-done.11
  90.9 3.1 %fusion.56 = (f32[16,128]{1,0:T(8,128)}, f32[16,128,384]{1,2,0:T(8,128)}) fusion(f32[16,384,128]{2,1,0:T(8,128)S(1)} %fusion.40, pred[128,384]{0,1:T(8,128)(4,1)S(1)} %copy-done.11), kind=kOutput, calls=%fused_computation.85 | output fusion | flops 4718975 | bytes 6348800 | tf_op jit(solution)/shard_map/sub | solution.py:154
  94.0 11.7 %all-to-all-done.1 = bf16[64,2,1280]{2,1,0:T(2,128)(2,1)S(1)} async-done(((bf16[64,2,1280]{2,1,0:T(2,128)(2,1)}), bf16[64,2,1280]{2,1,0:T(2,128)(2,1)S(1)}, u32[]{:S(2)}, u32[]{:S(2)}) %all-to-all-start.1) | async-done | bytes 327712 | tf_op jit(solution)/shard_map/all_to_all | solution.py:73
  105.7 0.3 reshape.174
  106.0 0.7 convert_element_type.46
  106.6 2.1 %fusion.33 = (f32[1,64,2560]{2,1,0:T(8,128)}, f32[64,2560]{1,0:T(8,128)S(1)}) fusion(f32[64,1,2560]{2,1,0:T(1,128)S(1)} %convert_element_type.46, pred[]{:T(512)S(6)} %eq.2, f32[64,2560]{1,0:T(8,128)S(1)} %squeeze.4, f32[64,2560]{1,0:T(8,128)} %collective-permute-done), kind=kLoop, calls=%fused_computation.47 | loop fusion | flops 655360 | bytes 3276801 | tf_op jit(solution)/shard_map/stack | solution.py:80
  108.7 4.8 %collective-permute-start.1 = (f32[64,2560]{1,0:T(8,128)S(1)}, f32[64,2560]{1,0:T(8,128)S(1)}, u32[]{:S(2)}, u32[]{:S(2)}) collective-permute-start(f32[64,2560]{1,0:T(8,128)S(1)} %get-tuple-element.9), channel_id=1, source_target_pairs={{0,4},{4,0},{1,5},{5,1},{2,6},{6,2},{3,7},{7,3},{8,12},{12,8},{9,1... | collective-permute-start | bytes 1966088 | tf_op jit(solution)/shard_map/ppermute | solution.py:79
  113.6 1.4 %pad_maximum_fusion.4 = bf16[384,2048]{0,1:T(8,128)(2,1)S(1)} fusion(bf16[128,2048]{0,1:T(8,128)(2,1)S(1)} %copy.49, bf16[128,2048]{0,1:T(8,128)(2,1)} %collective-permute-done.3, bf16[128,2048]{0,1:T(8,128)(2,1)} %collective-permute-done.2), kind=kLoop, calls=%fused_computation.9 | loop fusion | flops 4718592 | bytes 3145728 | tf_op jit(solution)/shard_map/concatenate | solution.py:137
  115.0 0.6 fusion.30
  115.6 1.0 copy.59
  116.6 0.8 copy-done.8
  117.5 1.4 %maximum_select_fusion = f32[2,64,2560]{2,1,0:T(8,128)S(1)} fusion(f32[1,64,2560]{2,1,0:T(8,128)} %bitcast.101, f32[1,64,2560]{2,1,0:T(8,128)S(1)} %copy-done.4, pred[]{:T(512)S(6)} %eq.2), kind=kLoop, calls=%fused_computation.37 | loop fusion | flops 983040 | bytes 2621441 | tf_op jit(solution)/shard_map/jit(_where)/select_n | solution.py:80
  118.9 0.1 select_n.65
  119.0 0.8 copy-done.6
  119.8 3.3 %convolution_bitcast_fusion = f32[128,16,128]{0,2,1:T(8,128)S(1)} fusion(f32[16,160,128]{2,1,0:T(8,128)S(1)} %select_n.65, f32[16,1,128]{2,1,0:T(1,128)S(1)} %broadcast.103, f32[16,136,128]{2,1,0:T(8,128)} %fusion.9, f32[16,16,128]{2,1,0:T(8,128)S(1)} %bitcast.97, f32[160]{0:T(256)S(1)} %pad.28.clone), kind=kOutput, calls=%fused_computation.22 | convolution fusion | flops 252641280 | bytes 3613312 | tf_op jit(solution)/shard_map/hpt,hpv->thv/dot_general | solution.py:114
  123.1 0.7 fusion.15
  123.8 0.3 copy-done.7
  124.1 0.3 copy-done.16
  124.5 0.5 fusion.11
  125.0 1.3 %copy.58 = f32[128,2048]{1,0:T(8,128)} copy(f32[128,2048]{0,1:T(8,128)S(1)} %bitcast.100) | data formatting | bytes 2097152
  (47 shorter events, 0.2 us)
Async XLA Ops:
  0.6 89.4 %copy-start = (bf16[128,2048]{1,0:T(8,128)(2,1)S(1)}, bf16[128,2048]{1,0:T(8,128)(2,1)}, u32[]{:S(2)}) copy-start(bf16[128,2048]{1,0:T(8,128)(2,1)} %param.14) | copy-start | bytes 1572868
  0.6 2.1 %copy-start.12 = (bf16[16,136,1]{1,0,2:T(8,128)(2,1)S(1)}, bf16[16,136,1]{1,0,2:T(8,128)(2,1)}, u32[]{:S(2)}) copy-start(bf16[16,136,1]{1,0,2:T(8,128)(2,1)} %constant.123) | copy-start | bytes 13060
  0.7 2.1 %copy-start.15 = (f32[136]{0:T(256)S(1)}, f32[136]{0:T(256)}, u32[]{:S(2)}) copy-start(f32[136]{0:T(256)} %constant.57.clone) | copy-start | bytes 1636
  6.9 1.3 %copy-start.3 = (f32[8,160,128]{2,1,0:T(8,128)S(1)}, f32[8,160,128]{2,1,0:T(8,128)}, u32[]{:S(2)}) copy-start(f32[8,160,128]{2,1,0:T(8,128)} %get-tuple-element.11) | copy-start | bytes 1966084
  8.3 9.8 %copy-start.9 = (bf16[128,2048]{1,0:T(8,128)(2,1)S(1)}, bf16[128,2048]{1,0:T(8,128)(2,1)}, u32[]{:S(2)}) copy-start(bf16[128,2048]{1,0:T(8,128)(2,1)} %param.15) | copy-start | bytes 1572868
  9.2 14.7 %copy-start.10 = (bf16[128,256]{1,0:T(8,128)(2,1)S(1)}, bf16[128,256]{1,0:T(8,128)(2,1)}, u32[]{:S(2)}) copy-start(bf16[128,256]{1,0:T(8,128)(2,1)} %param.11) | copy-start | bytes 196612
  9.2 14.8 %copy-start.13 = (bf16[16,136,1]{1,0,2:T(8,128)(2,1)S(1)}, bf16[16,136,1]{1,0,2:T(8,128)(2,1)}, u32[]{:S(2)}) copy-start(bf16[16,136,1]{1,0,2:T(8,128)(2,1)} %constant.122) | copy-start | bytes 13060
  9.2 18.2 %collective-permute-start = (f32[64,2560]{1,0:T(8,128)}, f32[64,2560]{1,0:T(8,128)}, u32[]{:S(2)}, u32[]{:S(2)}) collective-permute-start(f32[64,2560]{1,0:T(8,128)} %broadcast_select_fusion.3), channel_id=1, source_target_pairs={{0,4},{4,0},{1,5},{5,1},{2,6},{6,2},{3,7},{7,3},{8,12},{12,8},{9,1... | collective-permute-start | bytes 1966088 | tf_op jit(solution)/shard_map/ppermute | solution.py:67
  18.4 32.4 %collective-permute-start.4 = (bf16[128,2048]{0,1:T(8,128)(2,1)S(1)}, bf16[128,2048]{0,1:T(8,128)(2,1)}, u32[]{:S(2)}, u32[]{:S(2)}) collective-permute-start(bf16[128,2048]{0,1:T(8,128)(2,1)S(1)} %copy.52), channel_id=1, source_target_pairs={{0,8},{4,12},{8,16},{12,20},{16,24},{20,28},{24,32},{28,36},{32,40... | collective-permute-start | bytes 1572872 | tf_op jit(solution)/shard_map/ppermute | solution.py:128
  21.8 63.0 %collective-permute-start.2 = (bf16[128,2048]{0,1:T(8,128)(2,1)S(1)}, bf16[128,2048]{0,1:T(8,128)(2,1)}, u32[]{:S(2)}, u32[]{:S(2)}) collective-permute-start(bf16[128,2048]{0,1:T(8,128)(2,1)S(1)} %copy.49), channel_id=1, source_target_pairs={{0,8},{4,12},{8,16},{12,20},{16,24},{20,28},{24,32},{28,36},{32,40... | collective-permute-start | bytes 1572872 | tf_op jit(solution)/shard_map/ppermute | solution.py:128
  24.0 25.3 %copy-start.5 = (f32[128,256]{0,1:T(8,128)}, f32[128,256]{0,1:T(8,128)S(1)}, u32[]{:S(2)}) copy-start(f32[128,256]{0,1:T(8,128)S(1)} %copy.43) | copy-start | bytes 393220
  29.3 20.0 %copy-start.2 = (f32[16,128,136]{1,2,0:T(8,128)S(1)}, f32[16,128,136]{1,2,0:T(8,128)}, u32[]{:S(2)}) copy-start(f32[16,128,136]{1,2,0:T(8,128)} %fusion.58) | copy-start | bytes 3342340
  34.2 36.4 %all-to-all-start = ((bf16[64,2,1280]{2,1,0:T(2,128)(2,1)}), bf16[64,2,1280]{2,1,0:T(2,128)(2,1)}, u32[]{:S(2)}, u32[]{:S(2)}) async-start(bf16[64,2,1280]{2,1,0:T(2,128)(2,1)} %reshape.171), calls=%async_computation | async-start | bytes 655360 | tf_op jit(solution)/shard_map/all_to_all | solution.py:70
  52.6 36.0 %collective-permute-start.5 = (bf16[128,2048]{0,1:T(8,128)(2,1)}, bf16[128,2048]{0,1:T(8,128)(2,1)}, u32[]{:S(2)}, u32[]{:S(2)}) collective-permute-start(bf16[128,2048]{0,1:T(8,128)(2,1)} %broadcast_select_fusion), channel_id=1, source_target_pairs={{0,4},{4,0},{1,5},{5,1},{2,6},{6,2},{3,7},{7,3},{8,12},{12,8},{9,1... | collective-permute-start | bytes 1572872 | tf_op jit(solution)/shard_map/ppermute | solution.py:129
  77.5 28.2 %all-to-all-start.1 = ((bf16[64,2,1280]{2,1,0:T(2,128)(2,1)}), bf16[64,2,1280]{2,1,0:T(2,128)(2,1)S(1)}, u32[]{:S(2)}, u32[]{:S(2)}) async-start(bf16[64,2,1280]{2,1,0:T(2,128)(2,1)} %reshape.173), calls=%async_computation.1 | async-start | bytes 655360 | tf_op jit(solution)/shard_map/all_to_all | solution.py:73
  85.9 27.6 %collective-permute-start.3 = (bf16[128,2048]{0,1:T(8,128)(2,1)S(1)}, bf16[128,2048]{0,1:T(8,128)(2,1)}, u32[]{:S(2)}, u32[]{:S(2)}) collective-permute-start(bf16[128,2048]{0,1:T(8,128)(2,1)S(1)} %broadcast_select_fusion.1), channel_id=1, source_target_pairs={{0,4},{4,0},{1,5},{5,1},{2,6},{6,2},{3,7},{7,3},{8,12},{12,8},{9,1... | collective-permute-start | bytes 1572872 | tf_op jit(solution)/shard_map/ppermute | solution.py:129
  90.1 0.8 copy-start.11
  106.6 8.3 %copy-start.18 = (f32[16,128]{1,0:T(8,128)S(1)}, f32[16,128]{1,0:T(8,128)}, u32[]{:S(2)}) copy-start(f32[16,128]{1,0:T(8,128)} %get-tuple-element.14) | copy-start | bytes 24580
  108.7 6.3 %copy-start.17 = (f32[16,128,384]{1,2,0:T(8,128)S(1)}, f32[16,128,384]{1,2,0:T(8,128)}, u32[]{:S(2)}) copy-start(f32[16,128,384]{1,2,0:T(8,128)} %get-tuple-element.15) | copy-start | bytes 9437188
  108.7 7.9 %collective-permute-start.1 = (f32[64,2560]{1,0:T(8,128)S(1)}, f32[64,2560]{1,0:T(8,128)S(1)}, u32[]{:S(2)}, u32[]{:S(2)}) collective-permute-start(f32[64,2560]{1,0:T(8,128)S(1)} %get-tuple-element.9), channel_id=1, source_target_pairs={{0,4},{4,0},{1,5},{5,1},{2,6},{6,2},{3,7},{7,3},{8,12},{12,8},{9,1... | collective-permute-start | bytes 1966088 | tf_op jit(solution)/shard_map/ppermute | solution.py:79
  115.6 1.9 %copy-start.4 = (f32[1,64,2560]{2,1,0:T(8,128)S(1)}, f32[1,64,2560]{2,1,0:T(8,128)}, u32[]{:S(2)}) copy-start(f32[1,64,2560]{2,1,0:T(8,128)} %get-tuple-element.8) | copy-start | bytes 1966084
  116.6 0.8 copy-start.8
  118.9 0.9 copy-start.6
  119.8 3.3 %copy-start.1 = (f32[16,136,128]{2,1,0:T(8,128)S(1)}, f32[16,136,128]{2,1,0:T(8,128)}, u32[]{:S(2)}) copy-start(f32[16,136,128]{2,1,0:T(8,128)} %fusion.9) | copy-start | bytes 3342340
  123.0 0.7 copy-start.14
  123.1 1.0 copy-start.7
  123.1 1.4 %copy-start.16 = (f32[16,128,128]{1,2,0:T(8,128)S(1)}, f32[16,128,128]{1,2,0:T(8,128)}, u32[]{:S(2)}) copy-start(f32[16,128,128]{1,2,0:T(8,128)} %get-tuple-element.13) | copy-start | bytes 3145732

commit v7 on v6

--- a/solution.py
+++ b/solution.py
@@ -55,7 +55,7 @@
     )
 
 
-def prefix_before(local):
+def prefix_before(local, tied):
     chips = lax.axis_size("sx") * lax.axis_size("sz")
     core = lax.axis_index("sc")
     size = local.size
@@ -67,7 +67,8 @@
     other = lax.ppermute(sent, "sc", [(0, 1), (1, 0)])
     mine = jnp.where(core == 0, flat[0], flat[1])
     chip_half = mine + other
-    gathered = lax.all_to_all(chip_half.astype(LINK), ("sx", "sz"), 0, 0, tiled=True)
+    outgoing, tied = lax.optimization_barrier((chip_half.astype(LINK), tied))
+    gathered = lax.all_to_all(outgoing, ("sx", "sz"), 0, 0, tiled=True)
     gathered = gathered.astype(jnp.float32)
     before_chip = (jnp.cumsum(gathered, axis=0) - gathered).astype(LINK)
     chip_prefix = lax.all_to_all(before_chip, ("sx", "sz"), 0, 0, tiled=True)
@@ -78,7 +79,7 @@
     give = jnp.where(core == 0, with_first, chip_prefix)
     got = lax.ppermute(give, "sc", [(0, 1), (1, 0)])
     halves = jnp.where(core == 0, jnp.stack([keep, got]), jnp.stack([got, keep]))
-    return halves.reshape(-1)[:size].reshape(local.shape)
+    return halves.reshape(-1)[:size].reshape(local.shape), tied
 
 
 def on_device(linear_query, linear_key, values, window_query, window_key):
@@ -104,7 +105,11 @@
     norm_block = jnp.pad(local_norm, ((0, 0), (0, norm_rows * value_width - feat_total)))
     norm_block = norm_block.reshape(head_count, norm_rows, value_width)
     local = lax.dynamic_update_slice(local_state, norm_block, (0, feat_total, 0))
-    prior = prefix_before(local)
+    seq_count = lax.axis_size("sx") * lax.axis_size("sz") * lax.axis_size("sc")
+    flat_axes = ("sx", "sz", "sc")
+    route = [(i - 2, i) for i in range(2, seq_count)]
+    far = lax.ppermute((window_key, values), flat_axes, route)
+    prior, far = prefix_before(local, far)
     prior_state = prior
     prior_norm = prior[:, feat_total : feat_total + norm_rows].reshape(head_count, -1)[:, :feat_total]
     query_feats_only = query_feats[:, :feat_total]
@@ -124,8 +129,6 @@
     assert reach_count * row_count >= WINDOW
     flat_axes = ("sx", "sz", "sc")
     core = lax.axis_index("sc")
-    route = [(i - 2, i) for i in range(2, seq_count)]
-    far = lax.ppermute((window_key, values), flat_axes, route)
     near = lax.ppermute(
         jax.tree.map(lambda o, f: jnp.where(core == 0, o, f), (window_key, values), far),
         "sc",

time: 127 us -> 126 us (level)
  starting transfers between devices: 44.1 us -> 56.7 us
  other arithmetic: 24.5 us -> 19.1 us
  local copies, waits for them, and re-layouts: 15.4 us -> 12 us
  waiting for transfers between devices: 27.7 us -> 24.7 us
  matrix products: 13.5 us -> 11.3 us
    all_to_all x1, starting transfers between devices: 14.3 us -> 22.9 us  [prefix_before(): gathered = lax.all_to_all(outgoing, ('sx', 'sz'), 0, 0, tiled=True)]
    ppermute x1, starting transfers between devices: 8.87 us -> 4.2 us  [prefix_before(): other = lax.ppermute(sent, 'sc', [(0, 1), (1, 0)])]
    ppermute x2, starting transfers between devices: 4.2 us -> 8.72 us  [on_device(): far = lax.ppermute((window_key, values), flat_axes, route)]
    all_to_all x1, waiting for transfers between devices: 16 us -> 12 us  [prefix_before(): gathered = lax.all_to_all(outgoing, ('sx', 'sz'), 0, 0, tiled=True)]
    all_to_all x2 -> x1, other arithmetic: 4.41 us -> 0.74 us  [prefix_before(): gathered = lax.all_to_all(outgoing, ('sx', 'sz'), 0, 0, tiled=True)]
    unnamed x47 -> x49, local copies, waits for them, and re-layouts: 11.8 us -> 8.5 us
    ppermute x2, starting transfers between devices: 4.58 us -> 6.62 us  [on_device(): lax.ppermute(jax.tree.map(lambda o, f: jnp.where(core == 0, o, f), (windo...]
    dot_general x2, matrix products: 2.41 us -> 0.69 us  [pair_features(): left_side = jnp.einsum('hfr,fp->hpr', columns, pick_lower, precision=EXACT)]
  transfers between devices with their start and end apart: 8 -> 8, of which waited for: 2 -> 4; matrix products, arithmetic and copies ran while one was open for 28% -> 24% of each run, Pallas kernels for 0% -> 0%
where the time goes in v7:
time: 126 us; the launch traced here: 125 us
  starting transfers between devices  56.7 us (45%)
  waiting for transfers between devices  24.7 us (20%)
  other arithmetic  19.1 us (15%)
  local copies, waits for them, and re-layouts  12 us (10%)
  matrix products  11.3 us (9%)
    all_to_all x1, starting transfers between devices, prefix_before(): gathered = lax.all_to_all(outgoing, ('sx', 'sz'), 0, 0, tiled=True)  22.9 us
    all_to_all x1, waiting for transfers between devices, prefix_before(): gathered = lax.all_to_all(outgoing, ('sx', 'sz'), 0, 0, tiled=True)  12 us
    all_to_all x1, waiting for transfers between devices, prefix_before(): chip_prefix = lax.all_to_all(before_chip, ('sx', 'sz'), 0, 0, tiled=True)  11.3 us
    ppermute x2, starting transfers between devices, on_device(): far = lax.ppermute((window_key, values), flat_axes, route)  8.72 us
    unnamed x49, local copies, waits for them, and re-layouts  8.5 us
    all_to_all x1, starting transfers between devices, prefix_before(): chip_prefix = lax.all_to_all(before_chip, ('sx', 'sz'), 0, 0, tiled=True)  8.43 us
    ppermute x2, starting transfers between devices, on_device(): lax.ppermute(jax.tree.map(lambda o, f: jnp.where(core == 0, o, f), (windo...  6.62 us
    ppermute x1, starting transfers between devices, prefix_before(): got = lax.ppermute(give, 'sc', [(0, 1), (1, 0)])  5.83 us
  transfers between devices with their start and end apart: 8, of which 4 were waited for; matrix products, arithmetic and copies ran while one was open for 24% of the time, Pallas kernels for 0%

profile of v7, /device:TPU:1, one launch (start us, length us, event | category | flops | bytes accessed | tf_op | source)
XLA Modules:
  0.0 125.1 jit_solution(6866600096569029109)
XLA Ops:
  0.6 0.0 copy-start
  0.6 0.0 copy-start.16
  0.7 1.4 %copy.49 = bf16[128,2048]{0,1:T(8,128)(2,1)S(1)} copy(bf16[128,2048]{1,0:T(8,128)(2,1)} %param.13) | data formatting | bytes 1048576 | tf_op args[2]
  2.1 0.0 copy-start.15
  2.1 5.2 %collective-permute-start.2 = (bf16[128,2048]{0,1:T(8,128)(2,1)S(1)}, bf16[128,2048]{0,1:T(8,128)(2,1)}, u32[]{:S(2)}, u32[]{:S(2)}) collective-permute-start(bf16[128,2048]{0,1:T(8,128)(2,1)S(1)} %copy.49), channel_id=1, source_target_pairs={{0,8},{4,12},{8,16},{12,20},{16,24},{20,28},{24,32},{28,36},{32,40... | collective-permute-start | bytes 1572872 | tf_op jit(solution)/shard_map/ppermute | solution.py:111
  7.3 1.0 copy.48
  8.3 3.5 %collective-permute-start.1 = (bf16[128,2048]{0,1:T(8,128)(2,1)}, bf16[128,2048]{0,1:T(8,128)(2,1)}, u32[]{:S(2)}, u32[]{:S(2)}) collective-permute-start(bf16[128,2048]{0,1:T(8,128)(2,1)} %copy.48), channel_id=1, source_target_pairs={{0,8},{4,12},{8,16},{12,20},{16,24},{20,28},{24,32},{28,36},{32,40... | collective-permute-start | bytes 1572872 | tf_op jit(solution)/shard_map/ppermute | solution.py:111
  11.9 0.1 copy.44
  12.0 0.3 fusion.56
  12.3 0.4 fusion.7
  12.7 0.6 fusion.13
  13.4 0.1 pad.28.clone
  13.5 1.7 %fusion.19 = f32[16,160,128]{2,1,0:T(8,128)S(1)} fusion(f32[16,1,128]{2,1,0:T(1,128)S(1)} %broadcast.103, f32[16,136,128]{2,1,0:T(8,128)S(1)} %fusion.7, f32[16,16,128]{2,1,0:T(8,128)} %bitcast.91, f32[160]{0:T(256)S(1)} %pad.28.clone, bf16[128,2048]{1,0:T(8,128)(2,1)} %param.13), kind=kOutput, calls=%fused_computation.32 | convolution fusion | flops 252641280 | bytes 3089024 | tf_op jit(solution)/shard_map/hpr,rhv->hpv/dot_general | solution.py:103
  15.2 0.2 dynamic_update_slice.3
  15.4 1.2 fusion.53
  16.6 1.3 %squeeze.4 = f32[64,2560]{1,0:T(8,128)S(1)} reshape(f32[8,160,128]{2,1,0:T(8,128)} %get-tuple-element.16) | data formatting | bytes 1310720 | tf_op jit(solution)/shard_map/squeeze | solution.py:68
  17.8 0.0 copy-done.4
  17.8 0.1 squeeze.10
  18.0 0.9 broadcast_select_fusion.3
  18.9 4.2 %collective-permute-start = (f32[64,2560]{1,0:T(8,128)}, f32[64,2560]{1,0:T(8,128)S(1)}, u32[]{:S(2)}, u32[]{:S(2)}) collective-permute-start(f32[64,2560]{1,0:T(8,128)} %broadcast_select_fusion.3), channel_id=1, source_target_pairs={{0,4},{4,0},{1,5},{5,1},{2,6},{6,2},{3,7},{7,3},{8,12},{12,8},{9,1... | collective-permute-start | bytes 1966088 | tf_op jit(solution)/shard_map/ppermute | solution.py:67
  23.1 0.2 and_and_fusion
  23.3 0.7 convert_multiply_fusion.1
  24.0 1.0 collective-permute-done
  25.0 0.1 add_convert_fusion
  25.1 0.5 collective-permute-done.1
  25.6 0.5 broadcast.118
  26.1 0.7 reduce
  26.8 0.8 reshape.171
  27.6 22.9 %all-to-all-start = ((bf16[64,2,1280]{2,1,0:T(2,128)(2,1)}), bf16[64,2,1280]{2,1,0:T(2,128)(2,1)S(1)}, u32[]{:S(2)}, u32[]{:S(2)}) async-start(bf16[64,2,1280]{2,1,0:T(2,128)(2,1)} %reshape.171), calls=%async_computation | async-start | bytes 655360 | tf_op jit(solution)/shard_map/all_to_all | solution.py:71
  50.5 0.1 copy.43
  50.6 0.3 fusion.57
  51.0 1.4 %fusion.54 = (f32[16,128]{1,0:T(8,128)S(1)}, f32[16,128,128]{1,2,0:T(8,128)}) fusion(f32[128,16,16]{0,2,1:T(8,128)S(1)} %bitcast.94, f32[128,16,16]{0,2,1:T(8,128)S(1)} %bitcast.92, pred[128,128]{0,1:T(8,128)(4,1)S(1)} %iota_compare_fusion), kind=kOutput, calls=%fused_computation.83 | convolution fusion | flops 9959424 | bytes 1335296 | tf_op jit(solution)/shard_map/thf,jhf->htj/dot_general | solution.py:117
  52.4 1.4 %fusion.9 = f32[16,136,128]{2,1,0:T(8,128)} fusion(f32[16,128,136]{1,2,0:T(8,128)S(1)} %fusion.57, f32[16,16,128]{2,1,0:T(8,128)S(1)} %bitcast.95, bf16[16,136,1]{1,0,2:T(8,128)(2,1)S(1)} %copy-done.15, f32[136]{0:T(256)S(1)} %copy-done.17), kind=kOutput, calls=%fused_computation.21 | convolution fusion | flops 9469952 | bytes 2364192 | tf_op jit(solution)/shard_map/hfr,fp->hpr/dot_general | solution.py:44
  53.8 1.9 %broadcast_select_fusion = bf16[128,2048]{0,1:T(8,128)(2,1)} fusion(bf16[128,2048]{0,1:T(8,128)(2,1)} %copy.48, bf16[128,2048]{0,1:T(8,128)(2,1)} %collective-permute-done.1, pred[]{:T(512)S(6)} %eq.2), kind=kLoop, calls=%fused_computation.59 | loop fusion | flops 262144 | bytes 1572865 | tf_op jit(solution)/shard_map/jit(_where)/select_n | solution.py:133
  55.7 3.7 %collective-permute-start.5 = (bf16[128,2048]{0,1:T(8,128)(2,1)}, bf16[128,2048]{0,1:T(8,128)(2,1)}, u32[]{:S(2)}, u32[]{:S(2)}) collective-permute-start(bf16[128,2048]{0,1:T(8,128)(2,1)} %broadcast_select_fusion), channel_id=1, source_target_pairs={{0,4},{4,0},{1,5},{5,1},{2,6},{6,2},{3,7},{7,3},{8,12},{12,8},{9,1... | collective-permute-start | bytes 1572872 | tf_op jit(solution)/shard_map/ppermute | solution.py:132
  59.4 12.0 %all-to-all-done = bf16[64,2,1280]{2,1,0:T(2,128)(2,1)S(1)} async-done(((bf16[64,2,1280]{2,1,0:T(2,128)(2,1)}), bf16[64,2,1280]{2,1,0:T(2,128)(2,1)S(1)}, u32[]{:S(2)}, u32[]{:S(2)}) %all-to-all-start) | async-done | bytes 327712 | tf_op jit(solution)/shard_map/all_to_all | solution.py:71
  71.4 0.3 reshape.172
  71.6 1.0 subtract_convert_fusion
  72.7 2.5 %reduce.1 = bf16[64,2560]{1,0:T(8,128)(2,1)S(1)} reduce(bf16[64,1,2560]{2,1,0:T(2,128)(2,1)S(1)} %subtract_convert_fusion, bf16[]{:T(256)} %broadcast.118), dimensions={1}, to_apply=%subtract_convert_fusion.reduce_sub_computation | reduce | bytes 655362 | tf_op jit(solution)/shard_map/jit(cumsum)/reduce_window_sum | solution.py:73
  75.2 0.8 reshape.173
  76.0 8.4 %all-to-all-start.1 = ((bf16[64,2,1280]{2,1,0:T(2,128)(2,1)}), bf16[64,2,1280]{2,1,0:T(2,128)(2,1)S(1)}, u32[]{:S(2)}, u32[]{:S(2)}) async-start(bf16[64,2,1280]{2,1,0:T(2,128)(2,1)} %reshape.173), calls=%async_computation.1 | async-start | bytes 655360 | tf_op jit(solution)/shard_map/all_to_all | solution.py:74
  84.4 1.9 %broadcast_select_fusion.1 = bf16[128,2048]{0,1:T(8,128)(2,1)} fusion(bf16[128,2048]{0,1:T(8,128)(2,1)S(1)} %copy.49, bf16[128,2048]{0,1:T(8,128)(2,1)} %collective-permute-done.2, pred[]{:T(512)S(6)} %eq.2), kind=kLoop, calls=%fused_computation.60 | loop fusion | flops 262144 | bytes 1572865 | tf_op jit(solution)/shard_map/jit(_where)/select_n | solution.py:133
  86.3 2.9 %collective-permute-start.4 = (bf16[128,2048]{0,1:T(8,128)(2,1)}, bf16[128,2048]{0,1:T(8,128)(2,1)}, u32[]{:S(2)}, u32[]{:S(2)}) collective-permute-start(bf16[128,2048]{0,1:T(8,128)(2,1)} %broadcast_select_fusion.1), channel_id=1, source_target_pairs={{0,4},{4,0},{1,5},{5,1},{2,6},{6,2},{3,7},{7,3},{8,12},{12,8},{9,1... | collective-permute-start | bytes 1572872 | tf_op jit(solution)/shard_map/ppermute | solution.py:132
  89.2 1.6 %pad_maximum_fusion.5 = bf16[384,2048]{0,1:T(8,128)(2,1)S(1)} fusion(bf16[128,2048]{0,1:T(8,128)(2,1)} %copy.48, bf16[128,2048]{0,1:T(8,128)(2,1)} %collective-permute-done.5, bf16[128,2048]{0,1:T(8,128)(2,1)} %collective-permute-done.1), kind=kLoop, calls=%fused_computation.10 | loop fusion | flops 4718592 | bytes 3145728 | tf_op jit(solution)/shard_map/concatenate | solution.py:139
  90.8 0.6 fusion.40
  91.5 2.5 %fusion.55 = (f32[16,128]{1,0:T(8,128)S(1)}, f32[16,128,384]{1,2,0:T(8,128)}) fusion(f32[16,384,128]{2,1,0:T(8,128)S(1)} %fusion.40, pred[128,384]{0,1:T(8,128)(4,1)S(1)} %and_and_fusion), kind=kOutput, calls=%fused_computation.84 | output fusion | flops 4718975 | bytes 6348800 | tf_op jit(solution)/shard_map/sub | solution.py:157
  94.0 11.3 %all-to-all-done.1 = bf16[64,2,1280]{2,1,0:T(2,128)(2,1)S(1)} async-done(((bf16[64,2,1280]{2,1,0:T(2,128)(2,1)}), bf16[64,2,1280]{2,1,0:T(2,128)(2,1)S(1)}, u32[]{:S(2)}, u32[]{:S(2)}) %all-to-all-start.1) | async-done | bytes 327712 | tf_op jit(solution)/shard_map/all_to_all | solution.py:74
  105.3 0.3 reshape.174
  105.6 0.7 convert_element_type.46
  106.2 1.0 fusion.33
  107.2 5.8 %collective-permute-start.3 = (f32[64,2560]{1,0:T(8,128)S(1)}, f32[64,2560]{1,0:T(8,128)}, u32[]{:S(2)}, u32[]{:S(2)}) collective-permute-start(f32[64,2560]{1,0:T(8,128)S(1)} %get-tuple-element.15), channel_id=1, source_target_pairs={{0,4},{4,0},{1,5},{5,1},{2,6},{6,2},{3,7},{7,3},{8,12},{12,8},{9,1... | collective-permute-start | bytes 1966088 | tf_op jit(solution)/shard_map/ppermute | solution.py:80
  113.1 1.4 %pad_maximum_fusion.4 = bf16[384,2048]{0,1:T(8,128)(2,1)S(1)} fusion(bf16[128,2048]{0,1:T(8,128)(2,1)S(1)} %copy.49, bf16[128,2048]{0,1:T(8,128)(2,1)} %collective-permute-done.4, bf16[128,2048]{0,1:T(8,128)(2,1)} %collective-permute-done.2), kind=kLoop, calls=%fused_computation.9 | loop fusion | flops 4718592 | bytes 3145728 | tf_op jit(solution)/shard_map/concatenate | solution.py:140
  114.5 0.6 fusion.30
  115.1 1.0 copy.59
  116.2 0.1 copy-done.7
  116.2 1.4 %maximum_select_fusion = f32[2,64,2560]{2,1,0:T(8,128)S(1)} fusion(f32[1,64,2560]{2,1,0:T(8,128)} %bitcast.10, f32[1,64,2560]{2,1,0:T(8,128)S(1)} %copy-done.7, pred[]{:T(512)S(6)} %eq.2), kind=kLoop, calls=%fused_computation.37 | loop fusion | flops 983040 | bytes 2621441 | tf_op jit(solution)/shard_map/jit(_where)/select_n | solution.py:81
  117.6 0.1 select_n.65
  117.8 0.8 copy-done.9
  118.5 3.3 %convolution_bitcast_fusion = f32[128,16,128]{0,2,1:T(8,128)S(1)} fusion(f32[16,160,128]{2,1,0:T(8,128)S(1)} %select_n.65, f32[16,1,128]{2,1,0:T(1,128)S(1)} %broadcast.103, f32[16,136,128]{2,1,0:T(8,128)} %fusion.9, f32[16,16,128]{2,1,0:T(8,128)S(1)} %bitcast.96, f32[160]{0:T(256)S(1)} %pad.28.clone), kind=kOutput, calls=%fused_computation.22 | convolution fusion | flops 252641280 | bytes 3613312 | tf_op jit(solution)/shard_map/hpt,hpv->thv/dot_general | solution.py:119
  121.9 0.7 fusion.15
  122.5 0.3 copy-done.10
  122.9 0.3 copy-done.18
  123.2 0.5 fusion.11
  123.8 1.3 %copy.58 = f32[128,2048]{1,0:T(8,128)} copy(f32[128,2048]{0,1:T(8,128)S(1)} %bitcast.100) | data formatting | bytes 2097152
  (49 shorter events, 0.2 us)
Async XLA Ops:
  0.6 90.2 %copy-start = (bf16[128,2048]{1,0:T(8,128)(2,1)S(1)}, bf16[128,2048]{1,0:T(8,128)(2,1)}, u32[]{:S(2)}) copy-start(bf16[128,2048]{1,0:T(8,128)(2,1)} %param.14) | copy-start | bytes 1572868
  0.6 11.3 %copy-start.16 = (bf16[16,136,1]{1,0,2:T(8,128)(2,1)S(1)}, bf16[16,136,1]{1,0,2:T(8,128)(2,1)}, u32[]{:S(2)}) copy-start(bf16[16,136,1]{1,0,2:T(8,128)(2,1)} %constant.121) | copy-start | bytes 13060
  0.7 6.6 %copy-start.11 = (bf16[128,2048]{1,0:T(8,128)(2,1)S(1)}, bf16[128,2048]{1,0:T(8,128)(2,1)}, u32[]{:S(2)}) copy-start(bf16[128,2048]{1,0:T(8,128)(2,1)} %param.15) | copy-start | bytes 1572868
  0.7 11.2 %copy-start.13 = (bf16[128,256]{1,0:T(8,128)(2,1)S(1)}, bf16[128,256]{1,0:T(8,128)(2,1)}, u32[]{:S(2)}) copy-start(bf16[128,256]{1,0:T(8,128)(2,1)} %param.12) | copy-start | bytes 196612
  2.1 10.2 %copy-start.15 = (bf16[16,136,1]{1,0,2:T(8,128)(2,1)S(1)}, bf16[16,136,1]{1,0,2:T(8,128)(2,1)}, u32[]{:S(2)}) copy-start(bf16[16,136,1]{1,0,2:T(8,128)(2,1)} %constant.122) | copy-start | bytes 13060
  2.1 10.2 %copy-start.17 = (f32[136]{0:T(256)S(1)}, f32[136]{0:T(256)}, u32[]{:S(2)}) copy-start(f32[136]{0:T(256)} %constant.57.clone) | copy-start | bytes 1636
  2.1 23.0 %collective-permute-start.2 = (bf16[128,2048]{0,1:T(8,128)(2,1)S(1)}, bf16[128,2048]{0,1:T(8,128)(2,1)}, u32[]{:S(2)}, u32[]{:S(2)}) collective-permute-start(bf16[128,2048]{0,1:T(8,128)(2,1)S(1)} %copy.49), channel_id=1, source_target_pairs={{0,8},{4,12},{8,16},{12,20},{16,24},{20,28},{24,32},{28,36},{32,40... | collective-permute-start | bytes 1572872 | tf_op jit(solution)/shard_map/ppermute | solution.py:111
  8.3 17.3 %collective-permute-start.1 = (bf16[128,2048]{0,1:T(8,128)(2,1)}, bf16[128,2048]{0,1:T(8,128)(2,1)}, u32[]{:S(2)}, u32[]{:S(2)}) collective-permute-start(bf16[128,2048]{0,1:T(8,128)(2,1)} %copy.48), channel_id=1, source_target_pairs={{0,8},{4,12},{8,16},{12,20},{16,24},{20,28},{24,32},{28,36},{32,40... | collective-permute-start | bytes 1572872 | tf_op jit(solution)/shard_map/ppermute | solution.py:111
  12.0 1.4 %copy-start.2 = (f32[128,256]{0,1:T(8,128)}, f32[128,256]{0,1:T(8,128)S(1)}, u32[]{:S(2)}) copy-start(f32[128,256]{0,1:T(8,128)S(1)} %copy.44) | copy-start | bytes 393220
  16.6 1.3 %copy-start.4 = (f32[8,160,128]{2,1,0:T(8,128)S(1)}, f32[8,160,128]{2,1,0:T(8,128)}, u32[]{:S(2)}) copy-start(f32[8,160,128]{2,1,0:T(8,128)} %get-tuple-element.17) | copy-start | bytes 1966084
  17.9 5.4 %copy-start.14 = (bf16[128,256]{1,0:T(8,128)(2,1)S(1)}, bf16[128,256]{1,0:T(8,128)(2,1)}, u32[]{:S(2)}) copy-start(bf16[128,256]{1,0:T(8,128)(2,1)} %param.11) | copy-start | bytes 196612
  18.9 6.1 %collective-permute-start = (f32[64,2560]{1,0:T(8,128)}, f32[64,2560]{1,0:T(8,128)S(1)}, u32[]{:S(2)}, u32[]{:S(2)}) collective-permute-start(f32[64,2560]{1,0:T(8,128)} %broadcast_select_fusion.3), channel_id=1, source_target_pairs={{0,4},{4,0},{1,5},{5,1},{2,6},{6,2},{3,7},{7,3},{8,12},{12,8},{9,1... | collective-permute-start | bytes 1966088 | tf_op jit(solution)/shard_map/ppermute | solution.py:67
  25.0 1.1 copy-start.5
  25.1 25.4 %copy-start.12 = (f32[128,256]{1,0:T(8,128)S(1)}, f32[128,256]{1,0:T(8,128)}, u32[]{:S(2)}) copy-start(f32[128,256]{1,0:T(8,128)} %convert_multiply_fusion.1) | copy-start | bytes 393220
  26.8 24.2 %copy-start.3 = (f32[128,256]{0,1:T(8,128)S(1)}, f32[128,256]{0,1:T(8,128)}, u32[]{:S(2)}) copy-start(f32[128,256]{0,1:T(8,128)} %copy-done.2) | copy-start | bytes 393220
  27.6 43.7 %all-to-all-start = ((bf16[64,2,1280]{2,1,0:T(2,128)(2,1)}), bf16[64,2,1280]{2,1,0:T(2,128)(2,1)S(1)}, u32[]{:S(2)}, u32[]{:S(2)}) async-start(bf16[64,2,1280]{2,1,0:T(2,128)(2,1)} %reshape.171), calls=%async_computation | async-start | bytes 655360 | tf_op jit(solution)/shard_map/all_to_all | solution.py:71
  50.6 1.8 %copy-start.8 = (f32[128,256]{0,1:T(8,128)}, f32[128,256]{0,1:T(8,128)S(1)}, u32[]{:S(2)}) copy-start(f32[128,256]{0,1:T(8,128)S(1)} %copy.43) | copy-start | bytes 393220
  55.7 33.5 %collective-permute-start.5 = (bf16[128,2048]{0,1:T(8,128)(2,1)}, bf16[128,2048]{0,1:T(8,128)(2,1)}, u32[]{:S(2)}, u32[]{:S(2)}) collective-permute-start(bf16[128,2048]{0,1:T(8,128)(2,1)} %broadcast_select_fusion), channel_id=1, source_target_pairs={{0,4},{4,0},{1,5},{5,1},{2,6},{6,2},{3,7},{7,3},{8,12},{12,8},{9,1... | collective-permute-start | bytes 1572872 | tf_op jit(solution)/shard_map/ppermute | solution.py:132
  76.0 29.3 %all-to-all-start.1 = ((bf16[64,2,1280]{2,1,0:T(2,128)(2,1)}), bf16[64,2,1280]{2,1,0:T(2,128)(2,1)S(1)}, u32[]{:S(2)}, u32[]{:S(2)}) async-start(bf16[64,2,1280]{2,1,0:T(2,128)(2,1)} %reshape.173), calls=%async_computation.1 | async-start | bytes 655360 | tf_op jit(solution)/shard_map/all_to_all | solution.py:74
  86.3 26.8 %collective-permute-start.4 = (bf16[128,2048]{0,1:T(8,128)(2,1)}, bf16[128,2048]{0,1:T(8,128)(2,1)}, u32[]{:S(2)}, u32[]{:S(2)}) collective-permute-start(bf16[128,2048]{0,1:T(8,128)(2,1)} %broadcast_select_fusion.1), channel_id=1, source_target_pairs={{0,4},{4,0},{1,5},{5,1},{2,6},{6,2},{3,7},{7,3},{8,12},{12,8},{9,1... | collective-permute-start | bytes 1572872 | tf_op jit(solution)/shard_map/ppermute | solution.py:132
  94.0 12.2 %copy-start.6 = (f32[64,2560]{1,0:T(8,128)S(1)}, f32[64,2560]{1,0:T(8,128)}, u32[]{:S(2)}) copy-start(f32[64,2560]{1,0:T(8,128)} %copy-done.5) | copy-start | bytes 1966084
  107.2 7.3 %copy-start.19 = (f32[16,128,384]{1,2,0:T(8,128)S(1)}, f32[16,128,384]{1,2,0:T(8,128)}, u32[]{:S(2)}) copy-start(f32[16,128,384]{1,2,0:T(8,128)} %get-tuple-element.21) | copy-start | bytes 9437188
  107.2 8.9 %collective-permute-start.3 = (f32[64,2560]{1,0:T(8,128)S(1)}, f32[64,2560]{1,0:T(8,128)}, u32[]{:S(2)}, u32[]{:S(2)}) collective-permute-start(f32[64,2560]{1,0:T(8,128)S(1)} %get-tuple-element.15), channel_id=1, source_target_pairs={{0,4},{4,0},{1,5},{5,1},{2,6},{6,2},{3,7},{7,3},{8,12},{12,8},{9,1... | collective-permute-start | bytes 1966088 | tf_op jit(solution)/shard_map/ppermute | solution.py:80
  115.1 1.1 copy-start.7
  117.6 0.9 copy-start.9
  118.5 3.3 %copy-start.1 = (f32[16,136,128]{2,1,0:T(8,128)S(1)}, f32[16,136,128]{2,1,0:T(8,128)}, u32[]{:S(2)}) copy-start(f32[16,136,128]{2,1,0:T(8,128)} %fusion.9) | copy-start | bytes 3342340
  121.8 1.0 copy-start.10
  121.8 1.4 %copy-start.18 = (f32[16,128,128]{1,2,0:T(8,128)S(1)}, f32[16,128,128]{1,2,0:T(8,128)}, u32[]{:S(2)}) copy-start(f32[16,128,128]{1,2,0:T(8,128)} %get-tuple-element.19) | copy-start | bytes 3145732

commit v8 on v7

--- a/solution.py
+++ b/solution.py
@@ -55,7 +55,7 @@
     )
 
 
-def prefix_before(local, tied):
+def prefix_before(local, tied, settle):
     chips = lax.axis_size("sx") * lax.axis_size("sz")
     core = lax.axis_index("sc")
     size = local.size
@@ -69,6 +69,7 @@
     chip_half = mine + other
     outgoing, tied = lax.optimization_barrier((chip_half.astype(LINK), tied))
     gathered = lax.all_to_all(outgoing, ("sx", "sz"), 0, 0, tiled=True)
+    gathered, settled = lax.optimization_barrier((gathered, settle(tied)))
     gathered = gathered.astype(jnp.float32)
     before_chip = (jnp.cumsum(gathered, axis=0) - gathered).astype(LINK)
     chip_prefix = lax.all_to_all(before_chip, ("sx", "sz"), 0, 0, tiled=True)
@@ -79,7 +80,7 @@
     give = jnp.where(core == 0, with_first, chip_prefix)
     got = lax.ppermute(give, "sc", [(0, 1), (1, 0)])
     halves = jnp.where(core == 0, jnp.stack([keep, got]), jnp.stack([got, keep]))
-    return halves.reshape(-1)[:size].reshape(local.shape), tied
+    return halves.reshape(-1)[:size].reshape(local.shape), tied, settled
 
 
 def on_device(linear_query, linear_key, values, window_query, window_key):
@@ -109,7 +110,16 @@
     flat_axes = ("sx", "sz", "sc")
     route = [(i - 2, i) for i in range(2, seq_count)]
     far = lax.ppermute((window_key, values), flat_axes, route)
-    prior, far = prefix_before(local, far)
+    core = lax.axis_index("sc")
+
+    def near_of(far):
+        return lax.ppermute(
+            jax.tree.map(lambda o, f: jnp.where(core == 0, o, f), (window_key, values), far),
+            "sc",
+            [(0, 1), (1, 0)],
+        )
+
+    prior, far, near = prefix_before(local, far, near_of)
     prior_state = prior
     prior_norm = prior[:, feat_total : feat_total + norm_rows].reshape(head_count, -1)[:, :feat_total]
     query_feats_only = query_feats[:, :feat_total]
@@ -129,11 +139,6 @@
     assert reach_count * row_count >= WINDOW
     flat_axes = ("sx", "sz", "sc")
     core = lax.axis_index("sc")
-    near = lax.ppermute(
-        jax.tree.map(lambda o, f: jnp.where(core == 0, o, f), (window_key, values), far),
-        "sc",
-        [(0, 1), (1, 0)],
-    )
     moved_keys = [near[0], far[0]]
     moved_values = [near[1], far[1]]
     all_keys = jnp.concatenate(moved_keys[::-1] + [window_key], axis=0)

time: 126 us -> 146 us (1.16)
  waiting for transfers between devices: 24.7 us -> 37 us
  starting transfers between devices: 56.7 us -> 47.4 us
  local copies, waits for them, and re-layouts: 12 us -> 19.8 us
  other arithmetic: 19.1 us -> 23.9 us
  matrix products: 11.3 us -> 16 us
    ppermute x2, waiting for transfers between devices: 0.48 us -> 14.7 us  [on_device(): far = lax.ppermute((window_key, values), flat_axes, route)]
    unnamed x49 -> x56, local copies, waits for them, and re-layouts: 8.5 us -> 15.6 us
    all_to_all x1, starting transfers between devices: 22.9 us -> 17 us  [prefix_before(): gathered = lax.all_to_all(outgoing, ('sx', 'sz'), 0, 0, tiled=True)]
    ppermute x2, starting transfers between devices: 8.72 us -> 3.43 us  [on_device(): far = lax.ppermute((window_key, values), flat_axes, route)]
    ppermute x1, starting transfers between devices: 4.2 us -> 8.74 us  [prefix_before(): other = lax.ppermute(sent, 'sc', [(0, 1), (1, 0)])]
    all_to_all x0 -> x2, other arithmetic: none -> 4.41 us  [prefix_before(): chip_prefix = lax.all_to_all(before_chip, ('sx', 'sz'), 0, 0, tiled=True)]
    convert_element_type x1, other arithmetic: 0.09 us -> 1.91 us  [prefix_before(): outgoing, tied = lax.optimization_barrier((chip_half.astype(LINK), tied))]
    ppermute x2, starting transfers between devices: 6.62 us -> 4.97 us  [near_of(): lax.ppermute(jax.tree.map(lambda o, f: jnp.where(core == 0, o, f), (windo...]
  transfers between devices with their start and end apart: 8 -> 8, of which waited for: 4 -> 4; matrix products, arithmetic and copies ran while one was open for 24% -> 19% of each run, Pallas kernels for 0% -> 0%
where the time goes in v8:
time: 146 us; the launch traced here: 145 us
  starting transfers between devices  47.4 us (32%)
  waiting for transfers between devices  37 us (25%)
  other arithmetic  23.9 us (16%)
  local copies, waits for them, and re-layouts  19.8 us (14%)
  matrix products  16 us (11%)
    all_to_all x1, starting transfers between devices, prefix_before(): gathered = lax.all_to_all(outgoing, ('sx', 'sz'), 0, 0, tiled=True)  17 us
    unnamed x56, local copies, waits for them, and re-layouts  15.6 us
    ppermute x2, waiting for transfers between devices, on_device(): far = lax.ppermute((window_key, values), flat_axes, route)  14.7 us
    all_to_all x1, waiting for transfers between devices, prefix_before(): gathered = lax.all_to_all(outgoing, ('sx', 'sz'), 0, 0, tiled=True)  11.3 us
    all_to_all x1, waiting for transfers between devices, prefix_before(): chip_prefix = lax.all_to_all(before_chip, ('sx', 'sz'), 0, 0, tiled=True)  11 us
    ppermute x1, starting transfers between devices, prefix_before(): other = lax.ppermute(sent, 'sc', [(0, 1), (1, 0)])  8.74 us
    all_to_all x1, starting transfers between devices, prefix_before(): chip_prefix = lax.all_to_all(before_chip, ('sx', 'sz'), 0, 0, tiled=True)  8.25 us
    ppermute x1, starting transfers between devices, prefix_before(): got = lax.ppermute(give, 'sc', [(0, 1), (1, 0)])  4.98 us
  transfers between devices with their start and end apart: 8, of which 4 were waited for; matrix products, arithmetic and copies ran while one was open for 19% of the time, Pallas kernels for 0%

profile of v8, /device:TPU:1, one launch (start us, length us, event | category | flops | bytes accessed | tf_op | source)
XLA Modules:
  0.0 145.2 jit_solution(3933884460124810294)
XLA Ops:
  0.6 0.0 copy-start
  0.7 0.9 convert_multiply_fusion
  1.6 0.1 copy.58
  1.7 1.0 fusion.53
  2.8 0.4 fusion.7
  3.1 0.6 fusion.13
  3.8 0.1 pad.28.clone
  3.9 1.7 %fusion.19 = f32[16,160,128]{2,1,0:T(8,128)S(1)} fusion(f32[16,1,128]{2,1,0:T(1,128)S(1)} %broadcast.103, f32[16,136,128]{2,1,0:T(8,128)S(1)} %fusion.7, f32[16,16,128]{2,1,0:T(8,128)S(1)} %bitcast.97, f32[160]{0:T(256)S(1)} %pad.28.clone, bf16[128,2048]{1,0:T(8,128)(2,1)} %param.13), kind=kOutput, calls=%fused_computation.32 | convolution fusion | flops 252641280 | bytes 3089024 | tf_op jit(solution)/shard_map/hpr,rhv->hpv/dot_general | solution.py:104
  5.6 0.2 dynamic_update_slice.3
  5.7 1.1 fusion.50
  6.9 1.3 squeeze.4
  8.1 0.0 copy-done.3
  8.2 0.1 squeeze.10
  8.3 0.9 broadcast_select_fusion.3
  9.2 8.7 %collective-permute-start = (f32[64,2560]{1,0:T(8,128)}, f32[64,2560]{1,0:T(8,128)}, u32[]{:S(2)}, u32[]{:S(2)}) collective-permute-start(f32[64,2560]{1,0:T(8,128)} %broadcast_select_fusion.3), channel_id=1, source_target_pairs={{0,4},{4,0},{1,5},{5,1},{2,6},{6,2},{3,7},{7,3},{8,12},{12,8},{9,1... | collective-permute-start | bytes 1966088 | tf_op jit(solution)/shard_map/ppermute | solution.py:67
  17.9 0.3 copy.62
  18.2 1.3 collective-permute-start.1
  19.6 1.3 copy.63
  20.9 2.1 %collective-permute-start.2 = (bf16[128,2048]{0,1:T(8,128)(2,1)S(1)}, bf16[128,2048]{0,1:T(8,128)(2,1)}, u32[]{:S(2)}, u32[]{:S(2)}) collective-permute-start(bf16[128,2048]{0,1:T(8,128)(2,1)S(1)} %copy.63), channel_id=1, source_target_pairs={{0,8},{4,12},{8,16},{12,20},{16,24},{20,28},{24,32},{28,36},{32,40... | collective-permute-start | bytes 1572872 | tf_op jit(solution)/shard_map/ppermute | solution.py:112
  23.0 0.6 iota_add_fusion.1
  23.6 0.6 iota_add_fusion
  24.1 1.5 %convert_multiply_fusion.1 = f32[128,256]{1,0:T(8,128)} fusion(bf16[128,256]{1,0:T(8,128)(2,1)} %param.11), kind=kLoop, calls=%fused_computation.68 | loop fusion | flops 65536 | bytes 196608 | tf_op jit(solution)/shard_map/mul | solution.py:92
  25.6 1.9 %add_convert_fusion = bf16[64,2560]{1,0:T(8,128)(2,1)} fusion(f32[64,2560]{1,0:T(8,128)} %collective-permute-done, f32[64,2560]{1,0:T(8,128)S(1)} %squeeze.4, f32[64,2560]{1,0:T(8,128)S(1)} %squeeze.10, pred[]{:T(512)S(6)} %eq.2), kind=kLoop, calls=%fused_computation.52 | loop fusion | flops 491520 | bytes 2293761 | tf_op jit(solution)/shard_map/convert_element_type | solution.py:70
  27.6 3.5 %collective-permute-done.1 = bf16[128,2048]{0,1:T(8,128)(2,1)S(1)} collective-permute-done((bf16[128,2048]{0,1:T(8,128)(2,1)S(1)}, bf16[128,2048]{0,1:T(8,128)(2,1)S(1)}, u32[]{:S(2)}, u32[]{:S(2)}) %collective-permute-start.1) | collective-permute-done | bytes 524320 | tf_op jit(solution)/shard_map/ppermute | solution.py:112
  31.1 11.2 %collective-permute-done.2 = bf16[128,2048]{0,1:T(8,128)(2,1)} collective-permute-done((bf16[128,2048]{0,1:T(8,128)(2,1)S(1)}, bf16[128,2048]{0,1:T(8,128)(2,1)}, u32[]{:S(2)}, u32[]{:S(2)}) %collective-permute-start.2) | collective-permute-done | bytes 524320 | tf_op jit(solution)/shard_map/ppermute | solution.py:112
  42.3 0.5 broadcast.118
  42.8 1.8 %reduce = bf16[64,2560]{1,0:T(8,128)(2,1)S(1)} reduce(bf16[64,1,2560]{2,0,1:T(8,128)(2,1)} %bitcast.107, bf16[]{:T(256)} %broadcast.118), dimensions={1}, to_apply=%copy.64.reduce_sub_computation | reduce | bytes 655362 | tf_op jit(solution)/shard_map/all_to_all | solution.py:71
  44.6 0.8 reshape.169
  45.4 17.0 %all-to-all-start = ((bf16[64,2,1280]{2,1,0:T(2,128)(2,1)}), bf16[64,2,1280]{2,1,0:T(2,128)(2,1)}, u32[]{:S(2)}, u32[]{:S(2)}) async-start(bf16[64,2,1280]{2,1,0:T(2,128)(2,1)} %reshape.169), calls=%async_computation | async-start | bytes 655360 | tf_op jit(solution)/shard_map/all_to_all | solution.py:71
  62.4 0.9 broadcast_select_fusion.1
  63.3 3.1 %collective-permute-start.3 = (bf16[128,2048]{0,1:T(8,128)(2,1)}, bf16[128,2048]{0,1:T(8,128)(2,1)}, u32[]{:S(2)}, u32[]{:S(2)}) collective-permute-start(bf16[128,2048]{0,1:T(8,128)(2,1)} %broadcast_select_fusion.1), channel_id=1, source_target_pairs={{0,4},{4,0},{1,5},{5,1},{2,6},{6,2},{3,7},{7,3},{8,12},{12,8},{9,1... | collective-permute-start | bytes 1572872 | tf_op jit(solution)/shard_map/ppermute | solution.py:116
  66.4 1.9 %broadcast_select_fusion = bf16[128,2048]{0,1:T(8,128)(2,1)} fusion(bf16[128,2048]{0,1:T(8,128)(2,1)S(1)} %copy.63, bf16[128,2048]{0,1:T(8,128)(2,1)} %collective-permute-done.2, pred[]{:T(512)S(6)} %eq.2), kind=kLoop, calls=%fused_computation.58 | loop fusion | flops 262144 | bytes 1572865 | tf_op jit(solution)/shard_map/jit(_where)/select_n | solution.py:117
  68.3 1.9 %collective-permute-start.4 = (bf16[128,2048]{0,1:T(8,128)(2,1)}, bf16[128,2048]{0,1:T(8,128)(2,1)}, u32[]{:S(2)}, u32[]{:S(2)}) collective-permute-start(bf16[128,2048]{0,1:T(8,128)(2,1)} %broadcast_select_fusion), channel_id=1, source_target_pairs={{0,4},{4,0},{1,5},{5,1},{2,6},{6,2},{3,7},{7,3},{8,12},{12,8},{9,1... | collective-permute-start | bytes 1572872 | tf_op jit(solution)/shard_map/ppermute | solution.py:116
  70.2 0.8 copy.57
  71.0 0.2 and_and_fusion
  71.2 1.3 fusion.54
  72.4 11.3 %all-to-all-done = bf16[64,2,1280]{2,1,0:T(2,128)(2,1)} async-done(((bf16[64,2,1280]{2,1,0:T(2,128)(2,1)}), bf16[64,2,1280]{2,1,0:T(2,128)(2,1)}, u32[]{:S(2)}, u32[]{:S(2)}) %all-to-all-start) | async-done | bytes 327712 | tf_op jit(solution)/shard_map/all_to_all | solution.py:71
  83.7 3.2 %reshape.170 = bf16[64,1,2560]{2,1,0:T(2,128)(2,1)} reshape(bf16[64,2,1280]{2,1,0:T(2,128)(2,1)} %all-to-all-done) | data formatting | bytes 655360
  86.9 1.9 %copy.103 = bf16[64,1,2560]{2,0,1:T(8,128)(2,1)} copy(bf16[64,1,2560]{2,1,0:T(2,128)(2,1)} %reshape.170) | data formatting | bytes 655360
  88.8 2.4 %reduce_window_sum.11 = f32[64,2560]{1,0:T(8,128)} reduce-window(bf16[64,2560]{1,0:T(8,128)(2,1)} %bitcast.99, f32[]{:T(128)} %constant.21.clone.1), window={size=64x1 pad=63_0x0_0}, to_apply=%region_1.2 | reduce-window | flops 10321920 | bytes 983044 | tf_op jit(solution)/shard_map/jit(cumsum)/reduce_window_sum | solution.py:74
  91.2 1.9 %fusion.43 = bf16[64,1,2560]{2,0,1:T(8,128)(2,1)} fusion(f32[64,2560]{1,0:T(8,128)} %reduce_window_sum.11, bf16[64,2560]{1,0:T(8,128)(2,1)} %bitcast.100), kind=kLoop, calls=%fused_computation.62 | loop fusion | flops 491520 | bytes 1310720 | tf_op jit(solution)/shard_map/all_to_all | solution.py:75
  93.1 2.5 %reduce.1 = bf16[64,2560]{1,0:T(8,128)(2,1)} reduce(bf16[64,1,2560]{2,0,1:T(8,128)(2,1)} %fusion.43, bf16[]{:T(256)} %broadcast.118), dimensions={1}, to_apply=%copy.67.reduce_sub_computation | reduce | bytes 655362 | tf_op jit(solution)/shard_map/all_to_all | solution.py:75
  95.6 1.8 %reshape.171 = bf16[64,2,1280]{2,1,0:T(2,128)(2,1)} reshape(bf16[64,2560]{1,0:T(8,128)(2,1)} %reduce.1) | data formatting | bytes 655360
  97.3 8.2 %all-to-all-start.1 = ((bf16[64,2,1280]{2,1,0:T(2,128)(2,1)}), bf16[64,2,1280]{2,1,0:T(2,128)(2,1)}, u32[]{:S(2)}, u32[]{:S(2)}) async-start(bf16[64,2,1280]{2,1,0:T(2,128)(2,1)} %reshape.171), calls=%async_computation.1 | async-start | bytes 655360 | tf_op jit(solution)/shard_map/all_to_all | solution.py:75
  105.6 2.9 %fusion.51 = (f32[16,128]{1,0:T(8,128)}, f32[16,128,128]{1,2,0:T(8,128)}) fusion(f32[128,16,16]{0,2,1:T(8,128)} %bitcast.102, f32[128,16,16]{0,2,1:T(8,128)S(1)} %bitcast.98, pred[128,128]{0,1:T(8,128)(4,1)S(1)} %iota_compare_fusion), kind=kOutput, calls=%fused_computation.84 | convolution fusion | flops 9959424 | bytes 1335296 | tf_op jit(solution)/shard_map/thf,jhf->htj/dot_general | solution.py:127
  108.6 1.4 fusion.9
  109.9 2.9 %pad_maximum_fusion.4 = (bf16[384,2048]{0,1:T(8,128)(2,1)}, bf16[384,2048]{0,1:T(8,128)(2,1)S(1)}) fusion(bf16[128,2048]{0,1:T(8,128)(2,1)S(1)} %copy.63, bf16[128,2048]{0,1:T(8,128)(2,1)} %collective-permute-done.4, bf16[128,2048]{0,1:T(8,128)(2,1)} %collective-permute-done.2, bf16[128,2048]{0,1:T(8,128)(2,1)S(1)} %copy.62, ...), kind=kLoop, calls=%fused_computation.9 | loop fusion | flops 9437184 | bytes 6291456 | tf_op jit(solution)/shard_map/concatenate | solution.py:145
  112.9 2.3 %fusion.36 = f32[16,384,128]{2,1,0:T(8,128)} fusion(bf16[384,16,128]{0,2,1:T(8,128)(2,1)S(1)} %bitcast.93, bf16[128,2048]{1,0:T(8,128)(2,1)S(1)} %copy-done), kind=kOutput, calls=%fused_computation.53 | convolution fusion | flops 201326592 | bytes 5242880 | tf_op jit(solution)/shard_map/thd,jhd->htj/dot_general | solution.py:154
  115.2 11.0 %all-to-all-done.1 = bf16[64,2,1280]{2,1,0:T(2,128)(2,1)} async-done(((bf16[64,2,1280]{2,1,0:T(2,128)(2,1)}), bf16[64,2,1280]{2,1,0:T(2,128)(2,1)}, u32[]{:S(2)}, u32[]{:S(2)}) %all-to-all-start.1) | async-done | bytes 327712 | tf_op jit(solution)/shard_map/all_to_all | solution.py:75
  126.1 2.5 %reshape.172 = bf16[64,1,2560]{2,1,0:T(2,128)(2,1)S(1)} reshape(bf16[64,2,1280]{2,1,0:T(2,128)(2,1)} %all-to-all-done.1) | data formatting | bytes 655360
  128.6 1.4 fusion.33
  130.0 5.0 %collective-permute-start.5 = (f32[64,2560]{1,0:T(8,128)S(1)}, f32[64,2560]{1,0:T(8,128)S(1)}, u32[]{:S(2)}, u32[]{:S(2)}) collective-permute-start(f32[64,2560]{1,0:T(8,128)S(1)} %get-tuple-element.23), channel_id=1, source_target_pairs={{0,4},{4,0},{1,5},{5,1},{2,6},{6,2},{3,7},{7,3},{8,12},{12,8},{9,1... | collective-permute-start | bytes 1966088 | tf_op jit(solution)/shard_map/ppermute | solution.py:81
  135.0 0.9 fusion.52
  136.0 0.6 fusion.30
  136.6 1.0 copy.75
  137.6 0.1 maximum_select_fusion
  137.7 0.1 select_n.68
  137.8 0.8 copy-done.5
  138.6 3.3 %convolution_bitcast_fusion = f32[128,16,128]{0,2,1:T(8,128)S(1)} fusion(f32[16,160,128]{2,1,0:T(8,128)S(1)} %select_n.68, f32[16,1,128]{2,1,0:T(1,128)S(1)} %broadcast.103, f32[16,136,128]{2,1,0:T(8,128)} %fusion.9, f32[16,16,128]{2,1,0:T(8,128)S(1)} %bitcast.104, f32[160]{0:T(256)S(1)} %copy-done.15), kind=kOutput, calls=%fused_computation.22 | convolution fusion | flops 252641280 | bytes 3613312 | tf_op jit(solution)/shard_map/hpt,hpv->thv/dot_general | solution.py:129
  141.9 0.7 fusion.15
  142.6 0.3 copy-done.8
  142.9 0.3 copy-done.22
  143.3 0.6 fusion.11
  143.9 1.3 copy.74
  (55 shorter events, 0.2 us)
Async XLA Ops:
  0.6 112.2 %copy-start = (bf16[128,2048]{1,0:T(8,128)(2,1)S(1)}, bf16[128,2048]{1,0:T(8,128)(2,1)}, u32[]{:S(2)}) copy-start(bf16[128,2048]{1,0:T(8,128)(2,1)} %param.14) | copy-start | bytes 1572868
  0.6 2.1 %copy-start.12 = (bf16[16,136,1]{1,0,2:T(8,128)(2,1)S(1)}, bf16[16,136,1]{1,0,2:T(8,128)(2,1)}, u32[]{:S(2)}) copy-start(bf16[16,136,1]{1,0,2:T(8,128)(2,1)} %constant.124) | copy-start | bytes 13060
  0.7 2.1 %copy-start.18 = (f32[136]{0:T(256)S(1)}, f32[136]{0:T(256)}, u32[]{:S(2)}) copy-start(f32[136]{0:T(256)} %constant.57.clone) | copy-start | bytes 1636
  3.9 1.7 %copy-start.14 = (f32[160]{0:T(256)}, f32[160]{0:T(256)S(1)}, u32[]{:S(2)}) copy-start(f32[160]{0:T(256)S(1)} %pad.28.clone) | copy-start | bytes 1924
  6.9 1.3 copy-start.3
  8.3 9.7 %copy-start.10 = (bf16[128,2048]{1,0:T(8,128)(2,1)S(1)}, bf16[128,2048]{1,0:T(8,128)(2,1)}, u32[]{:S(2)}) copy-start(bf16[128,2048]{1,0:T(8,128)(2,1)} %param.15) | copy-start | bytes 1572868
  9.2 16.5 %collective-permute-start = (f32[64,2560]{1,0:T(8,128)}, f32[64,2560]{1,0:T(8,128)}, u32[]{:S(2)}, u32[]{:S(2)}) collective-permute-start(f32[64,2560]{1,0:T(8,128)} %broadcast_select_fusion.3), channel_id=1, source_target_pairs={{0,4},{4,0},{1,5},{5,1},{2,6},{6,2},{3,7},{7,3},{8,12},{12,8},{9,1... | collective-permute-start | bytes 1966088 | tf_op jit(solution)/shard_map/ppermute | solution.py:67
  18.2 12.8 %collective-permute-start.1 = (bf16[128,2048]{0,1:T(8,128)(2,1)S(1)}, bf16[128,2048]{0,1:T(8,128)(2,1)S(1)}, u32[]{:S(2)}, u32[]{:S(2)}) collective-permute-start(bf16[128,2048]{0,1:T(8,128)(2,1)S(1)} %copy.62), channel_id=1, source_target_pairs={{0,8},{4,12},{8,16},{12,20},{16,24},{20,28},{24,32},{28,36},{32,40... | collective-permute-start | bytes 1572872 | tf_op jit(solution)/shard_map/ppermute | solution.py:112
  20.9 21.4 %collective-permute-start.2 = (bf16[128,2048]{0,1:T(8,128)(2,1)S(1)}, bf16[128,2048]{0,1:T(8,128)(2,1)}, u32[]{:S(2)}, u32[]{:S(2)}) collective-permute-start(bf16[128,2048]{0,1:T(8,128)(2,1)S(1)} %copy.63), channel_id=1, source_target_pairs={{0,8},{4,12},{8,16},{12,20},{16,24},{20,28},{24,32},{28,36},{32,40... | collective-permute-start | bytes 1572872 | tf_op jit(solution)/shard_map/ppermute | solution.py:112
  31.0 32.2 %copy-start.6 = (bf16[128,2048]{0,1:T(8,128)(2,1)}, bf16[128,2048]{0,1:T(8,128)(2,1)S(1)}, u32[]{:S(2)}) copy-start(bf16[128,2048]{0,1:T(8,128)(2,1)S(1)} %collective-permute-done.1) | copy-start | bytes 1572868
  45.4 38.3 %all-to-all-start = ((bf16[64,2,1280]{2,1,0:T(2,128)(2,1)}), bf16[64,2,1280]{2,1,0:T(2,128)(2,1)}, u32[]{:S(2)}, u32[]{:S(2)}) async-start(bf16[64,2,1280]{2,1,0:T(2,128)(2,1)} %reshape.169), calls=%async_computation | async-start | bytes 655360 | tf_op jit(solution)/shard_map/all_to_all | solution.py:71
  62.4 7.8 %copy-start.11 = (f32[128,256]{1,0:T(8,128)S(1)}, f32[128,256]{1,0:T(8,128)}, u32[]{:S(2)}) copy-start(f32[128,256]{1,0:T(8,128)} %convert_multiply_fusion.1) | copy-start | bytes 393220
  63.3 7.7 %copy-start.17 = (s32[384]{0:T(512)S(1)}, s32[384]{0:T(512)}, u32[]{:S(2)}) copy-start(s32[384]{0:T(512)} %iota_add_fusion) | copy-start | bytes 4612
  63.3 7.7 %copy-start.20 = (s32[128]{0:T(128)S(1)}, s32[128]{0:T(128)}, u32[]{:S(2)}) copy-start(s32[128]{0:T(128)} %get-tuple-element.32) | copy-start | bytes 1540
  63.3 7.7 %copy-start.21 = (s32[128]{0:T(128)S(1)}, s32[128]{0:T(128)}, u32[]{:S(2)}) copy-start(s32[128]{0:T(128)} %get-tuple-element.33) | copy-start | bytes 1540
  63.3 25.5 %collective-permute-start.3 = (bf16[128,2048]{0,1:T(8,128)(2,1)}, bf16[128,2048]{0,1:T(8,128)(2,1)}, u32[]{:S(2)}, u32[]{:S(2)}) collective-permute-start(bf16[128,2048]{0,1:T(8,128)(2,1)} %broadcast_select_fusion.1), channel_id=1, source_target_pairs={{0,4},{4,0},{1,5},{5,1},{2,6},{6,2},{3,7},{7,3},{8,12},{12,8},{9,1... | collective-permute-start | bytes 1572872 | tf_op jit(solution)/shard_map/ppermute | solution.py:116
  66.4 4.8 %copy-start.13 = (bf16[16,136,1]{1,0,2:T(8,128)(2,1)S(1)}, bf16[16,136,1]{1,0,2:T(8,128)(2,1)}, u32[]{:S(2)}) copy-start(bf16[16,136,1]{1,0,2:T(8,128)(2,1)} %constant.123) | copy-start | bytes 13060
  68.3 20.5 %collective-permute-start.4 = (bf16[128,2048]{0,1:T(8,128)(2,1)}, bf16[128,2048]{0,1:T(8,128)(2,1)}, u32[]{:S(2)}, u32[]{:S(2)}) collective-permute-start(bf16[128,2048]{0,1:T(8,128)(2,1)} %broadcast_select_fusion), channel_id=1, source_target_pairs={{0,4},{4,0},{1,5},{5,1},{2,6},{6,2},{3,7},{7,3},{8,12},{12,8},{9,1... | collective-permute-start | bytes 1572872 | tf_op jit(solution)/shard_map/ppermute | solution.py:116
  97.3 28.8 %all-to-all-start.1 = ((bf16[64,2,1280]{2,1,0:T(2,128)(2,1)}), bf16[64,2,1280]{2,1,0:T(2,128)(2,1)}, u32[]{:S(2)}, u32[]{:S(2)}) async-start(bf16[64,2,1280]{2,1,0:T(2,128)(2,1)} %reshape.171), calls=%async_computation.1 | async-start | bytes 655360 | tf_op jit(solution)/shard_map/all_to_all | solution.py:75
  105.6 3.0 %copy-start.4 = (f32[128,256]{0,1:T(8,128)S(1)}, f32[128,256]{0,1:T(8,128)}, u32[]{:S(2)}) copy-start(f32[128,256]{0,1:T(8,128)} %copy.57) | copy-start | bytes 393220
  105.6 3.0 %copy-start.19 = (f32[136]{0:T(256)S(1)}, f32[136]{0:T(256)}, u32[]{:S(2)}) copy-start(f32[136]{0:T(256)} %constant.57.clone) | copy-start | bytes 1636
  108.6 1.4 copy-start.7
  128.6 6.4 %copy-start.2 = (f32[16,384,128]{2,1,0:T(8,128)S(1)}, f32[16,384,128]{2,1,0:T(8,128)}, u32[]{:S(2)}) copy-start(f32[16,384,128]{2,1,0:T(8,128)} %fusion.36) | copy-start | bytes 9437188
  130.0 6.0 %copy-start.9 = (bf16[384,2048]{0,1:T(8,128)(2,1)S(1)}, bf16[384,2048]{0,1:T(8,128)(2,1)}, u32[]{:S(2)}) copy-start(bf16[384,2048]{0,1:T(8,128)(2,1)} %get-tuple-element.30) | copy-start | bytes 4718596
  130.0 7.5 %collective-permute-start.5 = (f32[64,2560]{1,0:T(8,128)S(1)}, f32[64,2560]{1,0:T(8,128)S(1)}, u32[]{:S(2)}, u32[]{:S(2)}) collective-permute-start(f32[64,2560]{1,0:T(8,128)S(1)} %get-tuple-element.23), channel_id=1, source_target_pairs={{0,4},{4,0},{1,5},{5,1},{2,6},{6,2},{3,7},{7,3},{8,12},{12,8},{9,1... | collective-permute-start | bytes 1966088 | tf_op jit(solution)/shard_map/ppermute | solution.py:81
  137.7 0.9 copy-start.5
  137.7 0.9 copy-start.15
  138.6 3.3 %copy-start.1 = (f32[16,136,128]{2,1,0:T(8,128)S(1)}, f32[16,136,128]{2,1,0:T(8,128)}, u32[]{:S(2)}) copy-start(f32[16,136,128]{2,1,0:T(8,128)} %fusion.9) | copy-start | bytes 3342340
  141.9 0.7 copy-start.16
  141.9 1.0 copy-start.8
  141.9 1.4 copy-start.22
